TPU v7x, 256 devices: a whole 4x4x8 slice. The times are simulated.
256 devices in a mesh: group: 16 (over y, x), dp: 8 (over z), space: 2 (over core).
Axes of the slice: x: 4, y: 4, z: 8, core: 2. Of those that a mesh axis runs over, the one named last changes fastest.
Arguments:
- video: bfloat16 [8, 32, 16, 64, 256], P('dp', 'group', 'space'), may hold values from -6 to 6
- cotangent: bfloat16 [8, 32, 16, 64, 256], P('dp', 'group', 'space'), may hold values from -6 to 6
- weight: bfloat16 [6912, 256], replicated, may hold values from -0.078125 to 0.078125
- clip_id: int32 [8, 32], P('dp', 'group'), may hold values from 0 to 3, never falling along the last dimension, each value on 1 to 16 neighbouring positions
Outputs:
- activation: bfloat16 [8, 32, 16, 64, 256], P('dp', 'group', 'space')
- grad_video: bfloat16 [8, 32, 16, 64, 256], P('dp', 'group', 'space')
- grad_weight: float32 [27, 65536], P(None, ('group', 'dp', 'space'))
Inputs may be any that keep to these rules, and one draw needn't show every extreme that they name: `clip_id`: clip numbers never fall along a stream's frames; every clip spans at most 16 frames and one spans exactly that many.
All inputs are finite; a program needn't handle non-finite values.
Results may differ from a plain program's by a relative error of at most 0.0053.
Values may be sent and summed in bfloat16 or wider, within the bound.
No kernel may reach another device: no remote copies, remote signals or barrier semaphores. Data moves between devices by JAX's collectives and lax.ppermute only.
A program may use at most 128 MiB of HBM per device.

v0:
```python
import jax
import jax.numpy as jnp
from jax import lax
from jax.sharding import PartitionSpec as P


def passed_along(value, axis, by):
    length = lax.axis_size(axis)
    pairs = [(i, i + by) for i in range(length) if 0 <= i + by < length]
    return lax.ppermute(value, axis, pairs)


def row_halo(block, axis, dim):
    count = lax.axis_size(axis)
    forward = [(i, i + 1) for i in range(count - 1)]
    backward = [(target, source) for source, target in forward]
    low = lax.ppermute(
        lax.slice_in_dim(block, block.shape[dim] - 1, None, axis=dim), axis, forward
    )
    high = lax.ppermute(lax.slice_in_dim(block, 0, 1, axis=dim), axis, backward)
    return jnp.concatenate([low, block, high], axis=dim)


def halve(x, dim, axis, flip):
    size = x.shape[dim] // 2
    bit = (lax.axis_index(axis) // flip) % 2
    keep = lax.dynamic_slice_in_dim(x, bit * size, size, axis=dim)
    give = lax.dynamic_slice_in_dim(x, (1 - bit) * size, size, axis=dim)
    pairs = [(i, i ^ flip) for i in range(lax.axis_size(axis))]
    return keep + lax.ppermute(give, axis, pairs)


def bits_of(n):
    count = n.bit_length() - 1
    assert 1 << count == n
    return count


def owner_pairs(order, sizes):
    names = ("group", "dp", "space")
    count = sizes["group"] * sizes["dp"] * sizes["space"]
    pairs = []
    for linear in range(count):
        where = {
            "group": linear // (sizes["dp"] * sizes["space"]),
            "dp": (linear // sizes["space"]) % sizes["dp"],
            "space": linear % sizes["space"],
        }
        chunk = 0
        for axis, flip in order:
            chunk = chunk * 2 + (where[axis] // flip) % 2
        pairs.append((linear, chunk))
    return names, pairs


def reduce_weight_grad(total):
    ntaps, chans, outs = total.shape
    sizes = {name: lax.axis_size(name) for name in ("group", "dp", "space")}
    ng = sizes["group"]
    across = 4 if ng % 4 == 0 else ng
    down = ng // across
    assert chans == ng * sizes["dp"] * sizes["space"]
    first = ("space", 1)
    ys = [("group", across << b) for b in range(bits_of(down))]
    xs = [("group", 1 << b) for b in range(bits_of(across))]
    ds = [("dp", 1 << b) for b in range(bits_of(sizes["dp"]))]
    assert sizes["space"] == 2
    lanes = (ds, xs, ys)
    total = halve(total, 1, *first)
    spread = [lane[0] for lane in lanes]
    rest = [key for lane in (xs, ys, ds) for key in lane[1:]]
    per = ntaps // len(lanes)
    parts, orders = [], []
    for n in range(len(lanes)):
        order = [first] + spread[n:] + spread[:n]
        part = total[n * per : (n + 1) * per]
        for axis, flip in order[1:]:
            part = halve(part, 1, axis, flip)
        parts.append(part)
        orders.append(order + rest)
    joined = jnp.stack(parts)
    for axis, flip in rest:
        joined = halve(joined, 2, axis, flip)
    parts = []
    for n, order in enumerate(orders):
        names, pairs = owner_pairs(order, sizes)
        parts.append(lax.ppermute(joined[n], names, pairs).reshape(per, outs))
    return jnp.concatenate(parts, axis=0)


def clip_tables(clip_id, frames):
    ids = lax.all_gather(clip_id, "group", axis=1, tiled=True)
    total = ids.shape[1]
    index = jnp.arange(total, dtype=jnp.int32)[None, :]
    prev = jnp.concatenate([jnp.full_like(ids[:, :1], -1), ids[:, :-1]], axis=1)
    boundary = ids != prev
    start = lax.cummax(jnp.where(boundary, index, 0), axis=1)
    position = index - start
    ext = jnp.concatenate([jnp.full_like(ids[:, :2], -1), ids], axis=1)
    same = jnp.stack([ext[:, 2 - k : 2 - k + total] == ids for k in range(3)], axis=0)
    first = lax.axis_index("group") * frames
    pos_pad = jnp.concatenate([jnp.zeros_like(position[:, :2]), position], axis=1)
    pos_wide = lax.dynamic_slice_in_dim(pos_pad, first, frames + 2, axis=1)
    same_pad = jnp.concatenate([same, jnp.zeros_like(same[:, :, :2])], axis=2)
    own = lax.dynamic_slice_in_dim(same_pad, first, frames + 2, axis=2)
    fwd = own[:, :, :frames]
    bwd = jnp.stack([own[k, :, k : k + frames] for k in range(3)], axis=0)
    return pos_wide, fwd, bwd


def local(video, cotangent, weight, clip_id):
    frames = video.shape[1]
    rows = video.shape[2]
    cols = video.shape[3]
    chans = video.shape[4]
    past = passed_along(lax.slice_in_dim(video, frames - 2, None, axis=1), "group", 1)
    vwide = row_halo(jnp.concatenate([past, video], axis=1), "space", 2)
    pos_wide, same_fwd, same_bwd = clip_tables(clip_id, frames)
    omega = 0.37 * (jnp.arange(chans) % 8 + 1).astype(jnp.float32)
    embed = jnp.sin(pos_wide.astype(jnp.float32)[:, :, None] * omega)
    shifted = (vwide.astype(jnp.float32) + embed[:, :, None, None, :]).astype(jnp.bfloat16)
    row = jnp.arange(rows + 2)
    where_s = lax.axis_index("space")
    inside = ((row > 0) | (where_s > 0)) & ((row < rows + 1) | (where_s < lax.axis_size("space") - 1))
    shifted = jnp.where(inside[None, None, :, None, None], shifted, jnp.zeros_like(shifted))
    maskf = same_fwd.astype(jnp.float32)
    widened = jnp.pad(shifted, ((0, 0), (0, 0), (0, 0), (1, 1), (0, 0)))
    stacked = jnp.concatenate([widened[:, :, :, b : b + cols] for b in range(3)], axis=4)
    taps = weight.reshape(3, 3, 3 * chans, chans)
    pre = jnp.zeros(video.shape, jnp.float32)
    for k in range(3):
        part = jnp.zeros(video.shape, jnp.float32)
        for a in range(3):
            block = stacked[:, 2 - k : 2 - k + frames, a : a + rows]
            part = part + jnp.einsum(
                "sfhwk,kc->sfhwc", block, taps[k, a], preferred_element_type=jnp.float32
            )
        pre = pre + part * maskf[k][:, :, None, None, None]
    sigma = jax.nn.sigmoid(pre)
    activation = (pre * sigma).astype(jnp.bfloat16)
    delta = (cotangent.astype(jnp.float32) * sigma * (1.0 + pre * (1.0 - sigma))).astype(
        jnp.bfloat16
    )
    ahead = passed_along(lax.slice_in_dim(delta, 0, 2, axis=1), "group", -1)
    gwide = row_halo(jnp.concatenate([delta, ahead], axis=1), "space", 2)
    terms = []
    for k in range(3):
        masked = delta * same_fwd[k].astype(jnp.bfloat16)[:, :, None, None, None]
        for a in range(3):
            block = stacked[:, 2 - k : 2 - k + frames, a : a + rows]
            terms.append(
                jnp.einsum("sfhwk,sfhwc->kc", block, masked, preferred_element_type=jnp.float32)
            )
    total = jnp.stack(terms).reshape(27, chans, chans)
    reduced = reduce_weight_grad(total)
    gwide = jnp.pad(gwide, ((0, 0), (0, 0), (0, 0), (1, 1), (0, 0)))
    gstack = jnp.concatenate([gwide[:, :, :, 2 - b : 2 - b + cols] for b in range(3)], axis=4)
    back = (
        weight.reshape(3, 3, 3, chans, chans)
        .transpose(0, 1, 2, 4, 3)
        .reshape(3, 3, 3 * chans, chans)
    )
    grad = jnp.zeros(video.shape, jnp.float32)
    for k in range(3):
        part = jnp.zeros(video.shape, jnp.float32)
        for a in range(3):
            block = gstack[:, k : k + frames, 2 - a : 2 - a + rows]
            part = part + jnp.einsum(
                "sfhwk,kc->sfhwc", block, back[k, a], preferred_element_type=jnp.float32
            )
        grad = grad + part * same_bwd[k].astype(jnp.float32)[:, :, None, None, None]
    return (activation, grad.astype(jnp.bfloat16), reduced)


def solution(mesh):
    placed = (
        P("dp", "group", "space", None, None),
        P("dp", "group", "space", None, None),
        P(),
        P("dp", "group"),
    )
    return jax.shard_map(
        local,
        mesh=mesh,
        in_specs=placed,
        out_specs=(
            P("dp", "group", "space", None, None),
            P("dp", "group", "space", None, None),
            P(None, ("group", "dp", "space")),
        ),
        check_vma=False,
    )
```

profile of v0, /device:TPU:25, one launch (start us, length us, event | category | flops | bytes accessed | tf_op | source)
XLA Modules:
  0.0 186.3 jit_solution(17842599101035989753)
XLA Ops:
  0.6 3.1 %collective-permute-start = (bf16[1,2,8,64,256]{4,3,2,1,0:T(8,128)(2,1)}, bf16[1,2,8,64,256]{4,3,2,1,0:T(8,128)(2,1)S(1)}, u32[]{:S(2)}, u32[]{:S(2)}) collective-permute-start(bf16[1,2,8,64,256]{4,3,2,1,0:T(8,128)(2,1)} %param.4), channel_id=1, source_target_pairs={{0,16},{16,32},{32,48},{48,64},{64,80},{80,96},{96,112},{112,128},... | collective-permute-start | bytes 1572872 | tf_op jit(solution)/shard_map/ppermute | solution.py:10
  3.8 1.3 dynamic-slice
  5.7 0.8 bitcast_dynamic-update-slice_fusion
  6.5 14.6 %all-reduce.5 = s32[32]{0:T(128)S(1)} all-reduce(s32[32]{0:T(128)S(1)} %bitcast_dynamic-update-slice_fusion), channel_id=1, replica_groups=mesh['group'=16,'dp'=8,'space'=2] {'group'}, use_global_device_ids=true, to_apply=%add.5 | all-reduce | flops 32 | bytes 256
  22.4 1.1 constant_dynamic-update-slice_fusion
  23.5 5.2 %collective-permute-start.2 = (bf16[1,4,1,64,256]{4,3,2,1,0:T(8,128)(2,1)S(1)}, bf16[1,4,1,64,256]{4,3,2,1,0:T(8,128)(2,1)S(1)}, u32[]{:S(2)}, u32[]{:S(2)}) collective-permute-start(bf16[1,4,1,64,256]{4,3,2,1,0:T(8,128)(2,1)S(1)} %get-tuple-element.13), channel_id=1, source_target_pairs={{1,0},{3,2},{5,4},{7,6},{9,8},{11,10},{13,12},{15,14},{17,16},{19,... | collective-permute-start | bytes 393224 | tf_op jit(solution)/shard_map/ppermute | solution.py:20
  28.8 1.3 collective-permute-start.1
  30.6 1.4 collective-permute-done.1
  32.4 0.9 pad_slice_fusion.1
  33.8 1.4 copy-done
  38.8 0.6 fusion.40
  39.5 0.6 fusion.37
  40.5 2.0 %fusion.74 = (bf16[1,2,8,64,256]{4,3,2,1,0:T(8,128)(2,1)}, f32[2,8,64,256]{3,2,1,0:T(8,128)}) fusion(bf16[1,2,8,64,256]{4,3,2,1,0:T(8,128)(2,1)S(1)} %copy-done.8, f32[2,8,64,256]{3,2,1,0:T(8,128)S(1)} %fusion.37, f32[2]{0:T(128)S(1)} %copy-done.4, f32[2,8,64,256]{3,2,1,0:T(8,128)S(1)} %fusion.34, bf16[3,3,768,256]{3,2,1,0:T(8,128)(2,1)S(1)} %bitcast.450, ...), kind=kOutput, calls=%fused_computation.103 | convolution fusion | flops 406061056 | bytes 6160896 | tf_op jit(solution)/shard_map/sfhwk,kc->sfhwc/dot_general | solution.py:135
  42.5 1.7 fusion.72
  44.2 1.7 fusion.70
  46.0 1.7 fusion.68
  47.7 1.7 fusion.66
  49.4 1.7 fusion.64
  51.1 1.7 fusion.62
  52.8 1.7 fusion.60
  54.5 1.7 fusion.58
  56.2 1.7 fusion.56
  58.0 2.3 %constant_dynamic-slice_fusion.13 = f32[27,128,256]{2,1,0:T(8,128)} fusion(f32[27,256,256]{2,1,0:T(8,128)S(1)} %bitcast.452, s32[]{:T(128)S(6)} %select_n.192), kind=kLoop, calls=%fused_computation.189 | loop fusion | bytes 7077892 | tf_op jit(solution)/shard_map/dynamic_slice | solution.py:28
  60.3 1.6 copy-done.1
  62.0 5.5 %collective-permute-start.3 = (bf16[1,2,8,64,256]{4,3,2,1,0:T(8,128)(2,1)}, bf16[1,2,8,64,256]{4,3,2,1,0:T(8,128)(2,1)}, u32[]{:S(2)}, u32[]{:S(2)}) collective-permute-start(bf16[1,2,8,64,256]{4,3,2,1,0:T(8,128)(2,1)} %get-tuple-element.28), channel_id=1, source_target_pairs={{16,0},{32,16},{48,32},{64,48},{80,64},{96,80},{112,96},{128,112},... | collective-permute-start | bytes 1572872 | tf_op jit(solution)/shard_map/ppermute | solution.py:10
  67.8 4.2 %copy.12 = bf16[3,3,3,256,256]{3,4,2,1,0:T(8,128)(2,1)} copy(bf16[3,3,3,256,256]{4,3,2,1,0:T(8,128)(2,1)S(1)} %bitcast.451) | data formatting | bytes 7077888 | tf_op jit(solution)/shard_map/reshape | solution.py:159
  72.0 6.8 %collective-permute-done.3 = bf16[1,2,8,64,256]{4,3,2,1,0:T(8,128)(2,1)} collective-permute-done((bf16[1,2,8,64,256]{4,3,2,1,0:T(8,128)(2,1)}, bf16[1,2,8,64,256]{4,3,2,1,0:T(8,128)(2,1)}, u32[]{:S(2)}, u32[]{:S(2)}) %collective-permute-start.3) | collective-permute-done | bytes 524320 | tf_op jit(solution)/shard_map/ppermute | solution.py:10
  78.8 1.0 pad_maximum_fusion.4
  79.8 3.1 %collective-permute-start.5 = (bf16[1,4,1,64,256]{4,3,2,1,0:T(8,128)(2,1)S(1)}, bf16[1,4,1,64,256]{4,3,2,1,0:T(8,128)(2,1)S(1)}, u32[]{:S(2)}, u32[]{:S(2)}) collective-permute-start(bf16[1,4,1,64,256]{4,3,2,1,0:T(8,128)(2,1)S(1)} %get-tuple-element.11), channel_id=1, source_target_pairs={{1,0},{3,2},{5,4},{7,6},{9,8},{11,10},{13,12},{15,14},{17,16},{19,... | collective-permute-start | bytes 393224 | tf_op jit(solution)/shard_map/ppermute | solution.py:20
  82.9 1.3 collective-permute-start.4
  84.2 2.3 %fusion.84 = bf16[1,2,8,64,256]{4,3,2,1,0:T(8,128)(2,1)} fusion(f32[2,8,64,256]{3,2,1,0:T(8,128)} %get-tuple-element.29), kind=kLoop, calls=%fused_computation.119 | loop fusion | flops 1310720 | bytes 1572864 | tf_op jit(solution)/shard_map/convert_element_type | solution.py:140
  86.5 2.0 %select_maximum_fusion = bf16[1,4,10,66,256]{4,3,2,1,0:T(8,128)(2,1)S(1)} fusion(bf16[1,4,1,64,256]{4,3,2,1,0:T(8,128)(2,1)S(1)} %collective-permute-done.5, bf16[1,4,1,64,256]{4,3,2,1,0:T(8,128)(2,1)S(1)} %collective-permute-done.4, bf16[1,2,8,64,256]{4,3,2,1,0:T(8,128)(2,1)} %collective-permute-done.3, bf16[1,2,8,64,256]{4,3,2,1,0:T(8,128)(2,1)} %get-tuple-element.28), kind=kLoop, calls=%fused_computation.34 | loop fusion | flops 10137600 | bytes 2662400 | tf_op jit(solution)/shard_map/concatenate | solution.py:21
  88.5 0.9 fusion.115
  89.4 1.6 pad_maximum_fusion.1
  92.3 0.8 slice-done.1
  93.1 2.5 %dynamic-slice_add_fusion = f32[27,128,256]{2,1,0:T(8,128)S(1)} fusion(f32[27,128,256]{2,1,0:T(8,128)} %collective-permute-done.6, f32[27,256,256]{2,1,0:T(8,128)S(1)} %bitcast.455, s32[]{:T(128)S(6)} %select_n.191), kind=kLoop, calls=%fused_computation.4 | loop fusion | flops 884736 | bytes 10616836 | tf_op jit(solution)/shard_map/add | solution.py:30
  96.0 1.4 collective-permute-start.13
  97.4 0.6 fusion.52
  98.1 0.7 collective-permute-start.10
  99.5 1.7 collective-permute-start.7
  101.2 8.7 %collective-permute-done.13 = f32[9,64,256]{2,1,0:T(8,128)S(1)} collective-permute-done((f32[9,64,256]{2,1,0:T(8,128)S(1)}, f32[9,64,256]{2,1,0:T(8,128)S(1)}, u32[]{:S(2)}, u32[]{:S(2)}) %collective-permute-start.13) | collective-permute-done | bytes 589856 | tf_op jit(solution)/shard_map/ppermute | solution.py:30
  110.0 1.7 collective-permute-start.14
  111.9 1.4 collective-permute-start.11
  113.4 0.7 collective-permute-start.8
  114.2 5.2 %collective-permute-done.14 = f32[9,32,256]{2,1,0:T(8,128)S(1)} collective-permute-done((f32[9,32,256]{2,1,0:T(8,128)S(1)}, f32[9,32,256]{2,1,0:T(8,128)S(1)}, u32[]{:S(2)}, u32[]{:S(2)}) %collective-permute-start.14) | collective-permute-done | bytes 294944 | tf_op jit(solution)/shard_map/ppermute | solution.py:30
  119.5 1.2 collective-permute-start.15
  120.8 1.5 collective-permute-start.12
  123.0 2.4 %collective-permute-done.15 = f32[9,16,256]{2,1,0:T(8,128)S(1)} collective-permute-done((f32[9,16,256]{2,1,0:T(8,128)S(1)}, f32[9,16,256]{2,1,0:T(8,128)S(1)}, u32[]{:S(2)}, u32[]{:S(2)}) %collective-permute-start.15) | collective-permute-done | bytes 147488 | tf_op jit(solution)/shard_map/ppermute | solution.py:30
  125.5 1.3 collective-permute-done.9
  126.9 3.7 %collective-permute-start.16 = (f32[3,9,8,256]{3,2,1,0:T(8,128)S(1)}, f32[3,9,8,256]{3,2,1,0:T(8,128)S(1)}, u32[]{:S(2)}, u32[]{:S(2)}) collective-permute-start(f32[3,9,8,256]{3,2,1,0:T(8,128)S(1)} %constant_dynamic-slice_fusion.3), channel_id=1, source_target_pairs={{0,32},{16,48},{32,0},{48,16},{64,96},{80,112},{96,64},{112,80},{1... | collective-permute-start | bytes 663560 | tf_op jit(solution)/shard_map/ppermute | solution.py:30
  131.2 2.7 %collective-permute-done.16 = f32[3,9,8,256]{3,2,1,0:T(8,128)S(1)} collective-permute-done((f32[3,9,8,256]{3,2,1,0:T(8,128)S(1)}, f32[3,9,8,256]{3,2,1,0:T(8,128)S(1)}, u32[]{:S(2)}, u32[]{:S(2)}) %collective-permute-start.16) | collective-permute-done | bytes 221216 | tf_op jit(solution)/shard_map/ppermute | solution.py:30
  134.0 3.2 %collective-permute-start.17 = (f32[3,9,4,256]{3,2,1,0:T(4,128)S(1)}, f32[3,9,4,256]{3,2,1,0:T(4,128)S(1)}, u32[]{:S(2)}, u32[]{:S(2)}) collective-permute-start(f32[3,9,4,256]{3,2,1,0:T(4,128)S(1)} %constant_dynamic-slice_fusion.2), channel_id=1, source_target_pairs={{0,128},{16,144},{32,160},{48,176},{64,192},{80,208},{96,224},{112... | collective-permute-start | bytes 331784 | tf_op jit(solution)/shard_map/ppermute | solution.py:30
  137.2 0.6 fusion.49
  137.8 1.6 collective-permute-done.17
  139.5 3.1 %collective-permute-start.18 = (f32[3,9,2,256]{3,2,1,0:T(2,128)S(1)}, f32[3,9,2,256]{3,2,1,0:T(2,128)S(1)}, u32[]{:S(2)}, u32[]{:S(2)}) collective-permute-start(f32[3,9,2,256]{3,2,1,0:T(2,128)S(1)} %constant_dynamic-slice_fusion.1), channel_id=1, source_target_pairs={{0,4},{2,6},{4,0},{6,2},{8,12},{10,14},{12,8},{14,10},{1,5},{3,7},... | collective-permute-start | bytes 165896 | tf_op jit(solution)/shard_map/ppermute | solution.py:30
  143.1 1.0 collective-permute-done.18
  144.2 6.3 %collective-permute-start.19 = (f32[3,9,1,256]{3,2,1,0:T(1,128)S(1)}, f32[3,9,1,256]{3,2,1,0:T(1,128)S(1)}, u32[]{:S(2)}, u32[]{:S(2)}) collective-permute-start(f32[3,9,1,256]{3,2,1,0:T(1,128)S(1)} %constant_dynamic-slice_fusion), channel_id=1, source_target_pairs={{0,8},{2,10},{4,12},{6,14},{8,0},{10,2},{12,4},{14,6},{1,9},{3,11}... | collective-permute-start | bytes 82952 | tf_op jit(solution)/shard_map/ppermute | solution.py:30
  151.0 0.7 collective-permute-done.19
  151.8 12.8 %collective-permute-start.22 = (f32[9,1,256]{2,1,0:T(1,128)S(1)}, f32[9,1,256]{2,1,0:T(1,128)S(1)}, u32[]{:S(2)}, u32[]{:S(2)}) collective-permute-start(f32[9,1,256]{2,1,0:T(1,128)S(1)} %get-tuple-element.15), channel_id=1, source_target_pairs={{0,0},{1,128},{2,32},{3,160},{4,2},{5,130},{6,34},{7,162},{8,1},{9... | collective-permute-start | bytes 27656 | tf_op jit(solution)/shard_map/ppermute | solution.py:87
  164.6 11.5 %collective-permute-start.21 = (f32[9,1,256]{2,0,1:T(8,128)S(1)}, f32[9,1,256]{2,0,1:T(8,128)S(1)}, u32[]{:S(2)}, u32[]{:S(2)}) collective-permute-start(f32[9,1,256]{2,0,1:T(8,128)S(1)} %bitcast.468), channel_id=1, source_target_pairs={{0,0},{1,128},{2,16},{3,144},{4,2},{5,130},{6,18},{7,146},{8,1},{9... | collective-permute-start | bytes 27656 | tf_op jit(solution)/shard_map/ppermute | solution.py:87
  176.1 1.9 %collective-permute-start.20 = (f32[9,1,256]{2,0,1:T(8,128)S(1)}, f32[9,1,256]{2,0,1:T(8,128)S(1)}, u32[]{:S(2)}, u32[]{:S(2)}) collective-permute-start(f32[9,1,256]{2,0,1:T(8,128)S(1)} %bitcast.469), channel_id=1, source_target_pairs={{0,0},{1,128},{2,64},{3,192},{4,2},{5,130},{6,66},{7,194},{8,1},{9... | collective-permute-start | bytes 27656 | tf_op jit(solution)/shard_map/ppermute | solution.py:87
  178.0 1.4 fusion.73
  179.5 6.2 %collective-permute-done.20 = f32[9,1,256]{2,0,1:T(8,128)S(1)} collective-permute-done((f32[9,1,256]{2,0,1:T(8,128)S(1)}, f32[9,1,256]{2,0,1:T(8,128)S(1)}, u32[]{:S(2)}, u32[]{:S(2)}) %collective-permute-start.20) | collective-permute-done | bytes 9248 | tf_op jit(solution)/shard_map/ppermute | solution.py:87
  185.7 0.6 pad_maximum_fusion.5
  (97 shorter events, 12.6 us)
Async XLA Ops:
  0.6 21.7 %collective-permute-start = (bf16[1,2,8,64,256]{4,3,2,1,0:T(8,128)(2,1)}, bf16[1,2,8,64,256]{4,3,2,1,0:T(8,128)(2,1)S(1)}, u32[]{:S(2)}, u32[]{:S(2)}) collective-permute-start(bf16[1,2,8,64,256]{4,3,2,1,0:T(8,128)(2,1)} %param.4), channel_id=1, source_target_pairs={{0,16},{16,32},{32,48},{48,64},{64,80},{80,96},{96,112},{112,128},... | collective-permute-start | bytes 1572872 | tf_op jit(solution)/shard_map/ppermute | solution.py:10
  23.5 7.0 %collective-permute-start.2 = (bf16[1,4,1,64,256]{4,3,2,1,0:T(8,128)(2,1)S(1)}, bf16[1,4,1,64,256]{4,3,2,1,0:T(8,128)(2,1)S(1)}, u32[]{:S(2)}, u32[]{:S(2)}) collective-permute-start(bf16[1,4,1,64,256]{4,3,2,1,0:T(8,128)(2,1)S(1)} %get-tuple-element.13), channel_id=1, source_target_pairs={{1,0},{3,2},{5,4},{7,6},{9,8},{11,10},{13,12},{15,14},{17,16},{19,... | collective-permute-start | bytes 393224 | tf_op jit(solution)/shard_map/ppermute | solution.py:20
  28.8 3.2 %collective-permute-start.1 = (bf16[1,4,1,64,256]{4,3,2,1,0:T(8,128)(2,1)S(1)}, bf16[1,4,1,64,256]{4,3,2,1,0:T(8,128)(2,1)S(1)}, u32[]{:S(2)}, u32[]{:S(2)}) collective-permute-start(bf16[1,4,1,64,256]{4,3,2,1,0:T(8,128)(2,1)S(1)} %get-tuple-element.12), channel_id=1, source_target_pairs={{0,1},{2,3},{4,5},{6,7},{8,9},{10,11},{12,13},{14,15},{16,17},{18,... | collective-permute-start | bytes 393224 | tf_op jit(solution)/shard_map/ppermute | solution.py:17
  33.3 2.0 %copy-start = (bf16[6912,256]{1,0:T(8,128)(2,1)S(1)}, bf16[6912,256]{1,0:T(8,128)(2,1)}, u32[]{:S(2)}) copy-start(bf16[6912,256]{1,0:T(8,128)(2,1)} %param.6) | copy-start | bytes 10616836
  39.5 0.7 copy-start.4
  39.5 1.0 copy-start.8
  40.5 2.0 %copy-start.7 = (bf16[2]{0:T(256)(128)(2,1)S(1)}, bf16[2]{0:T(256)(128)(2,1)}, u32[]{:S(2)}) copy-start(bf16[2]{0:T(256)(128)(2,1)} %get-tuple-element.25) | copy-start | bytes 16
  45.9 1.7 copy-start.6
  51.1 1.7 copy-start.5
  58.0 3.9 %copy-start.1 = (f32[9,768,256]{2,1,0:T(8,128)}, f32[9,768,256]{2,1,0:T(8,128)S(1)}, u32[]{:S(2)}) copy-start(f32[9,768,256]{2,1,0:T(8,128)S(1)} %fusion.56) | copy-start | bytes 21233668
  61.9 30.3 %collective-permute-start.6 = (f32[27,128,256]{2,1,0:T(8,128)}, f32[27,128,256]{2,1,0:T(8,128)}, u32[]{:S(2)}, u32[]{:S(2)}) collective-permute-start(f32[27,128,256]{2,1,0:T(8,128)} %constant_dynamic-slice_fusion.13), channel_id=1, source_target_pairs={{0,1},{1,0},{2,3},{3,2},{4,5},{5,4},{6,7},{7,6},{8,9},{9,8},{10,11... | collective-permute-start | bytes 10616840 | tf_op jit(solution)/shard_map/ppermute | solution.py:30
  62.0 16.8 %collective-permute-start.3 = (bf16[1,2,8,64,256]{4,3,2,1,0:T(8,128)(2,1)}, bf16[1,2,8,64,256]{4,3,2,1,0:T(8,128)(2,1)}, u32[]{:S(2)}, u32[]{:S(2)}) collective-permute-start(bf16[1,2,8,64,256]{4,3,2,1,0:T(8,128)(2,1)} %get-tuple-element.28), channel_id=1, source_target_pairs={{16,0},{32,16},{48,32},{64,48},{80,64},{96,80},{112,96},{128,112},... | collective-permute-start | bytes 1572872 | tf_op jit(solution)/shard_map/ppermute | solution.py:10
  79.8 6.7 %collective-permute-start.5 = (bf16[1,4,1,64,256]{4,3,2,1,0:T(8,128)(2,1)S(1)}, bf16[1,4,1,64,256]{4,3,2,1,0:T(8,128)(2,1)S(1)}, u32[]{:S(2)}, u32[]{:S(2)}) collective-permute-start(bf16[1,4,1,64,256]{4,3,2,1,0:T(8,128)(2,1)S(1)} %get-tuple-element.11), channel_id=1, source_target_pairs={{1,0},{3,2},{5,4},{7,6},{9,8},{11,10},{13,12},{15,14},{17,16},{19,... | collective-permute-start | bytes 393224 | tf_op jit(solution)/shard_map/ppermute | solution.py:20
  82.9 3.6 %collective-permute-start.4 = (bf16[1,4,1,64,256]{4,3,2,1,0:T(8,128)(2,1)S(1)}, bf16[1,4,1,64,256]{4,3,2,1,0:T(8,128)(2,1)S(1)}, u32[]{:S(2)}, u32[]{:S(2)}) collective-permute-start(bf16[1,4,1,64,256]{4,3,2,1,0:T(8,128)(2,1)S(1)} %get-tuple-element.10), channel_id=1, source_target_pairs={{0,1},{2,3},{4,5},{6,7},{8,9},{10,11},{12,13},{14,15},{16,17},{18,... | collective-permute-start | bytes 393224 | tf_op jit(solution)/shard_map/ppermute | solution.py:17
  88.5 2.5 %copy-start.2 = (bf16[3,3,3,256,256]{3,4,2,1,0:T(8,128)(2,1)S(1)}, bf16[3,3,3,256,256]{3,4,2,1,0:T(8,128)(2,1)}, u32[]{:S(2)}) copy-start(bf16[3,3,3,256,256]{3,4,2,1,0:T(8,128)(2,1)} %copy.12) | copy-start | bytes 10616836
  89.4 2.9 %slice-start = ((s8[7077888]{0:T(1024)(128)(4,1)}), s8[4194304]{0:T(1024)(128)(4,1)S(1)}, s32[]{:S(2)}) async-start(s8[7077888]{0:T(1024)(128)(4,1)} %bitcast.453), calls=%async_computation | async-start | bytes 8388608
  89.4 3.7 %slice-start.1 = ((s8[7077888]{0:T(1024)(128)(4,1)}), s8[2883584]{0:T(1024)(128)(4,1)S(1)}, s32[]{:S(2)}) async-start(s8[7077888]{0:T(1024)(128)(4,1)} %bitcast.453), calls=%async_computation.1 | async-start | bytes 5767168
  95.6 1.8 copy-start.3
  96.0 13.8 %collective-permute-start.13 = (f32[9,64,256]{2,1,0:T(8,128)S(1)}, f32[9,64,256]{2,1,0:T(8,128)S(1)}, u32[]{:S(2)}, u32[]{:S(2)}) collective-permute-start(f32[9,64,256]{2,1,0:T(8,128)S(1)} %constant_dynamic-slice_fusion.6), channel_id=1, source_target_pairs={{0,64},{16,80},{32,96},{48,112},{64,0},{80,16},{96,32},{112,48},{1... | collective-permute-start | bytes 1769480 | tf_op jit(solution)/shard_map/ppermute | solution.py:30
  98.1 13.7 %collective-permute-start.10 = (f32[9,64,256]{2,1,0:T(8,128)S(1)}, f32[9,64,256]{2,1,0:T(8,128)S(1)}, u32[]{:S(2)}, u32[]{:S(2)}) collective-permute-start(f32[9,64,256]{2,1,0:T(8,128)S(1)} %constant_dynamic-slice_fusion.9), channel_id=1, source_target_pairs={{0,16},{16,0},{32,48},{48,32},{64,80},{80,64},{96,112},{112,96},{1... | collective-permute-start | bytes 1769480 | tf_op jit(solution)/shard_map/ppermute | solution.py:30
  99.5 13.8 %collective-permute-start.7 = (f32[9,64,256]{2,1,0:T(8,128)S(1)}, f32[9,64,256]{2,1,0:T(8,128)S(1)}, u32[]{:S(2)}, u32[]{:S(2)}) collective-permute-start(f32[9,64,256]{2,1,0:T(8,128)S(1)} %constant_dynamic-slice_fusion.12), channel_id=1, source_target_pairs={{0,2},{2,0},{4,6},{6,4},{8,10},{10,8},{12,14},{14,12},{1,3},{3,1},... | collective-permute-start | bytes 1769480 | tf_op jit(solution)/shard_map/ppermute | solution.py:30
  110.0 9.4 %collective-permute-start.14 = (f32[9,32,256]{2,1,0:T(8,128)S(1)}, f32[9,32,256]{2,1,0:T(8,128)S(1)}, u32[]{:S(2)}, u32[]{:S(2)}) collective-permute-start(f32[9,32,256]{2,1,0:T(8,128)S(1)} %constant_dynamic-slice_fusion.5), channel_id=1, source_target_pairs={{0,2},{2,0},{4,6},{6,4},{8,10},{10,8},{12,14},{14,12},{1,3},{3,1},... | collective-permute-start | bytes 884744 | tf_op jit(solution)/shard_map/ppermute | solution.py:30
  111.9 8.8 %collective-permute-start.11 = (f32[9,32,256]{2,1,0:T(8,128)S(1)}, f32[9,32,256]{2,1,0:T(8,128)S(1)}, u32[]{:S(2)}, u32[]{:S(2)}) collective-permute-start(f32[9,32,256]{2,1,0:T(8,128)S(1)} %constant_dynamic-slice_fusion.8), channel_id=1, source_target_pairs={{0,64},{16,80},{32,96},{48,112},{64,0},{80,16},{96,32},{112,48},{1... | collective-permute-start | bytes 884744 | tf_op jit(solution)/shard_map/ppermute | solution.py:30
  113.4 8.9 %collective-permute-start.8 = (f32[9,32,256]{2,1,0:T(8,128)S(1)}, f32[9,32,256]{2,1,0:T(8,128)S(1)}, u32[]{:S(2)}, u32[]{:S(2)}) collective-permute-start(f32[9,32,256]{2,1,0:T(8,128)S(1)} %constant_dynamic-slice_fusion.11), channel_id=1, source_target_pairs={{0,16},{16,0},{32,48},{48,32},{64,80},{80,64},{96,112},{112,96},{1... | collective-permute-start | bytes 884744 | tf_op jit(solution)/shard_map/ppermute | solution.py:30
  119.5 6.0 %collective-permute-start.15 = (f32[9,16,256]{2,1,0:T(8,128)S(1)}, f32[9,16,256]{2,1,0:T(8,128)S(1)}, u32[]{:S(2)}, u32[]{:S(2)}) collective-permute-start(f32[9,16,256]{2,1,0:T(8,128)S(1)} %constant_dynamic-slice_fusion.4), channel_id=1, source_target_pairs={{0,16},{16,0},{32,48},{48,32},{64,80},{80,64},{96,112},{112,96},{1... | collective-permute-start | bytes 442376 | tf_op jit(solution)/shard_map/ppermute | solution.py:30
  120.8 4.7 %collective-permute-start.12 = (f32[9,16,256]{2,1,0:T(8,128)S(1)}, f32[9,16,256]{2,1,0:T(8,128)S(1)}, u32[]{:S(2)}, u32[]{:S(2)}) collective-permute-start(f32[9,16,256]{2,1,0:T(8,128)S(1)} %constant_dynamic-slice_fusion.7), channel_id=1, source_target_pairs={{0,2},{2,0},{4,6},{6,4},{8,10},{10,8},{12,14},{14,12},{1,3},{3,1},... | collective-permute-start | bytes 442376 | tf_op jit(solution)/shard_map/ppermute | solution.py:30
  122.4 4.4 %collective-permute-start.9 = (f32[9,16,256]{2,1,0:T(8,128)S(1)}, f32[9,16,256]{2,1,0:T(8,128)S(1)}, u32[]{:S(2)}, u32[]{:S(2)}) collective-permute-start(f32[9,16,256]{2,1,0:T(8,128)S(1)} %constant_dynamic-slice_fusion.10), channel_id=1, source_target_pairs={{0,64},{16,80},{32,96},{48,112},{64,0},{80,16},{96,32},{112,48},{1... | collective-permute-start | bytes 442376 | tf_op jit(solution)/shard_map/ppermute | solution.py:30
  126.9 7.0 %collective-permute-start.16 = (f32[3,9,8,256]{3,2,1,0:T(8,128)S(1)}, f32[3,9,8,256]{3,2,1,0:T(8,128)S(1)}, u32[]{:S(2)}, u32[]{:S(2)}) collective-permute-start(f32[3,9,8,256]{3,2,1,0:T(8,128)S(1)} %constant_dynamic-slice_fusion.3), channel_id=1, source_target_pairs={{0,32},{16,48},{32,0},{48,16},{64,96},{80,112},{96,64},{112,80},{1... | collective-permute-start | bytes 663560 | tf_op jit(solution)/shard_map/ppermute | solution.py:30
  134.0 5.4 %collective-permute-start.17 = (f32[3,9,4,256]{3,2,1,0:T(4,128)S(1)}, f32[3,9,4,256]{3,2,1,0:T(4,128)S(1)}, u32[]{:S(2)}, u32[]{:S(2)}) collective-permute-start(f32[3,9,4,256]{3,2,1,0:T(4,128)S(1)} %constant_dynamic-slice_fusion.2), channel_id=1, source_target_pairs={{0,128},{16,144},{32,160},{48,176},{64,192},{80,208},{96,224},{112... | collective-permute-start | bytes 331784 | tf_op jit(solution)/shard_map/ppermute | solution.py:30
  139.5 4.6 %collective-permute-start.18 = (f32[3,9,2,256]{3,2,1,0:T(2,128)S(1)}, f32[3,9,2,256]{3,2,1,0:T(2,128)S(1)}, u32[]{:S(2)}, u32[]{:S(2)}) collective-permute-start(f32[3,9,2,256]{3,2,1,0:T(2,128)S(1)} %constant_dynamic-slice_fusion.1), channel_id=1, source_target_pairs={{0,4},{2,6},{4,0},{6,2},{8,12},{10,14},{12,8},{14,10},{1,5},{3,7},... | collective-permute-start | bytes 165896 | tf_op jit(solution)/shard_map/ppermute | solution.py:30
  144.2 7.6 %collective-permute-start.19 = (f32[3,9,1,256]{3,2,1,0:T(1,128)S(1)}, f32[3,9,1,256]{3,2,1,0:T(1,128)S(1)}, u32[]{:S(2)}, u32[]{:S(2)}) collective-permute-start(f32[3,9,1,256]{3,2,1,0:T(1,128)S(1)} %constant_dynamic-slice_fusion), channel_id=1, source_target_pairs={{0,8},{2,10},{4,12},{6,14},{8,0},{10,2},{12,4},{14,6},{1,9},{3,11}... | collective-permute-start | bytes 82952 | tf_op jit(solution)/shard_map/ppermute | solution.py:30
  151.8 27.7 %collective-permute-start.22 = (f32[9,1,256]{2,1,0:T(1,128)S(1)}, f32[9,1,256]{2,1,0:T(1,128)S(1)}, u32[]{:S(2)}, u32[]{:S(2)}) collective-permute-start(f32[9,1,256]{2,1,0:T(1,128)S(1)} %get-tuple-element.15), channel_id=1, source_target_pairs={{0,0},{1,128},{2,32},{3,160},{4,2},{5,130},{6,34},{7,162},{8,1},{9... | collective-permute-start | bytes 27656 | tf_op jit(solution)/shard_map/ppermute | solution.py:87
  164.6 14.9 %collective-permute-start.21 = (f32[9,1,256]{2,0,1:T(8,128)S(1)}, f32[9,1,256]{2,0,1:T(8,128)S(1)}, u32[]{:S(2)}, u32[]{:S(2)}) collective-permute-start(f32[9,1,256]{2,0,1:T(8,128)S(1)} %bitcast.468), channel_id=1, source_target_pairs={{0,0},{1,128},{2,16},{3,144},{4,2},{5,130},{6,18},{7,146},{8,1},{9... | collective-permute-start | bytes 27656 | tf_op jit(solution)/shard_map/ppermute | solution.py:87
  176.1 9.6 %collective-permute-start.20 = (f32[9,1,256]{2,0,1:T(8,128)S(1)}, f32[9,1,256]{2,0,1:T(8,128)S(1)}, u32[]{:S(2)}, u32[]{:S(2)}) collective-permute-start(f32[9,1,256]{2,0,1:T(8,128)S(1)} %bitcast.469), channel_id=1, source_target_pairs={{0,0},{1,128},{2,64},{3,192},{4,2},{5,130},{6,66},{7,194},{8,1},{9... | collective-permute-start | bytes 27656 | tf_op jit(solution)/shard_map/ppermute | solution.py:87
where the time goes:
time: 188 us; the launch traced here: 186 us
  starting transfers between devices  73.2 us (39%)
  waiting for transfers between devices  38.1 us (20%)
  matrix products  28.2 us (15%)
  local copies, waits for them, and re-layouts  17.2 us (9%)
  blocking collectives  14.6 us (8%)
  other arithmetic  12.8 us (7%)
  between operations  2.21 us (1%)
    ppermute x14, starting transfers between devices, halve(): return keep + lax.ppermute(give, axis, pairs)  27.4 us
    ppermute x3, starting transfers between devices, reduce_weight_grad(): parts.append(lax.ppermute(joined[n], names, pairs).reshape(per, outs))  26.2 us
    ppermute x14, waiting for transfers between devices, halve(): return keep + lax.ppermute(give, axis, pairs)  23.6 us
    dot_general x9, matrix products, local(): jnp.einsum('sfhwk,sfhwc->kc', block, masked, preferred_element_type=jnp.f...  15.3 us
    unnamed x1, blocking collectives  14.6 us
    ppermute x2, starting transfers between devices, passed_along(): return lax.ppermute(value, axis, pairs)  8.67 us
    ppermute x2, starting transfers between devices, row_halo(): high = lax.ppermute(lax.slice_in_dim(block, 0, 1, axis=dim), axis, backward)  8.29 us
    ppermute x2, waiting for transfers between devices, passed_along(): return lax.ppermute(value, axis, pairs)  6.83 us
  transfers between devices with their start and end apart: 23, of which 11 were waited for; matrix products, arithmetic and copies ran while one was open for 12% of the time, Pallas kernels for 0%

commit v1 on v0

--- a/solution.py
+++ b/solution.py
@@ -59,14 +59,13 @@
     ng = sizes["group"]
     across = 4 if ng % 4 == 0 else ng
     down = ng // across
-    assert chans == ng * sizes["dp"] * sizes["space"]
+    assert chans * sizes["space"] == ng * sizes["dp"] * sizes["space"]
     first = ("space", 1)
     ys = [("group", across << b) for b in range(bits_of(down))]
     xs = [("group", 1 << b) for b in range(bits_of(across))]
     ds = [("dp", 1 << b) for b in range(bits_of(sizes["dp"]))]
     assert sizes["space"] == 2
     lanes = (ds, xs, ys)
-    total = halve(total, 1, *first)
     spread = [lane[0] for lane in lanes]
     rest = [key for lane in (xs, ys, ds) for key in lane[1:]]
     per = ntaps // len(lanes)
@@ -143,15 +142,22 @@
     )
     ahead = passed_along(lax.slice_in_dim(delta, 0, 2, axis=1), "group", -1)
     gwide = row_halo(jnp.concatenate([delta, ahead], axis=1), "space", 2)
+    swap = [(0, 1), (1, 0)]
+    half = chans // 2
+    both = jnp.concatenate([shifted, lax.ppermute(shifted, "space", swap)], axis=0)
+    both = lax.dynamic_slice_in_dim(both, lax.axis_index("space") * half, half, axis=4)
+    both = jnp.pad(both, ((0, 0), (0, 0), (0, 0), (1, 1), (0, 0)))
+    bstack = jnp.concatenate([both[:, :, :, b : b + cols] for b in range(3)], axis=4)
+    bdelta = jnp.concatenate([delta, lax.ppermute(delta, "space", swap)], axis=0)
     terms = []
     for k in range(3):
-        masked = delta * same_fwd[k].astype(jnp.bfloat16)[:, :, None, None, None]
+        masked = bdelta * same_fwd[k].astype(jnp.bfloat16)[:, :, None, None, None]
         for a in range(3):
-            block = stacked[:, 2 - k : 2 - k + frames, a : a + rows]
+            block = bstack[:, 2 - k : 2 - k + frames, a : a + rows]
             terms.append(
                 jnp.einsum("sfhwk,sfhwc->kc", block, masked, preferred_element_type=jnp.float32)
             )
-    total = jnp.stack(terms).reshape(27, chans, chans)
+    total = jnp.stack(terms).reshape(27, half, chans)
     reduced = reduce_weight_grad(total)
     gwide = jnp.pad(gwide, ((0, 0), (0, 0), (0, 0), (1, 1), (0, 0)))
     gstack = jnp.concatenate([gwide[:, :, :, 2 - b : 2 - b + cols] for b in range(3)], axis=4)

time: 188 us -> 174 us (0.926)
  matrix products: 28.2 us -> 19.4 us
  other arithmetic: 12.8 us -> 8.03 us
  waiting for transfers between devices: 38.1 us -> 35.9 us
    dot_general x9, matrix products: 15.3 us -> 6.78 us  [local(): jnp.einsum('sfhwk,sfhwc->kc', block, masked, preferred_element_type=jnp.f...]
    ppermute x2, waiting for transfers between devices: 6.83 us -> 3.24 us  [passed_along(): return lax.ppermute(value, axis, pairs)]
    slice x1 -> x2, local copies, waits for them, and re-layouts: 0.37 us -> 3.64 us  [the longest x1 2.31 us: local(): block = bstack[:, 2 - k:2 - k + frames, a:a + rows]]
    add x11 -> x10, other arithmetic: 3.08 us -> 0.5 us  [halve(): return keep + lax.ppermute(give, axis, pairs)]
    dynamic_slice x14 -> x13, local copies, waits for them, and re-layouts: 2.71 us -> 0.41 us  [halve(): give = lax.dynamic_slice_in_dim(x, (1 - bit) * size, size, axis=dim)]
    mul x0 -> x1, other arithmetic: none -> 1.88 us  [local(): masked = bdelta * same_fwd[k].astype(jnp.bfloat16)[:, :, None, None, None]]
    ppermute x14 -> x13, waiting for transfers between devices: 23.6 us -> 24.5 us  [halve(): return keep + lax.ppermute(give, axis, pairs)]
    unnamed x29 -> x21, local copies, waits for them, and re-layouts: 6.45 us -> 5.72 us
  transfers between devices with their start and end apart: 23 -> 24, of which waited for: 11 -> 13; matrix products, arithmetic and copies ran while one was open for 12% -> 15% of each run, Pallas kernels for 0% -> 0%
where the time goes in v1:
time: 174 us; the launch traced here: 173 us
  starting transfers between devices  73.7 us (42%)
  waiting for transfers between devices  35.9 us (21%)
  matrix products  19.4 us (11%)
  local copies, waits for them, and re-layouts  18.8 us (11%)
  blocking collectives  14.6 us (8%)
  other arithmetic  8.03 us (5%)
  between operations  2.22 us (1%)
    ppermute x3, starting transfers between devices, reduce_weight_grad(): parts.append(lax.ppermute(joined[n], names, pairs).reshape(per, outs))  26.8 us
    ppermute x13, starting transfers between devices, halve(): return keep + lax.ppermute(give, axis, pairs)  26.8 us
    ppermute x13, waiting for transfers between devices, halve(): return keep + lax.ppermute(give, axis, pairs)  24.5 us
    unnamed x1, blocking collectives  14.6 us
    ppermute x2, starting transfers between devices, passed_along(): return lax.ppermute(value, axis, pairs)  8.67 us
    ppermute x2, starting transfers between devices, row_halo(): high = lax.ppermute(lax.slice_in_dim(block, 0, 1, axis=dim), axis, backward)  8.06 us
    dot_general x9, matrix products, local(): jnp.einsum('sfhwk,kc->sfhwc', block, back[k, a], preferred_element_type=j...  6.96 us
    dot_general x9, matrix products, local(): jnp.einsum('sfhwk,sfhwc->kc', block, masked, preferred_element_type=jnp.f...  6.78 us
  transfers between devices with their start and end apart: 24, of which 13 were waited for; matrix products, arithmetic and copies ran while one was open for 15% of the time, Pallas kernels for 0%

profile of v1, /device:TPU:25, one launch (start us, length us, event | category | flops | bytes accessed | tf_op | source)
XLA Modules:
  0.0 172.6 jit_solution(11079367132503185056)
XLA Ops:
  0.6 3.1 %collective-permute-start = (bf16[1,2,8,64,256]{4,3,2,1,0:T(8,128)(2,1)}, bf16[1,2,8,64,256]{4,3,2,1,0:T(8,128)(2,1)S(1)}, u32[]{:S(2)}, u32[]{:S(2)}) collective-permute-start(bf16[1,2,8,64,256]{4,3,2,1,0:T(8,128)(2,1)} %param.4), channel_id=1, source_target_pairs={{0,16},{16,32},{32,48},{48,64},{64,80},{80,96},{96,112},{112,128},... | collective-permute-start | bytes 1572872 | tf_op jit(solution)/shard_map/ppermute | solution.py:10
  3.8 1.3 dynamic-slice
  5.7 0.8 bitcast_dynamic-update-slice_fusion
  6.5 14.6 %all-reduce.6 = s32[32]{0:T(128)S(1)} all-reduce(s32[32]{0:T(128)S(1)} %bitcast_dynamic-update-slice_fusion), channel_id=1, replica_groups=mesh['group'=16,'dp'=8,'space'=2] {'group'}, use_global_device_ids=true, to_apply=%add.6 | all-reduce | flops 32 | bytes 256
  21.8 1.1 constant_dynamic-update-slice_fusion
  22.9 5.2 %collective-permute-start.2 = (bf16[1,4,1,64,256]{4,3,2,1,0:T(8,128)(2,1)S(1)}, bf16[1,4,1,64,256]{4,3,2,1,0:T(8,128)(2,1)S(1)}, u32[]{:S(2)}, u32[]{:S(2)}) collective-permute-start(bf16[1,4,1,64,256]{4,3,2,1,0:T(8,128)(2,1)S(1)} %get-tuple-element.24), channel_id=1, source_target_pairs={{1,0},{3,2},{5,4},{7,6},{9,8},{11,10},{13,12},{15,14},{17,16},{19,... | collective-permute-start | bytes 393224 | tf_op jit(solution)/shard_map/ppermute | solution.py:20
  28.2 1.3 collective-permute-start.1
  29.5 1.9 %collective-permute-done.1 = bf16[1,4,1,64,256]{4,3,2,1,0:T(8,128)(2,1)S(1)} collective-permute-done((bf16[1,4,1,64,256]{4,3,2,1,0:T(8,128)(2,1)S(1)}, bf16[1,4,1,64,256]{4,3,2,1,0:T(8,128)(2,1)S(1)}, u32[]{:S(2)}, u32[]{:S(2)}) %collective-permute-start.1) | collective-permute-done | bytes 131104 | tf_op jit(solution)/shard_map/ppermute | solution.py:17
  31.8 0.9 pad_slice_fusion.3
  33.0 1.6 copy-done.1
  38.1 0.6 fusion.50
  39.8 1.0 fusion.93
  40.8 5.5 %collective-permute-start.3 = (bf16[1,2,8,64,256]{4,3,2,1,0:T(8,128)(2,1)S(1)}, bf16[1,2,8,64,256]{4,3,2,1,0:T(8,128)(2,1)S(1)}, u32[]{:S(2)}, u32[]{:S(2)}) collective-permute-start(bf16[1,2,8,64,256]{4,3,2,1,0:T(8,128)(2,1)S(1)} %get-tuple-element.39), channel_id=1, source_target_pairs={{16,0},{32,16},{48,32},{64,48},{80,64},{96,80},{112,96},{128,112},... | collective-permute-start | bytes 1572872 | tf_op jit(solution)/shard_map/ppermute | solution.py:10
  46.6 6.0 %copy.34 = bf16[3,3,3,256,256]{3,4,2,1,0:T(8,128)(2,1)} copy(bf16[3,3,3,256,256]{4,3,2,1,0:T(8,128)(2,1)} %bitcast.369) | data formatting | bytes 7077888 | tf_op jit(solution)/shard_map/reshape | solution.py:165
  53.2 1.1 fusion.103
  54.3 3.2 %collective-permute-done.3 = bf16[1,2,8,64,256]{4,3,2,1,0:T(8,128)(2,1)S(1)} collective-permute-done((bf16[1,2,8,64,256]{4,3,2,1,0:T(8,128)(2,1)S(1)}, bf16[1,2,8,64,256]{4,3,2,1,0:T(8,128)(2,1)S(1)}, u32[]{:S(2)}, u32[]{:S(2)}) %collective-permute-start.3) | collective-permute-done | bytes 524320 | tf_op jit(solution)/shard_map/ppermute | solution.py:10
  57.6 2.8 %collective-permute-start.5 = (bf16[1,4,1,64,256]{4,3,2,1,0:T(8,128)(2,1)S(1)}, bf16[1,4,1,64,256]{4,3,2,1,0:T(8,128)(2,1)S(1)}, u32[]{:S(2)}, u32[]{:S(2)}) collective-permute-start(bf16[1,4,1,64,256]{4,3,2,1,0:T(8,128)(2,1)S(1)} %get-tuple-element.22), channel_id=1, source_target_pairs={{1,0},{3,2},{5,4},{7,6},{9,8},{11,10},{13,12},{15,14},{17,16},{19,... | collective-permute-start | bytes 393224 | tf_op jit(solution)/shard_map/ppermute | solution.py:20
  60.4 1.5 collective-permute-start.4
  61.9 1.9 %broadcast_multiply_fusion.2 = (bf16[2,2,8,64,256]{4,3,2,1,0:T(8,128)(2,1)}, bf16[2,2,8,64,256]{4,3,2,1,0:T(8,128)(2,1)}, bf16[2,2,8,64,256]{4,3,2,1,0:T(8,128)(2,1)}) fusion(bf16[2]{0:T(256)(128)(2,1)S(1)} %get-tuple-element.31, bf16[1,2,8,64,256]{4,3,2,1,0:T(8,128)(2,1)S(1)} %collective-permute-done.7, ...), kind=kLoop, calls=%fused_computation.130 | loop fusion | flops 2097152 | bytes 4194316 | tf_op jit(solution)/shard_map/mul | solution.py:154
  63.8 0.8 select_maximum_fusion
  64.6 0.9 fusion.116
  66.0 1.6 copy-done
  68.7 1.6 fusion.4
  71.1 1.3 pad_slice_fusion.1
  72.5 0.6 pad_maximum_fusion.2
  73.1 2.3 %fusion.115 = (bf16[2,2,8,64,384]{4,3,2,1,0:T(8,128)(2,1)S(1)}, bf16[2,2,8,64,384]{4,3,2,1,0:T(8,128)(2,1)S(1)}, bf16[2,2,8,64,384]{4,3,2,1,0:T(8,128)(2,1)S(1)}...) fusion(bf16[2,4,10,64,384]{4,3,2,1,0:T(8,128)(2,1)S(1)} %pad_ma, ...), kind=kLoop, calls=%fused_computation.215 | loop fusion | bytes 28311552 | tf_op jit(solution)/shard_map/slice | solution.py:156
  75.4 1.9 %fusion.90 = f32[1,384,256]{2,1,0:T(8,128)S(1)} fusion(bf16[2,2,8,64,384]{4,3,2,1,0:T(8,128)(2,1)S(1)} %get-tuple-element.4, bf16[2,2,8,64,256]{4,3,2,1,0:T(8,128)(2,1)} %get-tuple-element.20), kind=kOutput, calls=%fused_computation.106 | convolution fusion | flops 402653184 | bytes 3014656 | tf_op jit(solution)/shard_map/sfhwk,sfhwc->kc/dot_general | solution.py:158
  77.4 0.6 fusion.87
  78.0 0.6 fusion.84
  78.7 1.4 collective-permute-start.14
  80.1 0.6 fusion.81
  80.7 0.6 fusion.78
  81.4 0.6 fusion.75
  82.1 1.2 collective-permute-start.11
  83.4 0.6 fusion.72
  84.0 0.6 fusion.69
  84.6 0.6 fusion.66
  85.4 1.7 collective-permute-start.8
  87.1 5.5 %collective-permute-done.14 = f32[9,64,256]{2,1,0:T(8,128)S(1)} collective-permute-done((f32[9,64,256]{2,1,0:T(8,128)S(1)}, f32[9,64,256]{2,1,0:T(8,128)S(1)}, u32[]{:S(2)}, u32[]{:S(2)}) %collective-permute-start.14) | collective-permute-done | bytes 589856 | tf_op jit(solution)/shard_map/ppermute | solution.py:30
  92.7 1.7 collective-permute-start.15
  94.4 1.5 collective-permute-done.11
  96.0 1.4 collective-permute-start.12
  97.4 1.9 %collective-permute-done.8 = f32[9,64,256]{2,1,0:T(8,128)S(1)} collective-permute-done((f32[9,64,256]{2,1,0:T(8,128)S(1)}, f32[9,64,256]{2,1,0:T(8,128)S(1)}, u32[]{:S(2)}, u32[]{:S(2)}) %collective-permute-start.8) | collective-permute-done | bytes 589856 | tf_op jit(solution)/shard_map/ppermute | solution.py:30
  99.4 0.8 collective-permute-start.9
  100.2 5.4 %collective-permute-done.15 = f32[9,32,256]{2,1,0:T(8,128)S(1)} collective-permute-done((f32[9,32,256]{2,1,0:T(8,128)S(1)}, f32[9,32,256]{2,1,0:T(8,128)S(1)}, u32[]{:S(2)}, u32[]{:S(2)}) %collective-permute-start.15) | collective-permute-done | bytes 294944 | tf_op jit(solution)/shard_map/ppermute | solution.py:30
  105.7 0.8 collective-permute-start.16
  106.5 1.4 collective-permute-start.13
  108.0 0.9 collective-permute-start.10
  108.9 2.5 %collective-permute-done.16 = f32[9,16,256]{2,1,0:T(8,128)S(1)} collective-permute-done((f32[9,16,256]{2,1,0:T(8,128)S(1)}, f32[9,16,256]{2,1,0:T(8,128)S(1)}, u32[]{:S(2)}, u32[]{:S(2)}) %collective-permute-start.16) | collective-permute-done | bytes 147488 | tf_op jit(solution)/shard_map/ppermute | solution.py:30
  111.4 0.9 collective-permute-done.10
  112.4 3.7 %collective-permute-start.17 = (f32[3,9,8,256]{3,2,1,0:T(8,128)S(1)}, f32[3,9,8,256]{3,2,1,0:T(8,128)S(1)}, u32[]{:S(2)}, u32[]{:S(2)}) collective-permute-start(f32[3,9,8,256]{3,2,1,0:T(8,128)S(1)} %constant_dynamic-slice_fusion.3), channel_id=1, source_target_pairs={{0,32},{16,48},{32,0},{48,16},{64,96},{80,112},{96,64},{112,80},{1... | collective-permute-start | bytes 663560 | tf_op jit(solution)/shard_map/ppermute | solution.py:30
  116.7 2.7 %collective-permute-done.17 = f32[3,9,8,256]{3,2,1,0:T(8,128)S(1)} collective-permute-done((f32[3,9,8,256]{3,2,1,0:T(8,128)S(1)}, f32[3,9,8,256]{3,2,1,0:T(8,128)S(1)}, u32[]{:S(2)}, u32[]{:S(2)}) %collective-permute-start.17) | collective-permute-done | bytes 221216 | tf_op jit(solution)/shard_map/ppermute | solution.py:30
  119.5 3.3 %collective-permute-start.18 = (f32[3,9,4,256]{3,2,1,0:T(4,128)S(1)}, f32[3,9,4,256]{3,2,1,0:T(4,128)S(1)}, u32[]{:S(2)}, u32[]{:S(2)}) collective-permute-start(f32[3,9,4,256]{3,2,1,0:T(4,128)S(1)} %constant_dynamic-slice_fusion.2), channel_id=1, source_target_pairs={{0,128},{16,144},{32,160},{48,176},{64,192},{80,208},{96,224},{112... | collective-permute-start | bytes 331784 | tf_op jit(solution)/shard_map/ppermute | solution.py:30
  123.4 1.6 collective-permute-done.18
  125.1 3.1 %collective-permute-start.19 = (f32[3,9,2,256]{3,2,1,0:T(2,128)S(1)}, f32[3,9,2,256]{3,2,1,0:T(2,128)S(1)}, u32[]{:S(2)}, u32[]{:S(2)}) collective-permute-start(f32[3,9,2,256]{3,2,1,0:T(2,128)S(1)} %constant_dynamic-slice_fusion.1), channel_id=1, source_target_pairs={{0,4},{2,6},{4,0},{6,2},{8,12},{10,14},{12,8},{14,10},{1,5},{3,7},... | collective-permute-start | bytes 165896 | tf_op jit(solution)/shard_map/ppermute | solution.py:30
  128.7 1.9 %collective-permute-done.19 = f32[3,9,2,256]{3,2,1,0:T(2,128)S(1)} collective-permute-done((f32[3,9,2,256]{3,2,1,0:T(2,128)S(1)}, f32[3,9,2,256]{3,2,1,0:T(2,128)S(1)}, u32[]{:S(2)}, u32[]{:S(2)}) %collective-permute-start.19) | collective-permute-done | bytes 55328 | tf_op jit(solution)/shard_map/ppermute | solution.py:30
  130.7 5.5 %collective-permute-start.20 = (f32[3,9,1,256]{3,2,1,0:T(1,128)S(1)}, f32[3,9,1,256]{3,2,1,0:T(1,128)S(1)}, u32[]{:S(2)}, u32[]{:S(2)}) collective-permute-start(f32[3,9,1,256]{3,2,1,0:T(1,128)S(1)} %constant_dynamic-slice_fusion), channel_id=1, source_target_pairs={{0,8},{2,10},{4,12},{6,14},{8,0},{10,2},{12,4},{14,6},{1,9},{3,11}... | collective-permute-start | bytes 82952 | tf_op jit(solution)/shard_map/ppermute | solution.py:30
  136.7 0.7 collective-permute-done.20
  137.4 12.4 %collective-permute-start.23 = (f32[9,1,256]{2,1,0:T(1,128)S(1)}, f32[9,1,256]{2,1,0:T(1,128)S(1)}, u32[]{:S(2)}, u32[]{:S(2)}) collective-permute-start(f32[9,1,256]{2,1,0:T(1,128)S(1)} %get-tuple-element.26), channel_id=1, source_target_pairs={{0,0},{1,128},{2,32},{3,160},{4,2},{5,130},{6,34},{7,162},{8,1},{9... | collective-permute-start | bytes 27656 | tf_op jit(solution)/shard_map/ppermute | solution.py:86
  149.9 12.5 %collective-permute-start.22 = (f32[9,1,256]{2,0,1:T(8,128)S(1)}, f32[9,1,256]{2,0,1:T(8,128)S(1)}, u32[]{:S(2)}, u32[]{:S(2)}) collective-permute-start(f32[9,1,256]{2,0,1:T(8,128)S(1)} %bitcast.388), channel_id=1, source_target_pairs={{0,0},{1,128},{2,16},{3,144},{4,2},{5,130},{6,18},{7,146},{8,1},{9... | collective-permute-start | bytes 27656 | tf_op jit(solution)/shard_map/ppermute | solution.py:86
  162.4 1.9 %collective-permute-start.21 = (f32[9,1,256]{2,0,1:T(8,128)S(1)}, f32[9,1,256]{2,0,1:T(8,128)S(1)}, u32[]{:S(2)}, u32[]{:S(2)}) collective-permute-start(f32[9,1,256]{2,0,1:T(8,128)S(1)} %bitcast.389), channel_id=1, source_target_pairs={{0,0},{1,128},{2,64},{3,192},{4,2},{5,130},{6,66},{7,194},{8,1},{9... | collective-permute-start | bytes 27656 | tf_op jit(solution)/shard_map/ppermute | solution.py:86
  164.3 1.4 fusion.65
  165.7 6.3 %collective-permute-done.21 = f32[9,1,256]{2,0,1:T(8,128)S(1)} collective-permute-done((f32[9,1,256]{2,0,1:T(8,128)S(1)}, f32[9,1,256]{2,0,1:T(8,128)S(1)}, u32[]{:S(2)}, u32[]{:S(2)}) %collective-permute-start.21) | collective-permute-done | bytes 9248 | tf_op jit(solution)/shard_map/ppermute | solution.py:86
  172.0 0.6 pad_maximum_fusion.10
  (95 shorter events, 12.7 us)
Async XLA Ops:
  0.6 21.1 %collective-permute-start = (bf16[1,2,8,64,256]{4,3,2,1,0:T(8,128)(2,1)}, bf16[1,2,8,64,256]{4,3,2,1,0:T(8,128)(2,1)S(1)}, u32[]{:S(2)}, u32[]{:S(2)}) collective-permute-start(bf16[1,2,8,64,256]{4,3,2,1,0:T(8,128)(2,1)} %param.4), channel_id=1, source_target_pairs={{0,16},{16,32},{32,48},{48,64},{64,80},{80,96},{96,112},{112,128},... | collective-permute-start | bytes 1572872 | tf_op jit(solution)/shard_map/ppermute | solution.py:10
  22.9 6.6 %collective-permute-start.2 = (bf16[1,4,1,64,256]{4,3,2,1,0:T(8,128)(2,1)S(1)}, bf16[1,4,1,64,256]{4,3,2,1,0:T(8,128)(2,1)S(1)}, u32[]{:S(2)}, u32[]{:S(2)}) collective-permute-start(bf16[1,4,1,64,256]{4,3,2,1,0:T(8,128)(2,1)S(1)} %get-tuple-element.24), channel_id=1, source_target_pairs={{1,0},{3,2},{5,4},{7,6},{9,8},{11,10},{13,12},{15,14},{17,16},{19,... | collective-permute-start | bytes 393224 | tf_op jit(solution)/shard_map/ppermute | solution.py:20
  28.2 3.2 %collective-permute-start.1 = (bf16[1,4,1,64,256]{4,3,2,1,0:T(8,128)(2,1)S(1)}, bf16[1,4,1,64,256]{4,3,2,1,0:T(8,128)(2,1)S(1)}, u32[]{:S(2)}, u32[]{:S(2)}) collective-permute-start(bf16[1,4,1,64,256]{4,3,2,1,0:T(8,128)(2,1)S(1)} %get-tuple-element.23), channel_id=1, source_target_pairs={{0,1},{2,3},{4,5},{6,7},{8,9},{10,11},{12,13},{14,15},{16,17},{18,... | collective-permute-start | bytes 393224 | tf_op jit(solution)/shard_map/ppermute | solution.py:17
  32.6 2.0 %copy-start.1 = (bf16[6912,256]{1,0:T(8,128)(2,1)S(1)}, bf16[6912,256]{1,0:T(8,128)(2,1)}, u32[]{:S(2)}) copy-start(bf16[6912,256]{1,0:T(8,128)(2,1)} %param.6) | copy-start | bytes 10616836
  38.8 1.0 copy-start.6
  40.8 16.7 %collective-permute-start.3 = (bf16[1,2,8,64,256]{4,3,2,1,0:T(8,128)(2,1)S(1)}, bf16[1,2,8,64,256]{4,3,2,1,0:T(8,128)(2,1)S(1)}, u32[]{:S(2)}, u32[]{:S(2)}) collective-permute-start(bf16[1,2,8,64,256]{4,3,2,1,0:T(8,128)(2,1)S(1)} %get-tuple-element.39), channel_id=1, source_target_pairs={{16,0},{32,16},{48,32},{64,48},{80,64},{96,80},{112,96},{128,112},... | collective-permute-start | bytes 1572872 | tf_op jit(solution)/shard_map/ppermute | solution.py:10
  52.6 9.3 %collective-permute-start.7 = (bf16[1,2,8,64,256]{4,3,2,1,0:T(8,128)(2,1)S(1)}, bf16[1,2,8,64,256]{4,3,2,1,0:T(8,128)(2,1)S(1)}, u32[]{:S(2)}, u32[]{:S(2)}) collective-permute-start(bf16[1,2,8,64,256]{4,3,2,1,0:T(8,128)(2,1)S(1)} %get-tuple-element.39), channel_id=1, source_target_pairs={{0,1},{1,0},{2,3},{3,2},{4,5},{5,4},{6,7},{7,6},{8,9},{9,8},{10,11... | collective-permute-start | bytes 1572872 | tf_op jit(solution)/shard_map/ppermute | solution.py:151
  53.1 17.7 %collective-permute-start.6 = (bf16[1,4,10,64,256]{4,3,2,1,0:T(8,128)(2,1)S(1)}, bf16[1,4,10,64,256]{4,3,2,1,0:T(8,128)(2,1)S(1)}, u32[]{:S(2)}, u32[]{:S(2)}) collective-permute-start(bf16[1,4,10,64,256]{4,3,2,1,0:T(8,128)(2,1)S(1)} %fusion.62), channel_id=1, source_target_pairs={{0,1},{1,0},{2,3},{3,2},{4,5},{5,4},{6,7},{7,6},{8,9},{9,8},{10,11... | collective-permute-start | bytes 3932168 | tf_op jit(solution)/shard_map/ppermute | solution.py:147
  57.6 6.2 %collective-permute-start.5 = (bf16[1,4,1,64,256]{4,3,2,1,0:T(8,128)(2,1)S(1)}, bf16[1,4,1,64,256]{4,3,2,1,0:T(8,128)(2,1)S(1)}, u32[]{:S(2)}, u32[]{:S(2)}) collective-permute-start(bf16[1,4,1,64,256]{4,3,2,1,0:T(8,128)(2,1)S(1)} %get-tuple-element.22), channel_id=1, source_target_pairs={{1,0},{3,2},{5,4},{7,6},{9,8},{11,10},{13,12},{15,14},{17,16},{19,... | collective-permute-start | bytes 393224 | tf_op jit(solution)/shard_map/ppermute | solution.py:20
  60.4 3.4 %collective-permute-start.4 = (bf16[1,4,1,64,256]{4,3,2,1,0:T(8,128)(2,1)S(1)}, bf16[1,4,1,64,256]{4,3,2,1,0:T(8,128)(2,1)S(1)}, u32[]{:S(2)}, u32[]{:S(2)}) collective-permute-start(bf16[1,4,1,64,256]{4,3,2,1,0:T(8,128)(2,1)S(1)} %get-tuple-element.21), channel_id=1, source_target_pairs={{0,1},{2,3},{4,5},{6,7},{8,9},{10,11},{12,13},{14,15},{16,17},{18,... | collective-permute-start | bytes 393224 | tf_op jit(solution)/shard_map/ppermute | solution.py:17
  65.5 2.0 %copy-start = (bf16[3,3,3,256,256]{3,4,2,1,0:T(8,128)(2,1)S(1)}, bf16[3,3,3,256,256]{3,4,2,1,0:T(8,128)(2,1)}, u32[]{:S(2)}) copy-start(bf16[3,3,3,256,256]{3,4,2,1,0:T(8,128)(2,1)} %copy.34) | copy-start | bytes 10616836
  75.4 1.9 %copy-start.4 = (bf16[2,2,8,64,256]{4,3,2,1,0:T(8,128)(2,1)S(1)}, bf16[2,2,8,64,256]{4,3,2,1,0:T(8,128)(2,1)}, u32[]{:S(2)}) copy-start(bf16[2,2,8,64,256]{4,3,2,1,0:T(8,128)(2,1)} %get-tuple-element.20) | copy-start | bytes 3145732
  78.6 1.5 copy-start.3
  78.7 13.8 %collective-permute-start.14 = (f32[9,64,256]{2,1,0:T(8,128)S(1)}, f32[9,64,256]{2,1,0:T(8,128)S(1)}, u32[]{:S(2)}, u32[]{:S(2)}) collective-permute-start(f32[9,64,256]{2,1,0:T(8,128)S(1)} %constant_dynamic-slice_fusion.6), channel_id=1, source_target_pairs={{0,64},{16,80},{32,96},{48,112},{64,0},{80,16},{96,32},{112,48},{1... | collective-permute-start | bytes 1769480 | tf_op jit(solution)/shard_map/ppermute | solution.py:30
  82.0 1.4 copy-start.2
  82.1 13.8 %collective-permute-start.11 = (f32[9,64,256]{2,1,0:T(8,128)S(1)}, f32[9,64,256]{2,1,0:T(8,128)S(1)}, u32[]{:S(2)}, u32[]{:S(2)}) collective-permute-start(f32[9,64,256]{2,1,0:T(8,128)S(1)} %constant_dynamic-slice_fusion.9), channel_id=1, source_target_pairs={{0,16},{16,0},{32,48},{48,32},{64,80},{80,64},{96,112},{112,96},{1... | collective-permute-start | bytes 1769480 | tf_op jit(solution)/shard_map/ppermute | solution.py:30
  85.4 13.9 %collective-permute-start.8 = (f32[9,64,256]{2,1,0:T(8,128)S(1)}, f32[9,64,256]{2,1,0:T(8,128)S(1)}, u32[]{:S(2)}, u32[]{:S(2)}) collective-permute-start(f32[9,64,256]{2,1,0:T(8,128)S(1)} %constant_dynamic-slice_fusion.12), channel_id=1, source_target_pairs={{0,2},{2,0},{4,6},{6,4},{8,10},{10,8},{12,14},{14,12},{1,3},{3,1},... | collective-permute-start | bytes 1769480 | tf_op jit(solution)/shard_map/ppermute | solution.py:30
  92.7 12.9 %collective-permute-start.15 = (f32[9,32,256]{2,1,0:T(8,128)S(1)}, f32[9,32,256]{2,1,0:T(8,128)S(1)}, u32[]{:S(2)}, u32[]{:S(2)}) collective-permute-start(f32[9,32,256]{2,1,0:T(8,128)S(1)} %constant_dynamic-slice_fusion.5), channel_id=1, source_target_pairs={{0,2},{2,0},{4,6},{6,4},{8,10},{10,8},{12,14},{14,12},{1,3},{3,1},... | collective-permute-start | bytes 884744 | tf_op jit(solution)/shard_map/ppermute | solution.py:30
  96.0 10.4 %collective-permute-start.12 = (f32[9,32,256]{2,1,0:T(8,128)S(1)}, f32[9,32,256]{2,1,0:T(8,128)S(1)}, u32[]{:S(2)}, u32[]{:S(2)}) collective-permute-start(f32[9,32,256]{2,1,0:T(8,128)S(1)} %constant_dynamic-slice_fusion.8), channel_id=1, source_target_pairs={{0,64},{16,80},{32,96},{48,112},{64,0},{80,16},{96,32},{112,48},{1... | collective-permute-start | bytes 884744 | tf_op jit(solution)/shard_map/ppermute | solution.py:30
  99.4 8.5 %collective-permute-start.9 = (f32[9,32,256]{2,1,0:T(8,128)S(1)}, f32[9,32,256]{2,1,0:T(8,128)S(1)}, u32[]{:S(2)}, u32[]{:S(2)}) collective-permute-start(f32[9,32,256]{2,1,0:T(8,128)S(1)} %constant_dynamic-slice_fusion.11), channel_id=1, source_target_pairs={{0,16},{16,0},{32,48},{48,32},{64,80},{80,64},{96,112},{112,96},{1... | collective-permute-start | bytes 884744 | tf_op jit(solution)/shard_map/ppermute | solution.py:30
  105.7 5.7 %collective-permute-start.16 = (f32[9,16,256]{2,1,0:T(8,128)S(1)}, f32[9,16,256]{2,1,0:T(8,128)S(1)}, u32[]{:S(2)}, u32[]{:S(2)}) collective-permute-start(f32[9,16,256]{2,1,0:T(8,128)S(1)} %constant_dynamic-slice_fusion.4), channel_id=1, source_target_pairs={{0,16},{16,0},{32,48},{48,32},{64,80},{80,64},{96,112},{112,96},{1... | collective-permute-start | bytes 442376 | tf_op jit(solution)/shard_map/ppermute | solution.py:30
  106.5 4.9 %collective-permute-start.13 = (f32[9,16,256]{2,1,0:T(8,128)S(1)}, f32[9,16,256]{2,1,0:T(8,128)S(1)}, u32[]{:S(2)}, u32[]{:S(2)}) collective-permute-start(f32[9,16,256]{2,1,0:T(8,128)S(1)} %constant_dynamic-slice_fusion.7), channel_id=1, source_target_pairs={{0,2},{2,0},{4,6},{6,4},{8,10},{10,8},{12,14},{14,12},{1,3},{3,1},... | collective-permute-start | bytes 442376 | tf_op jit(solution)/shard_map/ppermute | solution.py:30
  108.0 4.4 %collective-permute-start.10 = (f32[9,16,256]{2,1,0:T(8,128)S(1)}, f32[9,16,256]{2,1,0:T(8,128)S(1)}, u32[]{:S(2)}, u32[]{:S(2)}) collective-permute-start(f32[9,16,256]{2,1,0:T(8,128)S(1)} %constant_dynamic-slice_fusion.10), channel_id=1, source_target_pairs={{0,64},{16,80},{32,96},{48,112},{64,0},{80,16},{96,32},{112,48},{1... | collective-permute-start | bytes 442376 | tf_op jit(solution)/shard_map/ppermute | solution.py:30
  112.4 10.4 %copy-start.5 = (f32[2,8,64,256]{3,2,1,0:T(8,128)S(1)}, f32[2,8,64,256]{3,2,1,0:T(8,128)}, u32[]{:S(2)}) copy-start(f32[2,8,64,256]{3,2,1,0:T(8,128)} %fusion.4) | copy-start | bytes 3145732
  112.4 7.0 %collective-permute-start.17 = (f32[3,9,8,256]{3,2,1,0:T(8,128)S(1)}, f32[3,9,8,256]{3,2,1,0:T(8,128)S(1)}, u32[]{:S(2)}, u32[]{:S(2)}) collective-permute-start(f32[3,9,8,256]{3,2,1,0:T(8,128)S(1)} %constant_dynamic-slice_fusion.3), channel_id=1, source_target_pairs={{0,32},{16,48},{32,0},{48,16},{64,96},{80,112},{96,64},{112,80},{1... | collective-permute-start | bytes 663560 | tf_op jit(solution)/shard_map/ppermute | solution.py:30
  119.5 5.4 %collective-permute-start.18 = (f32[3,9,4,256]{3,2,1,0:T(4,128)S(1)}, f32[3,9,4,256]{3,2,1,0:T(4,128)S(1)}, u32[]{:S(2)}, u32[]{:S(2)}) collective-permute-start(f32[3,9,4,256]{3,2,1,0:T(4,128)S(1)} %constant_dynamic-slice_fusion.2), channel_id=1, source_target_pairs={{0,128},{16,144},{32,160},{48,176},{64,192},{80,208},{96,224},{112... | collective-permute-start | bytes 331784 | tf_op jit(solution)/shard_map/ppermute | solution.py:30
  125.1 5.5 %collective-permute-start.19 = (f32[3,9,2,256]{3,2,1,0:T(2,128)S(1)}, f32[3,9,2,256]{3,2,1,0:T(2,128)S(1)}, u32[]{:S(2)}, u32[]{:S(2)}) collective-permute-start(f32[3,9,2,256]{3,2,1,0:T(2,128)S(1)} %constant_dynamic-slice_fusion.1), channel_id=1, source_target_pairs={{0,4},{2,6},{4,0},{6,2},{8,12},{10,14},{12,8},{14,10},{1,5},{3,7},... | collective-permute-start | bytes 165896 | tf_op jit(solution)/shard_map/ppermute | solution.py:30
  130.7 6.7 %collective-permute-start.20 = (f32[3,9,1,256]{3,2,1,0:T(1,128)S(1)}, f32[3,9,1,256]{3,2,1,0:T(1,128)S(1)}, u32[]{:S(2)}, u32[]{:S(2)}) collective-permute-start(f32[3,9,1,256]{3,2,1,0:T(1,128)S(1)} %constant_dynamic-slice_fusion), channel_id=1, source_target_pairs={{0,8},{2,10},{4,12},{6,14},{8,0},{10,2},{12,4},{14,6},{1,9},{3,11}... | collective-permute-start | bytes 82952 | tf_op jit(solution)/shard_map/ppermute | solution.py:30
  137.4 28.3 %collective-permute-start.23 = (f32[9,1,256]{2,1,0:T(1,128)S(1)}, f32[9,1,256]{2,1,0:T(1,128)S(1)}, u32[]{:S(2)}, u32[]{:S(2)}) collective-permute-start(f32[9,1,256]{2,1,0:T(1,128)S(1)} %get-tuple-element.26), channel_id=1, source_target_pairs={{0,0},{1,128},{2,32},{3,160},{4,2},{5,130},{6,34},{7,162},{8,1},{9... | collective-permute-start | bytes 27656 | tf_op jit(solution)/shard_map/ppermute | solution.py:86
  149.9 15.8 %collective-permute-start.22 = (f32[9,1,256]{2,0,1:T(8,128)S(1)}, f32[9,1,256]{2,0,1:T(8,128)S(1)}, u32[]{:S(2)}, u32[]{:S(2)}) collective-permute-start(f32[9,1,256]{2,0,1:T(8,128)S(1)} %bitcast.388), channel_id=1, source_target_pairs={{0,0},{1,128},{2,16},{3,144},{4,2},{5,130},{6,18},{7,146},{8,1},{9... | collective-permute-start | bytes 27656 | tf_op jit(solution)/shard_map/ppermute | solution.py:86
  162.4 9.6 %collective-permute-start.21 = (f32[9,1,256]{2,0,1:T(8,128)S(1)}, f32[9,1,256]{2,0,1:T(8,128)S(1)}, u32[]{:S(2)}, u32[]{:S(2)}) collective-permute-start(f32[9,1,256]{2,0,1:T(8,128)S(1)} %bitcast.389), channel_id=1, source_target_pairs={{0,0},{1,128},{2,64},{3,192},{4,2},{5,130},{6,66},{7,194},{8,1},{9... | collective-permute-start | bytes 27656 | tf_op jit(solution)/shard_map/ppermute | solution.py:86

commit v2 on v1

--- a/solution.py
+++ b/solution.py
@@ -36,7 +36,7 @@
     return count
 
 
-def owner_pairs(order, sizes):
+def owner_pairs(order, sizes, flipped=None):
     names = ("group", "dp", "space")
     count = sizes["group"] * sizes["dp"] * sizes["space"]
     pairs = []
@@ -46,6 +46,8 @@
             "dp": (linear // sizes["space"]) % sizes["dp"],
             "space": linear % sizes["space"],
         }
+        if flipped is not None:
+            where[flipped[0]] ^= flipped[1]
         chunk = 0
         for axis, flip in order:
             chunk = chunk * 2 + (where[axis] // flip) % 2
@@ -78,12 +80,19 @@
         parts.append(part)
         orders.append(order + rest)
     joined = jnp.stack(parts)
-    for axis, flip in rest:
+    for axis, flip in rest[:-1]:
         joined = halve(joined, 2, axis, flip)
+    last = rest[-1]
+    bit = (lax.axis_index(last[0]) // last[1]) % 2
+    size = joined.shape[2] // 2
+    keep = lax.dynamic_slice_in_dim(joined, bit * size, size, axis=2)
+    give = lax.dynamic_slice_in_dim(joined, (1 - bit) * size, size, axis=2)
     parts = []
     for n, order in enumerate(orders):
         names, pairs = owner_pairs(order, sizes)
-        parts.append(lax.ppermute(joined[n], names, pairs).reshape(per, outs))
+        _, cross = owner_pairs(order, sizes, last)
+        got = lax.ppermute(keep[n], names, pairs) + lax.ppermute(give[n], names, cross)
+        parts.append(got.reshape(per, outs))
     return jnp.concatenate(parts, axis=0)
 
 

time: 174 us -> 180 us (1.034)
  the two profiles are of different devices: /device:TPU:25 before, /device:TPU:100 now
where the time goes in v2:
time: 180 us
  waiting for transfers between devices  56.2 us (31%)
  starting transfers between devices  55.3 us (31%)
  matrix products  20.4 us (11%)
  local copies, waits for them, and re-layouts  19.7 us (11%)
  blocking collectives  17.8 us (10%)
  other arithmetic  8.01 us (4%)
  between operations  2.31 us (1%)
    ppermute x12, waiting for transfers between devices, halve(): return keep + lax.ppermute(give, axis, pairs)  40.9 us
    ppermute x3, starting transfers between devices, reduce_weight_grad(): lax.ppermute(keep[n], names, pairs) + lax.ppermute(give[n], names, cross)  24.1 us
    unnamed x1, blocking collectives  17.8 us
    ppermute x12, starting transfers between devices, halve(): return keep + lax.ppermute(give, axis, pairs)  10.1 us
    ppermute x2, starting transfers between devices, passed_along(): return lax.ppermute(value, axis, pairs)  9.25 us
    ppermute x3, waiting for transfers between devices, reduce_weight_grad(): lax.ppermute(give[n], names, cross)  8.74 us
    dot_general x9, matrix products, local(): jnp.einsum('sfhwk,kc->sfhwc', block, back[k, a], preferred_element_type=j...  7.94 us
    dot_general x9, matrix products, local(): jnp.einsum('sfhwk,sfhwc->kc', block, masked, preferred_element_type=jnp.f...  6.78 us
  transfers between devices with their start and end apart: 26, of which 15 were waited for; matrix products, arithmetic and copies ran while one was open for 15% of the time, Pallas kernels for 0%

profile of v2, /device:TPU:100, one launch (start us, length us, event | category | flops | bytes accessed | tf_op | source)
XLA Modules:
  0.0 179.6 jit_solution(10485599610097153759)
XLA Ops:
  0.6 3.1 %collective-permute-start = (bf16[1,2,8,64,256]{4,3,2,1,0:T(8,128)(2,1)}, bf16[1,2,8,64,256]{4,3,2,1,0:T(8,128)(2,1)S(1)}, u32[]{:S(2)}, u32[]{:S(2)}) collective-permute-start(bf16[1,2,8,64,256]{4,3,2,1,0:T(8,128)(2,1)} %param.4), channel_id=1, source_target_pairs={{0,16},{16,32},{32,48},{48,64},{64,80},{80,96},{96,112},{112,128},... | collective-permute-start | bytes 1572872 | tf_op jit(solution)/shard_map/ppermute | solution.py:10
  3.8 1.3 dynamic-slice
  5.7 0.8 bitcast_dynamic-update-slice_fusion
  6.4 17.8 %all-reduce.6 = s32[32]{0:T(128)S(1)} all-reduce(s32[32]{0:T(128)S(1)} %bitcast_dynamic-update-slice_fusion), channel_id=1, replica_groups=mesh['group'=16,'dp'=8,'space'=2] {'group'}, use_global_device_ids=true, to_apply=%add.6 | all-reduce | flops 32 | bytes 256
  25.0 1.1 constant_dynamic-update-slice_fusion
  26.1 1.3 collective-permute-start.2
  27.4 3.0 %collective-permute-start.1 = (bf16[1,4,1,64,256]{4,3,2,1,0:T(8,128)(2,1)S(1)}, bf16[1,4,1,64,256]{4,3,2,1,0:T(8,128)(2,1)S(1)}, u32[]{:S(2)}, u32[]{:S(2)}) collective-permute-start(bf16[1,4,1,64,256]{4,3,2,1,0:T(8,128)(2,1)S(1)} %get-tuple-element.23), channel_id=1, source_target_pairs={{0,1},{2,3},{4,5},{6,7},{8,9},{10,11},{12,13},{14,15},{16,17},{18,... | collective-permute-start | bytes 393224 | tf_op jit(solution)/shard_map/ppermute | solution.py:17
  30.5 0.9 collective-permute-done.1
  31.8 0.9 pad_slice_fusion.3
  33.0 1.6 copy-done.1
  35.3 0.6 fusion.11
  38.2 0.6 fusion.50
  38.8 0.6 fusion.47
  39.9 1.0 fusion.93
  40.9 6.1 %collective-permute-start.3 = (bf16[1,2,8,64,256]{4,3,2,1,0:T(8,128)(2,1)S(1)}, bf16[1,2,8,64,256]{4,3,2,1,0:T(8,128)(2,1)S(1)}, u32[]{:S(2)}, u32[]{:S(2)}) collective-permute-start(bf16[1,2,8,64,256]{4,3,2,1,0:T(8,128)(2,1)S(1)} %get-tuple-element.42), channel_id=1, source_target_pairs={{16,0},{32,16},{48,32},{64,48},{80,64},{96,80},{112,96},{128,112},... | collective-permute-start | bytes 1572872 | tf_op jit(solution)/shard_map/ppermute | solution.py:10
  47.2 6.1 %copy.34 = bf16[3,3,3,256,256]{3,4,2,1,0:T(8,128)(2,1)} copy(bf16[3,3,3,256,256]{4,3,2,1,0:T(8,128)(2,1)} %bitcast.380) | data formatting | bytes 7077888 | tf_op jit(solution)/shard_map/reshape | solution.py:174
  53.9 1.1 fusion.103
  55.0 4.4 %collective-permute-done.3 = bf16[1,2,8,64,256]{4,3,2,1,0:T(8,128)(2,1)S(1)} collective-permute-done((bf16[1,2,8,64,256]{4,3,2,1,0:T(8,128)(2,1)S(1)}, bf16[1,2,8,64,256]{4,3,2,1,0:T(8,128)(2,1)S(1)}, u32[]{:S(2)}, u32[]{:S(2)}) %collective-permute-start.3) | collective-permute-done | bytes 524320 | tf_op jit(solution)/shard_map/ppermute | solution.py:10
  59.4 1.3 collective-permute-start.5
  60.7 3.2 %collective-permute-start.4 = (bf16[1,4,1,64,256]{4,3,2,1,0:T(8,128)(2,1)S(1)}, bf16[1,4,1,64,256]{4,3,2,1,0:T(8,128)(2,1)S(1)}, u32[]{:S(2)}, u32[]{:S(2)}) collective-permute-start(bf16[1,4,1,64,256]{4,3,2,1,0:T(8,128)(2,1)S(1)} %get-tuple-element.21), channel_id=1, source_target_pairs={{0,1},{2,3},{4,5},{6,7},{8,9},{10,11},{12,13},{14,15},{16,17},{18,... | collective-permute-start | bytes 393224 | tf_op jit(solution)/shard_map/ppermute | solution.py:17
  64.0 1.9 %broadcast_multiply_fusion.2 = (bf16[2,2,8,64,256]{4,3,2,1,0:T(8,128)(2,1)}, bf16[2,2,8,64,256]{4,3,2,1,0:T(8,128)(2,1)}, bf16[2,2,8,64,256]{4,3,2,1,0:T(8,128)(2,1)}) fusion(bf16[2]{0:T(256)(128)(2,1)S(1)} %get-tuple-element.34, bf16[1,2,8,64,256]{4,3,2,1,0:T(8,128)(2,1)S(1)} %collective-permute-done.7, ...), kind=kLoop, calls=%fused_computation.130 | loop fusion | flops 2097152 | bytes 4194316 | tf_op jit(solution)/shard_map/mul | solution.py:163
  65.8 0.8 select_maximum_fusion
  66.7 0.9 fusion.116
  68.0 1.6 copy-done
  70.7 1.6 fusion.4
  72.3 1.5 fusion.5
  74.7 1.3 pad_slice_fusion.1
  76.0 0.6 pad_maximum_fusion.2
  76.7 2.3 %fusion.115 = (bf16[2,2,8,64,384]{4,3,2,1,0:T(8,128)(2,1)S(1)}, bf16[2,2,8,64,384]{4,3,2,1,0:T(8,128)(2,1)S(1)}, bf16[2,2,8,64,384]{4,3,2,1,0:T(8,128)(2,1)S(1)}...) fusion(bf16[2,4,10,64,384]{4,3,2,1,0:T(8,128)(2,1)S(1)} %pad_ma, ...), kind=kLoop, calls=%fused_computation.224 | loop fusion | bytes 28311552 | tf_op jit(solution)/shard_map/slice | solution.py:165
  79.0 1.9 %fusion.90 = f32[1,384,256]{2,1,0:T(8,128)S(1)} fusion(bf16[2,2,8,64,384]{4,3,2,1,0:T(8,128)(2,1)S(1)} %get-tuple-element.4, bf16[2,2,8,64,256]{4,3,2,1,0:T(8,128)(2,1)} %get-tuple-element.20), kind=kOutput, calls=%fused_computation.106 | convolution fusion | flops 402653184 | bytes 3014656 | tf_op jit(solution)/shard_map/sfhwk,sfhwc->kc/dot_general | solution.py:167
  81.0 0.6 fusion.87
  81.6 0.6 fusion.84
  82.6 0.8 copy-done.3
  83.4 0.6 fusion.81
  84.0 0.6 fusion.78
  84.6 0.6 fusion.75
  85.4 4.2 %collective-permute-start.11 = (f32[9,64,256]{2,1,0:T(8,128)S(1)}, f32[9,64,256]{2,1,0:T(8,128)S(1)}, u32[]{:S(2)}, u32[]{:S(2)}) collective-permute-start(f32[9,64,256]{2,1,0:T(8,128)S(1)} %constant_dynamic-slice_fusion.12), channel_id=1, source_target_pairs={{0,16},{16,0},{32,48},{48,32},{64,80},{80,64},{96,112},{112,96},{1... | collective-permute-start | bytes 1769480 | tf_op jit(solution)/shard_map/ppermute | solution.py:30
  89.6 0.6 fusion.72
  90.2 0.6 fusion.69
  90.8 0.6 fusion.66
  91.7 5.3 %collective-permute-done.14 = f32[9,64,256]{2,1,0:T(8,128)S(1)} collective-permute-done((f32[9,64,256]{2,1,0:T(8,128)S(1)}, f32[9,64,256]{2,1,0:T(8,128)S(1)}, u32[]{:S(2)}, u32[]{:S(2)}) %collective-permute-start.14) | collective-permute-done | bytes 589856 | tf_op jit(solution)/shard_map/ppermute | solution.py:30
  97.3 5.1 %collective-permute-done.11 = f32[9,64,256]{2,1,0:T(8,128)S(1)} collective-permute-done((f32[9,64,256]{2,1,0:T(8,128)S(1)}, f32[9,64,256]{2,1,0:T(8,128)S(1)}, u32[]{:S(2)}, u32[]{:S(2)}) %collective-permute-start.11) | collective-permute-done | bytes 589856 | tf_op jit(solution)/shard_map/ppermute | solution.py:30
  102.5 0.8 collective-permute-start.12
  103.4 4.4 %collective-permute-done.8 = f32[9,64,256]{2,1,0:T(8,128)S(1)} collective-permute-done((f32[9,64,256]{2,1,0:T(8,128)S(1)}, f32[9,64,256]{2,1,0:T(8,128)S(1)}, u32[]{:S(2)}, u32[]{:S(2)}) %collective-permute-start.8) | collective-permute-done | bytes 589856 | tf_op jit(solution)/shard_map/ppermute | solution.py:30
  107.9 0.8 collective-permute-start.9
  108.8 3.5 %collective-permute-done.15 = f32[9,32,256]{2,1,0:T(8,128)S(1)} collective-permute-done((f32[9,32,256]{2,1,0:T(8,128)S(1)}, f32[9,32,256]{2,1,0:T(8,128)S(1)}, u32[]{:S(2)}, u32[]{:S(2)}) %collective-permute-start.15) | collective-permute-done | bytes 294944 | tf_op jit(solution)/shard_map/ppermute | solution.py:30
  112.3 1.1 collective-permute-start.16
  113.9 2.3 %collective-permute-done.9 = f32[9,32,256]{2,1,0:T(8,128)S(1)} collective-permute-done((f32[9,32,256]{2,1,0:T(8,128)S(1)}, f32[9,32,256]{2,1,0:T(8,128)S(1)}, u32[]{:S(2)}, u32[]{:S(2)}) %collective-permute-start.9) | collective-permute-done | bytes 294944 | tf_op jit(solution)/shard_map/ppermute | solution.py:30
  116.3 1.2 collective-permute-start.10
  117.9 0.8 collective-permute-done.13
  118.8 2.8 %collective-permute-done.10 = f32[9,16,256]{2,1,0:T(8,128)S(1)} collective-permute-done((f32[9,16,256]{2,1,0:T(8,128)S(1)}, f32[9,16,256]{2,1,0:T(8,128)S(1)}, u32[]{:S(2)}, u32[]{:S(2)}) %collective-permute-start.10) | collective-permute-done | bytes 147488 | tf_op jit(solution)/shard_map/ppermute | solution.py:30
  121.8 0.6 fusion.58
  122.4 6.8 %collective-permute-done.17 = f32[3,9,8,256]{3,2,1,0:T(8,128)S(1)} collective-permute-done((f32[3,9,8,256]{3,2,1,0:T(8,128)S(1)}, f32[3,9,8,256]{3,2,1,0:T(8,128)S(1)}, u32[]{:S(2)}, u32[]{:S(2)}) %collective-permute-start.17) | collective-permute-done | bytes 221216 | tf_op jit(solution)/shard_map/ppermute | solution.py:30
  129.3 0.7 collective-permute-start.18
  130.6 5.0 %collective-permute-done.18 = f32[3,9,4,256]{3,2,1,0:T(4,128)S(1)} collective-permute-done((f32[3,9,4,256]{3,2,1,0:T(4,128)S(1)}, f32[3,9,4,256]{3,2,1,0:T(4,128)S(1)}, u32[]{:S(2)}, u32[]{:S(2)}) %collective-permute-start.18) | collective-permute-done | bytes 110624 | tf_op jit(solution)/shard_map/ppermute | solution.py:30
  136.3 4.5 %collective-permute-done.19 = f32[3,9,2,256]{3,2,1,0:T(2,128)S(1)} collective-permute-done((f32[3,9,2,256]{3,2,1,0:T(2,128)S(1)}, f32[3,9,2,256]{3,2,1,0:T(2,128)S(1)}, u32[]{:S(2)}, u32[]{:S(2)}) %collective-permute-start.19) | collective-permute-done | bytes 55328 | tf_op jit(solution)/shard_map/ppermute | solution.py:30
  140.9 3.2 %collective-permute-start.22 = (f32[9,1,256]{2,0,1:T(8,128)S(1)}, f32[9,1,256]{2,0,1:T(8,128)S(1)}, u32[]{:S(2)}, u32[]{:S(2)}) collective-permute-start(f32[9,1,256]{2,0,1:T(8,128)S(1)} %bitcast.398), channel_id=1, source_target_pairs={{0,0},{1,128},{2,16},{3,144},{4,2},{5,130},{6,18},{7,146},{8,1},{9... | collective-permute-start | bytes 27656 | tf_op jit(solution)/shard_map/ppermute | solution.py:94
  144.2 1.4 fusion.65
  145.6 2.2 %collective-permute-start.25 = (f32[9,1,256]{2,1,0:T(1,128)S(1)}, f32[9,1,256]{2,1,0:T(1,128)S(1)}, u32[]{:S(2)}, u32[]{:S(2)}) collective-permute-start(f32[9,1,256]{2,1,0:T(1,128)S(1)} %get-tuple-element.29), channel_id=1, source_target_pairs={{0,1},{1,129},{2,33},{3,161},{4,3},{5,131},{6,35},{7,163},{8,0},{9... | collective-permute-start | bytes 27656 | tf_op jit(solution)/shard_map/ppermute | solution.py:94
  147.8 3.6 %collective-permute-start.24 = (f32[9,1,256]{2,0,1:T(8,128)S(1)}, f32[9,1,256]{2,0,1:T(8,128)S(1)}, u32[]{:S(2)}, u32[]{:S(2)}) collective-permute-start(f32[9,1,256]{2,0,1:T(8,128)S(1)} %bitcast.400), channel_id=1, source_target_pairs={{0,0},{1,128},{2,32},{3,160},{4,2},{5,130},{6,34},{7,162},{8,1},{9... | collective-permute-start | bytes 27656 | tf_op jit(solution)/shard_map/ppermute | solution.py:94
  151.5 17.3 %collective-permute-start.20 = (f32[9,1,256]{2,0,1:T(8,128)S(1)}, f32[9,1,256]{2,0,1:T(8,128)S(1)}, u32[]{:S(2)}, u32[]{:S(2)}) collective-permute-start(f32[9,1,256]{2,0,1:T(8,128)S(1)} %bitcast.399), channel_id=1, source_target_pairs={{0,0},{1,128},{2,64},{3,192},{4,2},{5,130},{6,66},{7,194},{8,1},{9... | collective-permute-start | bytes 27656 | tf_op jit(solution)/shard_map/ppermute | solution.py:94
  169.0 1.2 collective-permute-done.20
  170.2 8.7 %collective-permute-done.21 = f32[9,1,256]{2,0,1:T(8,128)S(1)} collective-permute-done((f32[9,1,256]{2,0,1:T(8,128)S(1)}, f32[9,1,256]{2,0,1:T(8,128)S(1)}, u32[]{:S(2)}, u32[]{:S(2)}) %collective-permute-start.21) | collective-permute-done | bytes 9248 | tf_op jit(solution)/shard_map/ppermute | solution.py:94
  179.0 0.6 pad_maximum_fusion.10
  (105 shorter events, 12.1 us)
Async XLA Ops:
  0.6 24.3 %collective-permute-start = (bf16[1,2,8,64,256]{4,3,2,1,0:T(8,128)(2,1)}, bf16[1,2,8,64,256]{4,3,2,1,0:T(8,128)(2,1)S(1)}, u32[]{:S(2)}, u32[]{:S(2)}) collective-permute-start(bf16[1,2,8,64,256]{4,3,2,1,0:T(8,128)(2,1)} %param.4), channel_id=1, source_target_pairs={{0,16},{16,32},{32,48},{48,64},{64,80},{80,96},{96,112},{112,128},... | collective-permute-start | bytes 1572872 | tf_op jit(solution)/shard_map/ppermute | solution.py:10
  26.1 4.4 %collective-permute-start.2 = (bf16[1,4,1,64,256]{4,3,2,1,0:T(8,128)(2,1)S(1)}, bf16[1,4,1,64,256]{4,3,2,1,0:T(8,128)(2,1)S(1)}, u32[]{:S(2)}, u32[]{:S(2)}) collective-permute-start(bf16[1,4,1,64,256]{4,3,2,1,0:T(8,128)(2,1)S(1)} %get-tuple-element.24), channel_id=1, source_target_pairs={{1,0},{3,2},{5,4},{7,6},{9,8},{11,10},{13,12},{15,14},{17,16},{19,... | collective-permute-start | bytes 393224 | tf_op jit(solution)/shard_map/ppermute | solution.py:20
  27.4 4.0 %collective-permute-start.1 = (bf16[1,4,1,64,256]{4,3,2,1,0:T(8,128)(2,1)S(1)}, bf16[1,4,1,64,256]{4,3,2,1,0:T(8,128)(2,1)S(1)}, u32[]{:S(2)}, u32[]{:S(2)}) collective-permute-start(bf16[1,4,1,64,256]{4,3,2,1,0:T(8,128)(2,1)S(1)} %get-tuple-element.23), channel_id=1, source_target_pairs={{0,1},{2,3},{4,5},{6,7},{8,9},{10,11},{12,13},{14,15},{16,17},{18,... | collective-permute-start | bytes 393224 | tf_op jit(solution)/shard_map/ppermute | solution.py:17
  32.7 2.0 %copy-start.1 = (bf16[6912,256]{1,0:T(8,128)(2,1)S(1)}, bf16[6912,256]{1,0:T(8,128)(2,1)}, u32[]{:S(2)}) copy-start(bf16[6912,256]{1,0:T(8,128)(2,1)} %param.6) | copy-start | bytes 10616836
  38.8 1.0 copy-start.7
  40.9 18.5 %collective-permute-start.3 = (bf16[1,2,8,64,256]{4,3,2,1,0:T(8,128)(2,1)S(1)}, bf16[1,2,8,64,256]{4,3,2,1,0:T(8,128)(2,1)S(1)}, u32[]{:S(2)}, u32[]{:S(2)}) collective-permute-start(bf16[1,2,8,64,256]{4,3,2,1,0:T(8,128)(2,1)S(1)} %get-tuple-element.42), channel_id=1, source_target_pairs={{16,0},{32,16},{48,32},{64,48},{80,64},{96,80},{112,96},{128,112},... | collective-permute-start | bytes 1572872 | tf_op jit(solution)/shard_map/ppermute | solution.py:10
  53.3 10.6 %collective-permute-start.7 = (bf16[1,2,8,64,256]{4,3,2,1,0:T(8,128)(2,1)S(1)}, bf16[1,2,8,64,256]{4,3,2,1,0:T(8,128)(2,1)S(1)}, u32[]{:S(2)}, u32[]{:S(2)}) collective-permute-start(bf16[1,2,8,64,256]{4,3,2,1,0:T(8,128)(2,1)S(1)} %get-tuple-element.42), channel_id=1, source_target_pairs={{0,1},{1,0},{2,3},{3,2},{4,5},{5,4},{6,7},{7,6},{8,9},{9,8},{10,11... | collective-permute-start | bytes 1572872 | tf_op jit(solution)/shard_map/ppermute | solution.py:160
  53.5 21.0 %collective-permute-start.6 = (bf16[1,4,10,64,256]{4,3,2,1,0:T(8,128)(2,1)S(1)}, bf16[1,4,10,64,256]{4,3,2,1,0:T(8,128)(2,1)S(1)}, u32[]{:S(2)}, u32[]{:S(2)}) collective-permute-start(bf16[1,4,10,64,256]{4,3,2,1,0:T(8,128)(2,1)S(1)} %fusion.62), channel_id=1, source_target_pairs={{0,1},{1,0},{2,3},{3,2},{4,5},{5,4},{6,7},{7,6},{8,9},{9,8},{10,11... | collective-permute-start | bytes 3932168 | tf_op jit(solution)/shard_map/ppermute | solution.py:156
  59.4 6.4 %collective-permute-start.5 = (bf16[1,4,1,64,256]{4,3,2,1,0:T(8,128)(2,1)S(1)}, bf16[1,4,1,64,256]{4,3,2,1,0:T(8,128)(2,1)S(1)}, u32[]{:S(2)}, u32[]{:S(2)}) collective-permute-start(bf16[1,4,1,64,256]{4,3,2,1,0:T(8,128)(2,1)S(1)} %get-tuple-element.22), channel_id=1, source_target_pairs={{1,0},{3,2},{5,4},{7,6},{9,8},{11,10},{13,12},{15,14},{17,16},{19,... | collective-permute-start | bytes 393224 | tf_op jit(solution)/shard_map/ppermute | solution.py:20
  60.7 5.1 %collective-permute-start.4 = (bf16[1,4,1,64,256]{4,3,2,1,0:T(8,128)(2,1)S(1)}, bf16[1,4,1,64,256]{4,3,2,1,0:T(8,128)(2,1)S(1)}, u32[]{:S(2)}, u32[]{:S(2)}) collective-permute-start(bf16[1,4,1,64,256]{4,3,2,1,0:T(8,128)(2,1)S(1)} %get-tuple-element.21), channel_id=1, source_target_pairs={{0,1},{2,3},{4,5},{6,7},{8,9},{10,11},{12,13},{14,15},{16,17},{18,... | collective-permute-start | bytes 393224 | tf_op jit(solution)/shard_map/ppermute | solution.py:17
  67.6 2.0 %copy-start = (bf16[3,3,3,256,256]{3,4,2,1,0:T(8,128)(2,1)S(1)}, bf16[3,3,3,256,256]{3,4,2,1,0:T(8,128)(2,1)}, u32[]{:S(2)}) copy-start(bf16[3,3,3,256,256]{3,4,2,1,0:T(8,128)(2,1)} %copy.34) | copy-start | bytes 10616836
  79.0 1.9 %copy-start.4 = (bf16[2,2,8,64,256]{4,3,2,1,0:T(8,128)(2,1)S(1)}, bf16[2,2,8,64,256]{4,3,2,1,0:T(8,128)(2,1)}, u32[]{:S(2)}) copy-start(bf16[2,2,8,64,256]{4,3,2,1,0:T(8,128)(2,1)} %get-tuple-element.20) | copy-start | bytes 3145732
  82.2 1.2 copy-start.3
  82.3 14.7 %collective-permute-start.14 = (f32[9,64,256]{2,1,0:T(8,128)S(1)}, f32[9,64,256]{2,1,0:T(8,128)S(1)}, u32[]{:S(2)}, u32[]{:S(2)}) collective-permute-start(f32[9,64,256]{2,1,0:T(8,128)S(1)} %constant_dynamic-slice_fusion.9), channel_id=1, source_target_pairs={{0,64},{16,80},{32,96},{48,112},{64,0},{80,16},{96,32},{112,48},{1... | collective-permute-start | bytes 1769480 | tf_op jit(solution)/shard_map/ppermute | solution.py:30
  85.2 4.3 %copy-start.2 = (bf16[2,2,8,64,256]{4,3,2,1,0:T(8,128)(2,1)S(1)}, bf16[2,2,8,64,256]{4,3,2,1,0:T(8,128)(2,1)}, u32[]{:S(2)}) copy-start(bf16[2,2,8,64,256]{4,3,2,1,0:T(8,128)(2,1)} %get-tuple-element.18) | copy-start | bytes 3145732
  85.4 17.0 %collective-permute-start.11 = (f32[9,64,256]{2,1,0:T(8,128)S(1)}, f32[9,64,256]{2,1,0:T(8,128)S(1)}, u32[]{:S(2)}, u32[]{:S(2)}) collective-permute-start(f32[9,64,256]{2,1,0:T(8,128)S(1)} %constant_dynamic-slice_fusion.12), channel_id=1, source_target_pairs={{0,16},{16,0},{32,48},{48,32},{64,80},{80,64},{96,112},{112,96},{1... | collective-permute-start | bytes 1769480 | tf_op jit(solution)/shard_map/ppermute | solution.py:30
  91.5 16.3 %collective-permute-start.8 = (f32[9,64,256]{2,1,0:T(8,128)S(1)}, f32[9,64,256]{2,1,0:T(8,128)S(1)}, u32[]{:S(2)}, u32[]{:S(2)}) collective-permute-start(f32[9,64,256]{2,1,0:T(8,128)S(1)} %constant_dynamic-slice_fusion.15), channel_id=1, source_target_pairs={{0,2},{2,0},{4,6},{6,4},{8,10},{10,8},{12,14},{14,12},{1,3},{3,1},... | collective-permute-start | bytes 1769480 | tf_op jit(solution)/shard_map/ppermute | solution.py:30
  97.1 15.1 %collective-permute-start.15 = (f32[9,32,256]{2,1,0:T(8,128)S(1)}, f32[9,32,256]{2,1,0:T(8,128)S(1)}, u32[]{:S(2)}, u32[]{:S(2)}) collective-permute-start(f32[9,32,256]{2,1,0:T(8,128)S(1)} %constant_dynamic-slice_fusion.8), channel_id=1, source_target_pairs={{0,2},{2,0},{4,6},{6,4},{8,10},{10,8},{12,14},{14,12},{1,3},{3,1},... | collective-permute-start | bytes 884744 | tf_op jit(solution)/shard_map/ppermute | solution.py:30
  102.5 10.9 %collective-permute-start.12 = (f32[9,32,256]{2,1,0:T(8,128)S(1)}, f32[9,32,256]{2,1,0:T(8,128)S(1)}, u32[]{:S(2)}, u32[]{:S(2)}) collective-permute-start(f32[9,32,256]{2,1,0:T(8,128)S(1)} %constant_dynamic-slice_fusion.11), channel_id=1, source_target_pairs={{0,64},{16,80},{32,96},{48,112},{64,0},{80,16},{96,32},{112,48},{1... | collective-permute-start | bytes 884744 | tf_op jit(solution)/shard_map/ppermute | solution.py:30
  107.9 8.3 %collective-permute-start.9 = (f32[9,32,256]{2,1,0:T(8,128)S(1)}, f32[9,32,256]{2,1,0:T(8,128)S(1)}, u32[]{:S(2)}, u32[]{:S(2)}) collective-permute-start(f32[9,32,256]{2,1,0:T(8,128)S(1)} %constant_dynamic-slice_fusion.14), channel_id=1, source_target_pairs={{0,16},{16,0},{32,48},{48,32},{64,80},{80,64},{96,112},{112,96},{1... | collective-permute-start | bytes 884744 | tf_op jit(solution)/shard_map/ppermute | solution.py:30
  112.3 5.6 %collective-permute-start.16 = (f32[9,16,256]{2,1,0:T(8,128)S(1)}, f32[9,16,256]{2,1,0:T(8,128)S(1)}, u32[]{:S(2)}, u32[]{:S(2)}) collective-permute-start(f32[9,16,256]{2,1,0:T(8,128)S(1)} %constant_dynamic-slice_fusion.7), channel_id=1, source_target_pairs={{0,16},{16,0},{32,48},{48,32},{64,80},{80,64},{96,112},{112,96},{1... | collective-permute-start | bytes 442376 | tf_op jit(solution)/shard_map/ppermute | solution.py:30
  113.5 5.2 %collective-permute-start.13 = (f32[9,16,256]{2,1,0:T(8,128)S(1)}, f32[9,16,256]{2,1,0:T(8,128)S(1)}, u32[]{:S(2)}, u32[]{:S(2)}) collective-permute-start(f32[9,16,256]{2,1,0:T(8,128)S(1)} %constant_dynamic-slice_fusion.10), channel_id=1, source_target_pairs={{0,2},{2,0},{4,6},{6,4},{8,10},{10,8},{12,14},{14,12},{1,3},{3,1},... | collective-permute-start | bytes 442376 | tf_op jit(solution)/shard_map/ppermute | solution.py:30
  116.3 5.5 %copy-start.5 = (f32[2,8,64,256]{3,2,1,0:T(8,128)S(1)}, f32[2,8,64,256]{3,2,1,0:T(8,128)}, u32[]{:S(2)}) copy-start(f32[2,8,64,256]{3,2,1,0:T(8,128)} %fusion.4) | copy-start | bytes 3145732
  116.3 5.5 %copy-start.6 = (f32[2,8,64,256]{3,2,1,0:T(8,128)S(1)}, f32[2,8,64,256]{3,2,1,0:T(8,128)}, u32[]{:S(2)}) copy-start(f32[2,8,64,256]{3,2,1,0:T(8,128)} %fusion.5) | copy-start | bytes 3145732
  116.3 5.2 %collective-permute-start.10 = (f32[9,16,256]{2,1,0:T(8,128)S(1)}, f32[9,16,256]{2,1,0:T(8,128)S(1)}, u32[]{:S(2)}, u32[]{:S(2)}) collective-permute-start(f32[9,16,256]{2,1,0:T(8,128)S(1)} %constant_dynamic-slice_fusion.13), channel_id=1, source_target_pairs={{0,64},{16,80},{32,96},{48,112},{64,0},{80,16},{96,32},{112,48},{1... | collective-permute-start | bytes 442376 | tf_op jit(solution)/shard_map/ppermute | solution.py:30
  121.7 7.5 %collective-permute-start.17 = (f32[3,9,8,256]{3,2,1,0:T(8,128)S(1)}, f32[3,9,8,256]{3,2,1,0:T(8,128)S(1)}, u32[]{:S(2)}, u32[]{:S(2)}) collective-permute-start(f32[3,9,8,256]{3,2,1,0:T(8,128)S(1)} %constant_dynamic-slice_fusion.6), channel_id=1, source_target_pairs={{0,32},{16,48},{32,0},{48,16},{64,96},{80,112},{96,64},{112,80},{1... | collective-permute-start | bytes 663560 | tf_op jit(solution)/shard_map/ppermute | solution.py:30
  129.3 6.3 %collective-permute-start.18 = (f32[3,9,4,256]{3,2,1,0:T(4,128)S(1)}, f32[3,9,4,256]{3,2,1,0:T(4,128)S(1)}, u32[]{:S(2)}, u32[]{:S(2)}) collective-permute-start(f32[3,9,4,256]{3,2,1,0:T(4,128)S(1)} %constant_dynamic-slice_fusion.5), channel_id=1, source_target_pairs={{0,128},{16,144},{32,160},{48,176},{64,192},{80,208},{96,224},{112... | collective-permute-start | bytes 331784 | tf_op jit(solution)/shard_map/ppermute | solution.py:30
  135.7 5.1 %collective-permute-start.19 = (f32[3,9,2,256]{3,2,1,0:T(2,128)S(1)}, f32[3,9,2,256]{3,2,1,0:T(2,128)S(1)}, u32[]{:S(2)}, u32[]{:S(2)}) collective-permute-start(f32[3,9,2,256]{3,2,1,0:T(2,128)S(1)} %constant_dynamic-slice_fusion.4), channel_id=1, source_target_pairs={{0,4},{2,6},{4,0},{6,2},{8,12},{10,14},{12,8},{14,10},{1,5},{3,7},... | collective-permute-start | bytes 165896 | tf_op jit(solution)/shard_map/ppermute | solution.py:30
  140.9 27.9 %collective-permute-start.22 = (f32[9,1,256]{2,0,1:T(8,128)S(1)}, f32[9,1,256]{2,0,1:T(8,128)S(1)}, u32[]{:S(2)}, u32[]{:S(2)}) collective-permute-start(f32[9,1,256]{2,0,1:T(8,128)S(1)} %bitcast.398), channel_id=1, source_target_pairs={{0,0},{1,128},{2,16},{3,144},{4,2},{5,130},{6,18},{7,146},{8,1},{9... | collective-permute-start | bytes 27656 | tf_op jit(solution)/shard_map/ppermute | solution.py:94
  144.1 24.8 %collective-permute-start.23 = (f32[9,1,256]{2,0,1:T(8,128)S(1)}, f32[9,1,256]{2,0,1:T(8,128)S(1)}, u32[]{:S(2)}, u32[]{:S(2)}) collective-permute-start(f32[9,1,256]{2,0,1:T(8,128)S(1)} %bitcast.397), channel_id=1, source_target_pairs={{0,1},{1,129},{2,17},{3,145},{4,3},{5,131},{6,19},{7,147},{8,0},{9... | collective-permute-start | bytes 27656 | tf_op jit(solution)/shard_map/ppermute | solution.py:94
  145.6 23.3 %collective-permute-start.25 = (f32[9,1,256]{2,1,0:T(1,128)S(1)}, f32[9,1,256]{2,1,0:T(1,128)S(1)}, u32[]{:S(2)}, u32[]{:S(2)}) collective-permute-start(f32[9,1,256]{2,1,0:T(1,128)S(1)} %get-tuple-element.29), channel_id=1, source_target_pairs={{0,1},{1,129},{2,33},{3,161},{4,3},{5,131},{6,35},{7,163},{8,0},{9... | collective-permute-start | bytes 27656 | tf_op jit(solution)/shard_map/ppermute | solution.py:94
  147.8 21.1 %collective-permute-start.24 = (f32[9,1,256]{2,0,1:T(8,128)S(1)}, f32[9,1,256]{2,0,1:T(8,128)S(1)}, u32[]{:S(2)}, u32[]{:S(2)}) collective-permute-start(f32[9,1,256]{2,0,1:T(8,128)S(1)} %bitcast.400), channel_id=1, source_target_pairs={{0,0},{1,128},{2,32},{3,160},{4,2},{5,130},{6,34},{7,162},{8,1},{9... | collective-permute-start | bytes 27656 | tf_op jit(solution)/shard_map/ppermute | solution.py:94
  151.5 18.8 %collective-permute-start.20 = (f32[9,1,256]{2,0,1:T(8,128)S(1)}, f32[9,1,256]{2,0,1:T(8,128)S(1)}, u32[]{:S(2)}, u32[]{:S(2)}) collective-permute-start(f32[9,1,256]{2,0,1:T(8,128)S(1)} %bitcast.399), channel_id=1, source_target_pairs={{0,0},{1,128},{2,64},{3,192},{4,2},{5,130},{6,66},{7,194},{8,1},{9... | collective-permute-start | bytes 27656 | tf_op jit(solution)/shard_map/ppermute | solution.py:94
  168.8 10.1 %collective-permute-start.21 = (f32[9,1,256]{2,0,1:T(8,128)S(1)}, f32[9,1,256]{2,0,1:T(8,128)S(1)}, u32[]{:S(2)}, u32[]{:S(2)}) collective-permute-start(f32[9,1,256]{2,0,1:T(8,128)S(1)} %bitcast.401), channel_id=1, source_target_pairs={{0,1},{1,129},{2,65},{3,193},{4,3},{5,131},{6,67},{7,195},{8,0},{9... | collective-permute-start | bytes 27656 | tf_op jit(solution)/shard_map/ppermute | solution.py:94

commit v3 on v1

--- a/solution.py
+++ b/solution.py
@@ -4,8 +4,19 @@
 from jax.sharding import PartitionSpec as P
 
 
+GROUP = ("gy", "gx")
+
+
+def axis_count(axis):
+    names = axis if isinstance(axis, tuple) else (axis,)
+    count = 1
+    for name in names:
+        count *= lax.axis_size(name)
+    return count
+
+
 def passed_along(value, axis, by):
-    length = lax.axis_size(axis)
+    length = axis_count(axis)
     pairs = [(i, i + by) for i in range(length) if 0 <= i + by < length]
     return lax.ppermute(value, axis, pairs)
 
@@ -26,7 +37,7 @@
     bit = (lax.axis_index(axis) // flip) % 2
     keep = lax.dynamic_slice_in_dim(x, bit * size, size, axis=dim)
     give = lax.dynamic_slice_in_dim(x, (1 - bit) * size, size, axis=dim)
-    pairs = [(i, i ^ flip) for i in range(lax.axis_size(axis))]
+    pairs = [(i, i ^ flip) for i in range(axis_count(axis))]
     return keep + lax.ppermute(give, axis, pairs)
 
 
@@ -37,15 +48,16 @@
 
 
 def owner_pairs(order, sizes):
-    names = ("group", "dp", "space")
-    count = sizes["group"] * sizes["dp"] * sizes["space"]
+    names = tuple(sizes)
+    count = 1
+    for name in names:
+        count *= sizes[name]
     pairs = []
     for linear in range(count):
-        where = {
-            "group": linear // (sizes["dp"] * sizes["space"]),
-            "dp": (linear // sizes["space"]) % sizes["dp"],
-            "space": linear % sizes["space"],
-        }
+        where, rest = {}, linear
+        for name in reversed(names):
+            where[name] = rest % sizes[name]
+            rest //= sizes[name]
         chunk = 0
         for axis, flip in order:
             chunk = chunk * 2 + (where[axis] // flip) % 2
@@ -55,14 +67,12 @@
 
 def reduce_weight_grad(total):
     ntaps, chans, outs = total.shape
-    sizes = {name: lax.axis_size(name) for name in ("group", "dp", "space")}
-    ng = sizes["group"]
-    across = 4 if ng % 4 == 0 else ng
-    down = ng // across
-    assert chans * sizes["space"] == ng * sizes["dp"] * sizes["space"]
+    sizes = {name: lax.axis_size(name) for name in GROUP + ("dp", "space")}
+    down, across = sizes["gy"], sizes["gx"]
+    assert chans * 2 == down * across * sizes["dp"] * sizes["space"]
     first = ("space", 1)
-    ys = [("group", across << b) for b in range(bits_of(down))]
-    xs = [("group", 1 << b) for b in range(bits_of(across))]
+    ys = [("gy", 1 << b) for b in range(bits_of(down))]
+    xs = [("gx", 1 << b) for b in range(bits_of(across))]
     ds = [("dp", 1 << b) for b in range(bits_of(sizes["dp"]))]
     assert sizes["space"] == 2
     lanes = (ds, xs, ys)
@@ -88,7 +98,8 @@
 
 
 def clip_tables(clip_id, frames):
-    ids = lax.all_gather(clip_id, "group", axis=1, tiled=True)
+    ids = lax.all_gather(clip_id, "gx", axis=1, tiled=True)
+    ids = lax.all_gather(ids, "gy", axis=1, tiled=True)
     total = ids.shape[1]
     index = jnp.arange(total, dtype=jnp.int32)[None, :]
     prev = jnp.concatenate([jnp.full_like(ids[:, :1], -1), ids[:, :-1]], axis=1)
@@ -97,7 +108,7 @@
     position = index - start
     ext = jnp.concatenate([jnp.full_like(ids[:, :2], -1), ids], axis=1)
     same = jnp.stack([ext[:, 2 - k : 2 - k + total] == ids for k in range(3)], axis=0)
-    first = lax.axis_index("group") * frames
+    first = lax.axis_index(GROUP) * frames
     pos_pad = jnp.concatenate([jnp.zeros_like(position[:, :2]), position], axis=1)
     pos_wide = lax.dynamic_slice_in_dim(pos_pad, first, frames + 2, axis=1)
     same_pad = jnp.concatenate([same, jnp.zeros_like(same[:, :, :2])], axis=2)
@@ -112,7 +123,7 @@
     rows = video.shape[2]
     cols = video.shape[3]
     chans = video.shape[4]
-    past = passed_along(lax.slice_in_dim(video, frames - 2, None, axis=1), "group", 1)
+    past = passed_along(lax.slice_in_dim(video, frames - 2, None, axis=1), GROUP, 1)
     vwide = row_halo(jnp.concatenate([past, video], axis=1), "space", 2)
     pos_wide, same_fwd, same_bwd = clip_tables(clip_id, frames)
     omega = 0.37 * (jnp.arange(chans) % 8 + 1).astype(jnp.float32)
@@ -140,7 +151,7 @@
     delta = (cotangent.astype(jnp.float32) * sigma * (1.0 + pre * (1.0 - sigma))).astype(
         jnp.bfloat16
     )
-    ahead = passed_along(lax.slice_in_dim(delta, 0, 2, axis=1), "group", -1)
+    ahead = passed_along(lax.slice_in_dim(delta, 0, 2, axis=1), GROUP, -1)
     gwide = row_halo(jnp.concatenate([delta, ahead], axis=1), "space", 2)
     swap = [(0, 1), (1, 0)]
     half = chans // 2
@@ -179,20 +190,16 @@
 
 
 def solution(mesh):
-    placed = (
-        P("dp", "group", "space", None, None),
-        P("dp", "group", "space", None, None),
-        P(),
-        P("dp", "group"),
-    )
+    whole = mesh.devices
+    across = 4 if whole.shape[0] % 4 == 0 else whole.shape[0]
+    fine = jax.sharding.Mesh(
+        whole.reshape((whole.shape[0] // across, across) + whole.shape[1:]), GROUP + ("dp", "space")
+    )
+    video_spec = P("dp", GROUP, "space", None, None)
     return jax.shard_map(
         local,
-        mesh=mesh,
-        in_specs=placed,
-        out_specs=(
-            P("dp", "group", "space", None, None),
-            P("dp", "group", "space", None, None),
-            P(None, ("group", "dp", "space")),
-        ),
+        mesh=fine,
+        in_specs=(video_spec, video_spec, P(), P("dp", GROUP)),
+        out_specs=(video_spec, video_spec, P(None, GROUP + ("dp", "space"))),
         check_vma=False,
     )

time: 174 us -> 177 us (1.017)
  starting transfers between devices: 73.7 us -> 70.6 us
  waiting for transfers between devices: 35.9 us -> 38.3 us
  blocking collectives: 14.6 us -> 16.5 us
    unnamed x1 -> x2, blocking collectives: 14.6 us -> 16.5 us
    unnamed x21 -> x24, local copies, waits for them, and re-layouts: 5.72 us -> 7.23 us
where the time goes in v3:
time: 177 us; the launch traced here: 176 us
  starting transfers between devices  70.6 us (40%)
  waiting for transfers between devices  38.3 us (22%)
  local copies, waits for them, and re-layouts  20.3 us (11%)
  matrix products  19.4 us (11%)
  blocking collectives  16.5 us (9%)
  other arithmetic  8.02 us (5%)
  between operations  2.87 us (2%)
    ppermute x3, starting transfers between devices, reduce_weight_grad(): parts.append(lax.ppermute(joined[n], names, pairs).reshape(per, outs))  26.6 us
    ppermute x13, waiting for transfers between devices, halve(): return keep + lax.ppermute(give, axis, pairs)  25.8 us
    ppermute x13, starting transfers between devices, halve(): return keep + lax.ppermute(give, axis, pairs)  25.1 us
    unnamed x2, blocking collectives  16.5 us
    ppermute x2, starting transfers between devices, row_halo(): high = lax.ppermute(lax.slice_in_dim(block, 0, 1, axis=dim), axis, backward)  8.1 us
    ppermute x2, starting transfers between devices, passed_along(): return lax.ppermute(value, axis, pairs)  7.54 us
    unnamed x24, local copies, waits for them, and re-layouts  7.23 us
    dot_general x9, matrix products, local(): jnp.einsum('sfhwk,kc->sfhwc', block, back[k, a], preferred_element_type=j...  6.97 us
  transfers between devices with their start and end apart: 24, of which 13 were waited for; matrix products, arithmetic and copies ran while one was open for 15% of the time, Pallas kernels for 0%

profile of v3, /device:TPU:25, one launch (start us, length us, event | category | flops | bytes accessed | tf_op | source)
XLA Modules:
  0.0 176.1 jit_solution(4436425073861890189)
XLA Ops:
  0.6 3.1 %collective-permute-start = (bf16[1,2,8,64,256]{4,3,2,1,0:T(8,128)(2,1)}, bf16[1,2,8,64,256]{4,3,2,1,0:T(8,128)(2,1)S(1)}, u32[]{:S(2)}, u32[]{:S(2)}) collective-permute-start(bf16[1,2,8,64,256]{4,3,2,1,0:T(8,128)(2,1)} %param.4), channel_id=1, source_target_pairs={{0,16},{16,32},{32,48},{48,64},{64,80},{80,96},{96,112},{112,128},... | collective-permute-start | bytes 1572872 | tf_op jit(solution)/shard_map/ppermute | solution.py:21
  3.8 1.3 dynamic-slice
  5.7 0.8 bitcast_dynamic-update-slice_fusion
  6.5 11.5 %all-reduce.6 = s32[8]{0:T(128)S(1)} all-reduce(s32[8]{0:T(128)S(1)} %bitcast_dynamic-update-slice_fusion), channel_id=1, replica_groups=mesh['gy'=4,'gx'=4,'dp'=8,'space'=2] {'gx'}, use_global_device_ids=true, to_apply=%add.6 | all-reduce | flops 8 | bytes 64
  17.9 1.3 dynamic-slice.1
  20.1 5.1 %all-reduce.7 = s32[32]{0:T(128)S(1)} all-reduce(s32[32]{0:T(128)S(1)} %dynamic-update-slice.1), channel_id=1, replica_groups=mesh['gy'=4,'gx'=4,'dp'=8,'space'=2] {'gy'}, use_global_device_ids=true, to_apply=%add.7 | all-reduce | flops 32 | bytes 256
  26.0 1.1 constant_dynamic-update-slice_fusion
  27.1 5.5 %collective-permute-start.2 = (bf16[1,4,1,64,256]{4,3,2,1,0:T(8,128)(2,1)S(1)}, bf16[1,4,1,64,256]{4,3,2,1,0:T(8,128)(2,1)S(1)}, u32[]{:S(2)}, u32[]{:S(2)}) collective-permute-start(bf16[1,4,1,64,256]{4,3,2,1,0:T(8,128)(2,1)S(1)} %get-tuple-element.24), channel_id=1, source_target_pairs={{1,0},{3,2},{5,4},{7,6},{9,8},{11,10},{13,12},{15,14},{17,16},{19,... | collective-permute-start | bytes 393224 | tf_op jit(solution)/shard_map/ppermute | solution.py:31
  32.5 1.3 collective-permute-start.1
  33.9 1.9 %collective-permute-done.1 = bf16[1,4,1,64,256]{4,3,2,1,0:T(8,128)(2,1)S(1)} collective-permute-done((bf16[1,4,1,64,256]{4,3,2,1,0:T(8,128)(2,1)S(1)}, bf16[1,4,1,64,256]{4,3,2,1,0:T(8,128)(2,1)S(1)}, u32[]{:S(2)}, u32[]{:S(2)}) %collective-permute-start.1) | collective-permute-done | bytes 131104 | tf_op jit(solution)/shard_map/ppermute | solution.py:28
  36.1 0.9 pad_slice_fusion.3
  37.4 1.6 copy-done.1
  42.5 0.6 fusion.50
  44.2 1.0 fusion.93
  45.2 4.4 %collective-permute-start.3 = (bf16[1,2,8,64,256]{4,3,2,1,0:T(8,128)(2,1)S(1)}, bf16[1,2,8,64,256]{4,3,2,1,0:T(8,128)(2,1)S(1)}, u32[]{:S(2)}, u32[]{:S(2)}) collective-permute-start(bf16[1,2,8,64,256]{4,3,2,1,0:T(8,128)(2,1)S(1)} %get-tuple-element.39), channel_id=1, source_target_pairs={{16,0},{32,16},{48,32},{64,48},{80,64},{96,80},{112,96},{128,112},... | collective-permute-start | bytes 1572872 | tf_op jit(solution)/shard_map/ppermute | solution.py:21
  49.9 6.1 %copy.34 = bf16[3,3,3,256,256]{3,4,2,1,0:T(8,128)(2,1)} copy(bf16[3,3,3,256,256]{4,3,2,1,0:T(8,128)(2,1)} %bitcast.370) | data formatting | bytes 7077888 | tf_op jit(solution)/shard_map/reshape | solution.py:176
  56.5 1.1 fusion.103
  57.6 4.4 %collective-permute-done.3 = bf16[1,2,8,64,256]{4,3,2,1,0:T(8,128)(2,1)S(1)} collective-permute-done((bf16[1,2,8,64,256]{4,3,2,1,0:T(8,128)(2,1)S(1)}, bf16[1,2,8,64,256]{4,3,2,1,0:T(8,128)(2,1)S(1)}, u32[]{:S(2)}, u32[]{:S(2)}) %collective-permute-start.3) | collective-permute-done | bytes 524320 | tf_op jit(solution)/shard_map/ppermute | solution.py:21
  62.0 2.6 %collective-permute-start.5 = (bf16[1,4,1,64,256]{4,3,2,1,0:T(8,128)(2,1)S(1)}, bf16[1,4,1,64,256]{4,3,2,1,0:T(8,128)(2,1)S(1)}, u32[]{:S(2)}, u32[]{:S(2)}) collective-permute-start(bf16[1,4,1,64,256]{4,3,2,1,0:T(8,128)(2,1)S(1)} %get-tuple-element.22), channel_id=1, source_target_pairs={{1,0},{3,2},{5,4},{7,6},{9,8},{11,10},{13,12},{15,14},{17,16},{19,... | collective-permute-start | bytes 393224 | tf_op jit(solution)/shard_map/ppermute | solution.py:31
  64.6 1.5 collective-permute-start.4
  66.1 1.9 %broadcast_multiply_fusion.2 = (bf16[2,2,8,64,256]{4,3,2,1,0:T(8,128)(2,1)}, bf16[2,2,8,64,256]{4,3,2,1,0:T(8,128)(2,1)}, bf16[2,2,8,64,256]{4,3,2,1,0:T(8,128)(2,1)}) fusion(bf16[2]{0:T(256)(128)(2,1)S(1)} %get-tuple-element.31, bf16[1,2,8,64,256]{4,3,2,1,0:T(8,128)(2,1)S(1)} %collective-permute-done.7, ...), kind=kLoop, calls=%fused_computation.130 | loop fusion | flops 2097152 | bytes 4194316 | tf_op jit(solution)/shard_map/mul | solution.py:165
  68.0 0.8 select_maximum_fusion
  68.8 0.9 fusion.116
  70.2 1.6 copy-done
  72.9 1.6 fusion.4
  75.3 1.3 pad_slice_fusion.1
  76.7 0.6 pad_maximum_fusion.2
  77.3 2.3 %fusion.115 = (bf16[2,2,8,64,384]{4,3,2,1,0:T(8,128)(2,1)S(1)}, bf16[2,2,8,64,384]{4,3,2,1,0:T(8,128)(2,1)S(1)}, bf16[2,2,8,64,384]{4,3,2,1,0:T(8,128)(2,1)S(1)}...) fusion(bf16[2,4,10,64,384]{4,3,2,1,0:T(8,128)(2,1)S(1)} %pad_ma, ...), kind=kLoop, calls=%fused_computation.215 | loop fusion | bytes 28311552 | tf_op jit(solution)/shard_map/slice | solution.py:167
  79.6 1.9 %fusion.90 = f32[1,384,256]{2,1,0:T(8,128)S(1)} fusion(bf16[2,2,8,64,384]{4,3,2,1,0:T(8,128)(2,1)S(1)} %get-tuple-element.4, bf16[2,2,8,64,256]{4,3,2,1,0:T(8,128)(2,1)} %get-tuple-element.20), kind=kOutput, calls=%fused_computation.106 | convolution fusion | flops 402653184 | bytes 3014656 | tf_op jit(solution)/shard_map/sfhwk,sfhwc->kc/dot_general | solution.py:169
  81.6 0.6 fusion.87
  82.2 0.6 fusion.84
  82.9 1.3 collective-permute-start.14
  84.9 0.6 fusion.78
  85.5 0.6 fusion.75
  86.3 1.5 collective-permute-start.11
  87.8 0.6 fusion.72
  88.4 0.6 fusion.69
  89.0 0.6 fusion.66
  89.8 1.7 collective-permute-start.8
  91.5 5.3 %collective-permute-done.14 = f32[9,64,256]{2,1,0:T(8,128)S(1)} collective-permute-done((f32[9,64,256]{2,1,0:T(8,128)S(1)}, f32[9,64,256]{2,1,0:T(8,128)S(1)}, u32[]{:S(2)}, u32[]{:S(2)}) %collective-permute-start.14) | collective-permute-done | bytes 589856 | tf_op jit(solution)/shard_map/ppermute | solution.py:41
  96.9 1.7 collective-permute-start.15
  98.6 1.4 collective-permute-done.11
  100.1 1.3 collective-permute-start.12
  101.5 2.2 %collective-permute-done.8 = f32[9,64,256]{2,1,0:T(8,128)S(1)} collective-permute-done((f32[9,64,256]{2,1,0:T(8,128)S(1)}, f32[9,64,256]{2,1,0:T(8,128)S(1)}, u32[]{:S(2)}, u32[]{:S(2)}) %collective-permute-start.8) | collective-permute-done | bytes 589856 | tf_op jit(solution)/shard_map/ppermute | solution.py:41
  103.8 1.1 collective-permute-start.9
  104.9 5.1 %collective-permute-done.15 = f32[9,32,256]{2,1,0:T(8,128)S(1)} collective-permute-done((f32[9,32,256]{2,1,0:T(8,128)S(1)}, f32[9,32,256]{2,1,0:T(8,128)S(1)}, u32[]{:S(2)}, u32[]{:S(2)}) %collective-permute-start.15) | collective-permute-done | bytes 294944 | tf_op jit(solution)/shard_map/ppermute | solution.py:41
  110.1 1.1 collective-permute-start.16
  111.2 1.4 collective-permute-start.13
  113.0 2.8 %collective-permute-done.16 = f32[9,16,256]{2,1,0:T(8,128)S(1)} collective-permute-done((f32[9,16,256]{2,1,0:T(8,128)S(1)}, f32[9,16,256]{2,1,0:T(8,128)S(1)}, u32[]{:S(2)}, u32[]{:S(2)}) %collective-permute-start.16) | collective-permute-done | bytes 147488 | tf_op jit(solution)/shard_map/ppermute | solution.py:41
  115.8 1.2 collective-permute-done.10
  117.1 2.3 %collective-permute-start.17 = (f32[3,9,8,256]{3,2,1,0:T(8,128)S(1)}, f32[3,9,8,256]{3,2,1,0:T(8,128)S(1)}, u32[]{:S(2)}, u32[]{:S(2)}) collective-permute-start(f32[3,9,8,256]{3,2,1,0:T(8,128)S(1)} %constant_dynamic-slice_fusion.3), channel_id=1, source_target_pairs={{0,32},{16,48},{32,0},{48,16},{1,33},{17,49},{33,1},{49,17},{2,34}... | collective-permute-start | bytes 663560 | tf_op jit(solution)/shard_map/ppermute | solution.py:41
  120.0 3.5 %collective-permute-done.17 = f32[3,9,8,256]{3,2,1,0:T(8,128)S(1)} collective-permute-done((f32[3,9,8,256]{3,2,1,0:T(8,128)S(1)}, f32[3,9,8,256]{3,2,1,0:T(8,128)S(1)}, u32[]{:S(2)}, u32[]{:S(2)}) %collective-permute-start.17) | collective-permute-done | bytes 221216 | tf_op jit(solution)/shard_map/ppermute | solution.py:41
  123.6 2.8 %collective-permute-start.18 = (f32[3,9,4,256]{3,2,1,0:T(4,128)S(1)}, f32[3,9,4,256]{3,2,1,0:T(4,128)S(1)}, u32[]{:S(2)}, u32[]{:S(2)}) collective-permute-start(f32[3,9,4,256]{3,2,1,0:T(4,128)S(1)} %constant_dynamic-slice_fusion.2), channel_id=1, source_target_pairs={{0,128},{64,192},{128,0},{192,64},{1,129},{65,193},{129,1},{193,65... | collective-permute-start | bytes 331784 | tf_op jit(solution)/shard_map/ppermute | solution.py:41
  127.0 1.8 %collective-permute-done.18 = f32[3,9,4,256]{3,2,1,0:T(4,128)S(1)} collective-permute-done((f32[3,9,4,256]{3,2,1,0:T(4,128)S(1)}, f32[3,9,4,256]{3,2,1,0:T(4,128)S(1)}, u32[]{:S(2)}, u32[]{:S(2)}) %collective-permute-start.18) | collective-permute-done | bytes 110624 | tf_op jit(solution)/shard_map/ppermute | solution.py:41
  128.8 3.1 %collective-permute-start.19 = (f32[3,9,2,256]{3,2,1,0:T(2,128)S(1)}, f32[3,9,2,256]{3,2,1,0:T(2,128)S(1)}, u32[]{:S(2)}, u32[]{:S(2)}) collective-permute-start(f32[3,9,2,256]{3,2,1,0:T(2,128)S(1)} %constant_dynamic-slice_fusion.1), channel_id=1, source_target_pairs={{0,4},{2,6},{4,0},{6,2},{8,12},{10,14},{12,8},{14,10},{1,5},{3,7},... | collective-permute-start | bytes 165896 | tf_op jit(solution)/shard_map/ppermute | solution.py:41
  132.5 1.9 %collective-permute-done.19 = f32[3,9,2,256]{3,2,1,0:T(2,128)S(1)} collective-permute-done((f32[3,9,2,256]{3,2,1,0:T(2,128)S(1)}, f32[3,9,2,256]{3,2,1,0:T(2,128)S(1)}, u32[]{:S(2)}, u32[]{:S(2)}) %collective-permute-start.19) | collective-permute-done | bytes 55328 | tf_op jit(solution)/shard_map/ppermute | solution.py:41
  134.5 5.5 %collective-permute-start.20 = (f32[3,9,1,256]{3,2,1,0:T(1,128)S(1)}, f32[3,9,1,256]{3,2,1,0:T(1,128)S(1)}, u32[]{:S(2)}, u32[]{:S(2)}) collective-permute-start(f32[3,9,1,256]{3,2,1,0:T(1,128)S(1)} %constant_dynamic-slice_fusion), channel_id=1, source_target_pairs={{0,8},{2,10},{4,12},{6,14},{8,0},{10,2},{12,4},{14,6},{1,9},{3,11}... | collective-permute-start | bytes 82952 | tf_op jit(solution)/shard_map/ppermute | solution.py:41
  140.5 0.7 collective-permute-done.20
  141.2 12.1 %collective-permute-start.23 = (f32[9,1,256]{2,1,0:T(1,128)S(1)}, f32[9,1,256]{2,1,0:T(1,128)S(1)}, u32[]{:S(2)}, u32[]{:S(2)}) collective-permute-start(f32[9,1,256]{2,1,0:T(1,128)S(1)} %get-tuple-element.26), channel_id=1, source_target_pairs={{0,0},{1,128},{2,32},{3,160},{4,2},{5,130},{6,34},{7,162},{8,1},{9... | collective-permute-start | bytes 27656 | tf_op jit(solution)/shard_map/ppermute | solution.py:96
  153.4 12.5 %collective-permute-start.22 = (f32[9,1,256]{2,0,1:T(8,128)S(1)}, f32[9,1,256]{2,0,1:T(8,128)S(1)}, u32[]{:S(2)}, u32[]{:S(2)}) collective-permute-start(f32[9,1,256]{2,0,1:T(8,128)S(1)} %bitcast.389), channel_id=1, source_target_pairs={{0,0},{1,128},{2,16},{3,144},{4,2},{5,130},{6,18},{7,146},{8,1},{9... | collective-permute-start | bytes 27656 | tf_op jit(solution)/shard_map/ppermute | solution.py:96
  165.9 1.9 %collective-permute-start.21 = (f32[9,1,256]{2,0,1:T(8,128)S(1)}, f32[9,1,256]{2,0,1:T(8,128)S(1)}, u32[]{:S(2)}, u32[]{:S(2)}) collective-permute-start(f32[9,1,256]{2,0,1:T(8,128)S(1)} %bitcast.390), channel_id=1, source_target_pairs={{0,0},{1,128},{2,64},{3,192},{4,2},{5,130},{6,66},{7,194},{8,1},{9... | collective-permute-start | bytes 27656 | tf_op jit(solution)/shard_map/ppermute | solution.py:96
  167.8 1.4 fusion.65
  169.2 6.3 %collective-permute-done.21 = f32[9,1,256]{2,0,1:T(8,128)S(1)} collective-permute-done((f32[9,1,256]{2,0,1:T(8,128)S(1)}, f32[9,1,256]{2,0,1:T(8,128)S(1)}, u32[]{:S(2)}, u32[]{:S(2)}) %collective-permute-start.21) | collective-permute-done | bytes 9248 | tf_op jit(solution)/shard_map/ppermute | solution.py:96
  175.5 0.6 pad_maximum_fusion.10
  (99 shorter events, 13.9 us)
Async XLA Ops:
  0.6 25.3 %collective-permute-start = (bf16[1,2,8,64,256]{4,3,2,1,0:T(8,128)(2,1)}, bf16[1,2,8,64,256]{4,3,2,1,0:T(8,128)(2,1)S(1)}, u32[]{:S(2)}, u32[]{:S(2)}) collective-permute-start(bf16[1,2,8,64,256]{4,3,2,1,0:T(8,128)(2,1)} %param.4), channel_id=1, source_target_pairs={{0,16},{16,32},{32,48},{48,64},{64,80},{80,96},{96,112},{112,128},... | collective-permute-start | bytes 1572872 | tf_op jit(solution)/shard_map/ppermute | solution.py:21
  27.1 6.8 %collective-permute-start.2 = (bf16[1,4,1,64,256]{4,3,2,1,0:T(8,128)(2,1)S(1)}, bf16[1,4,1,64,256]{4,3,2,1,0:T(8,128)(2,1)S(1)}, u32[]{:S(2)}, u32[]{:S(2)}) collective-permute-start(bf16[1,4,1,64,256]{4,3,2,1,0:T(8,128)(2,1)S(1)} %get-tuple-element.24), channel_id=1, source_target_pairs={{1,0},{3,2},{5,4},{7,6},{9,8},{11,10},{13,12},{15,14},{17,16},{19,... | collective-permute-start | bytes 393224 | tf_op jit(solution)/shard_map/ppermute | solution.py:31
  32.5 3.2 %collective-permute-start.1 = (bf16[1,4,1,64,256]{4,3,2,1,0:T(8,128)(2,1)S(1)}, bf16[1,4,1,64,256]{4,3,2,1,0:T(8,128)(2,1)S(1)}, u32[]{:S(2)}, u32[]{:S(2)}) collective-permute-start(bf16[1,4,1,64,256]{4,3,2,1,0:T(8,128)(2,1)S(1)} %get-tuple-element.23), channel_id=1, source_target_pairs={{0,1},{2,3},{4,5},{6,7},{8,9},{10,11},{12,13},{14,15},{16,17},{18,... | collective-permute-start | bytes 393224 | tf_op jit(solution)/shard_map/ppermute | solution.py:28
  37.0 2.0 %copy-start.1 = (bf16[6912,256]{1,0:T(8,128)(2,1)S(1)}, bf16[6912,256]{1,0:T(8,128)(2,1)}, u32[]{:S(2)}) copy-start(bf16[6912,256]{1,0:T(8,128)(2,1)} %param.6) | copy-start | bytes 10616836
  43.2 1.0 copy-start.6
  45.2 16.7 %collective-permute-start.3 = (bf16[1,2,8,64,256]{4,3,2,1,0:T(8,128)(2,1)S(1)}, bf16[1,2,8,64,256]{4,3,2,1,0:T(8,128)(2,1)S(1)}, u32[]{:S(2)}, u32[]{:S(2)}) collective-permute-start(bf16[1,2,8,64,256]{4,3,2,1,0:T(8,128)(2,1)S(1)} %get-tuple-element.39), channel_id=1, source_target_pairs={{16,0},{32,16},{48,32},{64,48},{80,64},{96,80},{112,96},{128,112},... | collective-permute-start | bytes 1572872 | tf_op jit(solution)/shard_map/ppermute | solution.py:21
  55.9 10.2 %collective-permute-start.7 = (bf16[1,2,8,64,256]{4,3,2,1,0:T(8,128)(2,1)S(1)}, bf16[1,2,8,64,256]{4,3,2,1,0:T(8,128)(2,1)S(1)}, u32[]{:S(2)}, u32[]{:S(2)}) collective-permute-start(bf16[1,2,8,64,256]{4,3,2,1,0:T(8,128)(2,1)S(1)} %get-tuple-element.39), channel_id=1, source_target_pairs={{0,1},{1,0},{2,3},{3,2},{4,5},{5,4},{6,7},{7,6},{8,9},{9,8},{10,11... | collective-permute-start | bytes 1572872 | tf_op jit(solution)/shard_map/ppermute | solution.py:162
  56.4 18.6 %collective-permute-start.6 = (bf16[1,4,10,64,256]{4,3,2,1,0:T(8,128)(2,1)S(1)}, bf16[1,4,10,64,256]{4,3,2,1,0:T(8,128)(2,1)S(1)}, u32[]{:S(2)}, u32[]{:S(2)}) collective-permute-start(bf16[1,4,10,64,256]{4,3,2,1,0:T(8,128)(2,1)S(1)} %fusion.62), channel_id=1, source_target_pairs={{0,1},{1,0},{2,3},{3,2},{4,5},{5,4},{6,7},{7,6},{8,9},{9,8},{10,11... | collective-permute-start | bytes 3932168 | tf_op jit(solution)/shard_map/ppermute | solution.py:158
  62.0 6.0 %collective-permute-start.5 = (bf16[1,4,1,64,256]{4,3,2,1,0:T(8,128)(2,1)S(1)}, bf16[1,4,1,64,256]{4,3,2,1,0:T(8,128)(2,1)S(1)}, u32[]{:S(2)}, u32[]{:S(2)}) collective-permute-start(bf16[1,4,1,64,256]{4,3,2,1,0:T(8,128)(2,1)S(1)} %get-tuple-element.22), channel_id=1, source_target_pairs={{1,0},{3,2},{5,4},{7,6},{9,8},{11,10},{13,12},{15,14},{17,16},{19,... | collective-permute-start | bytes 393224 | tf_op jit(solution)/shard_map/ppermute | solution.py:31
  64.6 3.4 %collective-permute-start.4 = (bf16[1,4,1,64,256]{4,3,2,1,0:T(8,128)(2,1)S(1)}, bf16[1,4,1,64,256]{4,3,2,1,0:T(8,128)(2,1)S(1)}, u32[]{:S(2)}, u32[]{:S(2)}) collective-permute-start(bf16[1,4,1,64,256]{4,3,2,1,0:T(8,128)(2,1)S(1)} %get-tuple-element.21), channel_id=1, source_target_pairs={{0,1},{2,3},{4,5},{6,7},{8,9},{10,11},{12,13},{14,15},{16,17},{18,... | collective-permute-start | bytes 393224 | tf_op jit(solution)/shard_map/ppermute | solution.py:28
  69.7 2.0 %copy-start = (bf16[3,3,3,256,256]{3,4,2,1,0:T(8,128)(2,1)S(1)}, bf16[3,3,3,256,256]{3,4,2,1,0:T(8,128)(2,1)}, u32[]{:S(2)}) copy-start(bf16[3,3,3,256,256]{3,4,2,1,0:T(8,128)(2,1)} %copy.34) | copy-start | bytes 10616836
  79.6 1.9 %copy-start.4 = (bf16[2,2,8,64,256]{4,3,2,1,0:T(8,128)(2,1)S(1)}, bf16[2,2,8,64,256]{4,3,2,1,0:T(8,128)(2,1)}, u32[]{:S(2)}) copy-start(bf16[2,2,8,64,256]{4,3,2,1,0:T(8,128)(2,1)} %get-tuple-element.20) | copy-start | bytes 3145732
  82.8 1.5 copy-start.3
  82.9 13.8 %collective-permute-start.14 = (f32[9,64,256]{2,1,0:T(8,128)S(1)}, f32[9,64,256]{2,1,0:T(8,128)S(1)}, u32[]{:S(2)}, u32[]{:S(2)}) collective-permute-start(f32[9,64,256]{2,1,0:T(8,128)S(1)} %constant_dynamic-slice_fusion.6), channel_id=1, source_target_pairs={{0,64},{64,0},{128,192},{192,128},{1,65},{65,1},{129,193},{193,129... | collective-permute-start | bytes 1769480 | tf_op jit(solution)/shard_map/ppermute | solution.py:41
  86.1 1.7 copy-start.2
  86.3 13.8 %collective-permute-start.11 = (f32[9,64,256]{2,1,0:T(8,128)S(1)}, f32[9,64,256]{2,1,0:T(8,128)S(1)}, u32[]{:S(2)}, u32[]{:S(2)}) collective-permute-start(f32[9,64,256]{2,1,0:T(8,128)S(1)} %constant_dynamic-slice_fusion.9), channel_id=1, source_target_pairs={{0,16},{16,0},{32,48},{48,32},{1,17},{17,1},{33,49},{49,33},{2,18}... | collective-permute-start | bytes 1769480 | tf_op jit(solution)/shard_map/ppermute | solution.py:41
  89.8 13.9 %collective-permute-start.8 = (f32[9,64,256]{2,1,0:T(8,128)S(1)}, f32[9,64,256]{2,1,0:T(8,128)S(1)}, u32[]{:S(2)}, u32[]{:S(2)}) collective-permute-start(f32[9,64,256]{2,1,0:T(8,128)S(1)} %constant_dynamic-slice_fusion.12), channel_id=1, source_target_pairs={{0,2},{2,0},{4,6},{6,4},{8,10},{10,8},{12,14},{14,12},{1,3},{3,1},... | collective-permute-start | bytes 1769480 | tf_op jit(solution)/shard_map/ppermute | solution.py:41
  96.9 13.1 %collective-permute-start.15 = (f32[9,32,256]{2,1,0:T(8,128)S(1)}, f32[9,32,256]{2,1,0:T(8,128)S(1)}, u32[]{:S(2)}, u32[]{:S(2)}) collective-permute-start(f32[9,32,256]{2,1,0:T(8,128)S(1)} %constant_dynamic-slice_fusion.5), channel_id=1, source_target_pairs={{0,2},{2,0},{4,6},{6,4},{8,10},{10,8},{12,14},{14,12},{1,3},{3,1},... | collective-permute-start | bytes 884744 | tf_op jit(solution)/shard_map/ppermute | solution.py:41
  100.1 11.0 %collective-permute-start.12 = (f32[9,32,256]{2,1,0:T(8,128)S(1)}, f32[9,32,256]{2,1,0:T(8,128)S(1)}, u32[]{:S(2)}, u32[]{:S(2)}) collective-permute-start(f32[9,32,256]{2,1,0:T(8,128)S(1)} %constant_dynamic-slice_fusion.8), channel_id=1, source_target_pairs={{0,64},{64,0},{128,192},{192,128},{1,65},{65,1},{129,193},{193,129... | collective-permute-start | bytes 884744 | tf_op jit(solution)/shard_map/ppermute | solution.py:41
  103.8 8.8 %collective-permute-start.9 = (f32[9,32,256]{2,1,0:T(8,128)S(1)}, f32[9,32,256]{2,1,0:T(8,128)S(1)}, u32[]{:S(2)}, u32[]{:S(2)}) collective-permute-start(f32[9,32,256]{2,1,0:T(8,128)S(1)} %constant_dynamic-slice_fusion.11), channel_id=1, source_target_pairs={{0,16},{16,0},{32,48},{48,32},{1,17},{17,1},{33,49},{49,33},{2,18}... | collective-permute-start | bytes 884744 | tf_op jit(solution)/shard_map/ppermute | solution.py:41
  110.1 5.7 %collective-permute-start.16 = (f32[9,16,256]{2,1,0:T(8,128)S(1)}, f32[9,16,256]{2,1,0:T(8,128)S(1)}, u32[]{:S(2)}, u32[]{:S(2)}) collective-permute-start(f32[9,16,256]{2,1,0:T(8,128)S(1)} %constant_dynamic-slice_fusion.4), channel_id=1, source_target_pairs={{0,16},{16,0},{32,48},{48,32},{1,17},{17,1},{33,49},{49,33},{2,18}... | collective-permute-start | bytes 442376 | tf_op jit(solution)/shard_map/ppermute | solution.py:41
  111.2 4.6 %collective-permute-start.13 = (f32[9,16,256]{2,1,0:T(8,128)S(1)}, f32[9,16,256]{2,1,0:T(8,128)S(1)}, u32[]{:S(2)}, u32[]{:S(2)}) collective-permute-start(f32[9,16,256]{2,1,0:T(8,128)S(1)} %constant_dynamic-slice_fusion.7), channel_id=1, source_target_pairs={{0,2},{2,0},{4,6},{6,4},{8,10},{10,8},{12,14},{14,12},{1,3},{3,1},... | collective-permute-start | bytes 442376 | tf_op jit(solution)/shard_map/ppermute | solution.py:41
  112.7 4.4 %collective-permute-start.10 = (f32[9,16,256]{2,1,0:T(8,128)S(1)}, f32[9,16,256]{2,1,0:T(8,128)S(1)}, u32[]{:S(2)}, u32[]{:S(2)}) collective-permute-start(f32[9,16,256]{2,1,0:T(8,128)S(1)} %constant_dynamic-slice_fusion.10), channel_id=1, source_target_pairs={{0,64},{64,0},{128,192},{192,128},{1,65},{65,1},{129,193},{193,129... | collective-permute-start | bytes 442376 | tf_op jit(solution)/shard_map/ppermute | solution.py:41
  117.1 9.3 %copy-start.5 = (f32[2,8,64,256]{3,2,1,0:T(8,128)S(1)}, f32[2,8,64,256]{3,2,1,0:T(8,128)}, u32[]{:S(2)}) copy-start(f32[2,8,64,256]{3,2,1,0:T(8,128)} %fusion.4) | copy-start | bytes 3145732
  117.1 6.4 %collective-permute-start.17 = (f32[3,9,8,256]{3,2,1,0:T(8,128)S(1)}, f32[3,9,8,256]{3,2,1,0:T(8,128)S(1)}, u32[]{:S(2)}, u32[]{:S(2)}) collective-permute-start(f32[3,9,8,256]{3,2,1,0:T(8,128)S(1)} %constant_dynamic-slice_fusion.3), channel_id=1, source_target_pairs={{0,32},{16,48},{32,0},{48,16},{1,33},{17,49},{33,1},{49,17},{2,34}... | collective-permute-start | bytes 663560 | tf_op jit(solution)/shard_map/ppermute | solution.py:41
  123.6 5.2 %collective-permute-start.18 = (f32[3,9,4,256]{3,2,1,0:T(4,128)S(1)}, f32[3,9,4,256]{3,2,1,0:T(4,128)S(1)}, u32[]{:S(2)}, u32[]{:S(2)}) collective-permute-start(f32[3,9,4,256]{3,2,1,0:T(4,128)S(1)} %constant_dynamic-slice_fusion.2), channel_id=1, source_target_pairs={{0,128},{64,192},{128,0},{192,64},{1,129},{65,193},{129,1},{193,65... | collective-permute-start | bytes 331784 | tf_op jit(solution)/shard_map/ppermute | solution.py:41
  128.8 5.5 %collective-permute-start.19 = (f32[3,9,2,256]{3,2,1,0:T(2,128)S(1)}, f32[3,9,2,256]{3,2,1,0:T(2,128)S(1)}, u32[]{:S(2)}, u32[]{:S(2)}) collective-permute-start(f32[3,9,2,256]{3,2,1,0:T(2,128)S(1)} %constant_dynamic-slice_fusion.1), channel_id=1, source_target_pairs={{0,4},{2,6},{4,0},{6,2},{8,12},{10,14},{12,8},{14,10},{1,5},{3,7},... | collective-permute-start | bytes 165896 | tf_op jit(solution)/shard_map/ppermute | solution.py:41
  134.5 6.7 %collective-permute-start.20 = (f32[3,9,1,256]{3,2,1,0:T(1,128)S(1)}, f32[3,9,1,256]{3,2,1,0:T(1,128)S(1)}, u32[]{:S(2)}, u32[]{:S(2)}) collective-permute-start(f32[3,9,1,256]{3,2,1,0:T(1,128)S(1)} %constant_dynamic-slice_fusion), channel_id=1, source_target_pairs={{0,8},{2,10},{4,12},{6,14},{8,0},{10,2},{12,4},{14,6},{1,9},{3,11}... | collective-permute-start | bytes 82952 | tf_op jit(solution)/shard_map/ppermute | solution.py:41
  141.2 28.0 %collective-permute-start.23 = (f32[9,1,256]{2,1,0:T(1,128)S(1)}, f32[9,1,256]{2,1,0:T(1,128)S(1)}, u32[]{:S(2)}, u32[]{:S(2)}) collective-permute-start(f32[9,1,256]{2,1,0:T(1,128)S(1)} %get-tuple-element.26), channel_id=1, source_target_pairs={{0,0},{1,128},{2,32},{3,160},{4,2},{5,130},{6,34},{7,162},{8,1},{9... | collective-permute-start | bytes 27656 | tf_op jit(solution)/shard_map/ppermute | solution.py:96
  153.4 15.9 %collective-permute-start.22 = (f32[9,1,256]{2,0,1:T(8,128)S(1)}, f32[9,1,256]{2,0,1:T(8,128)S(1)}, u32[]{:S(2)}, u32[]{:S(2)}) collective-permute-start(f32[9,1,256]{2,0,1:T(8,128)S(1)} %bitcast.389), channel_id=1, source_target_pairs={{0,0},{1,128},{2,16},{3,144},{4,2},{5,130},{6,18},{7,146},{8,1},{9... | collective-permute-start | bytes 27656 | tf_op jit(solution)/shard_map/ppermute | solution.py:96
  165.9 9.6 %collective-permute-start.21 = (f32[9,1,256]{2,0,1:T(8,128)S(1)}, f32[9,1,256]{2,0,1:T(8,128)S(1)}, u32[]{:S(2)}, u32[]{:S(2)}) collective-permute-start(f32[9,1,256]{2,0,1:T(8,128)S(1)} %bitcast.390), channel_id=1, source_target_pairs={{0,0},{1,128},{2,64},{3,192},{4,2},{5,130},{6,66},{7,194},{8,1},{9... | collective-permute-start | bytes 27656 | tf_op jit(solution)/shard_map/ppermute | solution.py:96

commit v4 on v1

--- a/solution.py
+++ b/solution.py
@@ -112,16 +112,29 @@
     rows = video.shape[2]
     cols = video.shape[3]
     chans = video.shape[4]
-    past = passed_along(lax.slice_in_dim(video, frames - 2, None, axis=1), "group", 1)
-    vwide = row_halo(jnp.concatenate([past, video], axis=1), "space", 2)
+    assert lax.axis_size("space") == 2
+    swap = [(0, 1), (1, 0)]
+    where_s = lax.axis_index("space")
+    tail = lax.slice_in_dim(video, frames - 2, None, axis=1)
+    past = passed_along(tail, "group", 1)
+    other_now = lax.ppermute(video, "space", swap)
+    count = lax.axis_size("group")
+    diagonal = [(g * 2 + c, (g + 1) * 2 + 1 - c) for g in range(count - 1) for c in range(2)]
+    other_past = lax.ppermute(tail, ("group", "space"), diagonal)
+    mine = jnp.concatenate([past, video], axis=1)
+    theirs = jnp.concatenate([other_past, other_now], axis=1)
+    full = jnp.where(
+        where_s == 0,
+        jnp.concatenate([mine, theirs], axis=2),
+        jnp.concatenate([theirs, mine], axis=2),
+    )
     pos_wide, same_fwd, same_bwd = clip_tables(clip_id, frames)
     omega = 0.37 * (jnp.arange(chans) % 8 + 1).astype(jnp.float32)
     embed = jnp.sin(pos_wide.astype(jnp.float32)[:, :, None] * omega)
-    shifted = (vwide.astype(jnp.float32) + embed[:, :, None, None, :]).astype(jnp.bfloat16)
-    row = jnp.arange(rows + 2)
-    where_s = lax.axis_index("space")
-    inside = ((row > 0) | (where_s > 0)) & ((row < rows + 1) | (where_s < lax.axis_size("space") - 1))
-    shifted = jnp.where(inside[None, None, :, None, None], shifted, jnp.zeros_like(shifted))
+    whole = (full.astype(jnp.float32) + embed[:, :, None, None, :]).astype(jnp.bfloat16)
+    whole = jnp.pad(whole, ((0, 0), (0, 0), (1, 1), (0, 0), (0, 0)))
+    shifted = lax.dynamic_slice_in_dim(whole, where_s * rows, rows + 2, axis=2)
+    shifted_other = lax.dynamic_slice_in_dim(whole, (1 - where_s) * rows, rows + 2, axis=2)
     maskf = same_fwd.astype(jnp.float32)
     widened = jnp.pad(shifted, ((0, 0), (0, 0), (0, 0), (1, 1), (0, 0)))
     stacked = jnp.concatenate([widened[:, :, :, b : b + cols] for b in range(3)], axis=4)
@@ -142,9 +155,8 @@
     )
     ahead = passed_along(lax.slice_in_dim(delta, 0, 2, axis=1), "group", -1)
     gwide = row_halo(jnp.concatenate([delta, ahead], axis=1), "space", 2)
-    swap = [(0, 1), (1, 0)]
     half = chans // 2
-    both = jnp.concatenate([shifted, lax.ppermute(shifted, "space", swap)], axis=0)
+    both = jnp.concatenate([shifted, shifted_other], axis=0)
     both = lax.dynamic_slice_in_dim(both, lax.axis_index("space") * half, half, axis=4)
     both = jnp.pad(both, ((0, 0), (0, 0), (0, 0), (1, 1), (0, 0)))
     bstack = jnp.concatenate([both[:, :, :, b : b + cols] for b in range(3)], axis=4)

time: 174 us -> 171 us (0.983)
  blocking collectives: 14.6 us -> 23.7 us
  waiting for transfers between devices: 35.9 us -> 26.9 us
  matrix products: 19.4 us -> 17.3 us
    unnamed x1, blocking collectives: 14.6 us -> 23.7 us
    ppermute x13, waiting for transfers between devices: 24.5 us -> 20.7 us  [halve(): return keep + lax.ppermute(give, axis, pairs)]
    ppermute x1 -> x2, starting transfers between devices: 0.1 us -> 3.78 us  [the longest x1 3.68 us: local(): other_past = lax.ppermute(tail, ('group', 'space'), diagonal)]
    ppermute x2 -> x1, starting transfers between devices: 8.06 us -> 4.77 us  [row_halo(): high = lax.ppermute(lax.slice_in_dim(block, 0, 1, axis=dim), axis, backward)]
    ppermute x2, waiting for transfers between devices: 3.24 us -> 0.01 us  [passed_along(): return lax.ppermute(value, axis, pairs)]
    ppermute x1, starting transfers between devices: 0.43 us -> 3.55 us  [local(): lax.ppermute(delta, 'space', swap)]
    ppermute x2 -> x1, waiting for transfers between devices: 1.9 us -> 0.01 us  [row_halo(): lax.ppermute(lax.slice_in_dim(block, block.shape[dim] - 1, None, axis=dim...]
    reshape x1, local copies, waits for them, and re-layouts: 6.03 us -> 4.27 us  [local(): weight.reshape(3, 3, 3, chans, chans).transpose(0, 1, 2, 4, 3)]
  transfers between devices with their start and end apart: 24 -> 23, of which waited for: 13 -> 11; matrix products, arithmetic and copies ran while one was open for 15% -> 19% of each run, Pallas kernels for 0% -> 0%
where the time goes in v4:
time: 171 us; the launch traced here: 169 us
  starting transfers between devices  73 us (43%)
  waiting for transfers between devices  26.9 us (16%)
  blocking collectives  23.7 us (14%)
  local copies, waits for them, and re-layouts  18.9 us (11%)
  matrix products  17.3 us (10%)
  other arithmetic  7.18 us (4%)
  between operations  2.2 us (1%)
    ppermute x3, starting transfers between devices, reduce_weight_grad(): parts.append(lax.ppermute(joined[n], names, pairs).reshape(per, outs))  26.2 us
    ppermute x13, starting transfers between devices, halve(): return keep + lax.ppermute(give, axis, pairs)  25.6 us
    unnamed x1, blocking collectives  23.7 us
    ppermute x13, waiting for transfers between devices, halve(): return keep + lax.ppermute(give, axis, pairs)  20.7 us
    ppermute x2, starting transfers between devices, passed_along(): return lax.ppermute(value, axis, pairs)  7.8 us
    unnamed x20, local copies, waits for them, and re-layouts  6.27 us
    ppermute x3, waiting for transfers between devices, reduce_weight_grad(): parts.append(lax.ppermute(joined[n], names, pairs).reshape(per, outs))  6.23 us
    dot_general x9, matrix products, local(): jnp.einsum('sfhwk,kc->sfhwc', block, back[k, a], preferred_element_type=j...  6.15 us
  transfers between devices with their start and end apart: 23, of which 11 were waited for; matrix products, arithmetic and copies ran while one was open for 19% of the time, Pallas kernels for 0%

profile of v4, /device:TPU:25, one launch (start us, length us, event | category | flops | bytes accessed | tf_op | source)
XLA Modules:
  0.0 169.2 jit_solution(12621837426245575524)
XLA Ops:
  0.6 3.7 %collective-permute-start.1 = (bf16[1,2,8,64,256]{4,3,2,1,0:T(8,128)(2,1)}, bf16[1,2,8,64,256]{4,3,2,1,0:T(8,128)(2,1)}, u32[]{:S(2)}, u32[]{:S(2)}) collective-permute-start(bf16[1,2,8,64,256]{4,3,2,1,0:T(8,128)(2,1)} %param.4), channel_id=1, source_target_pairs={{0,17},{1,16},{16,33},{17,32},{32,49},{33,48},{48,65},{49,64},{64,... | collective-permute-start | bytes 1572872 | tf_op jit(solution)/shard_map/ppermute | solution.py:123
  4.4 3.1 %collective-permute-start = (bf16[1,2,8,64,256]{4,3,2,1,0:T(8,128)(2,1)}, bf16[1,2,8,64,256]{4,3,2,1,0:T(8,128)(2,1)}, u32[]{:S(2)}, u32[]{:S(2)}) collective-permute-start(bf16[1,2,8,64,256]{4,3,2,1,0:T(8,128)(2,1)} %param.4), channel_id=1, source_target_pairs={{0,16},{16,32},{32,48},{48,64},{64,80},{80,96},{96,112},{112,128},... | collective-permute-start | bytes 1572872 | tf_op jit(solution)/shard_map/ppermute | solution.py:10
  7.6 1.3 dynamic-slice
  9.5 0.8 bitcast_dynamic-update-slice_fusion
  10.3 23.7 %all-reduce.7 = s32[32]{0:T(128)S(1)} all-reduce(s32[32]{0:T(128)S(1)} %bitcast_dynamic-update-slice_fusion), channel_id=1, replica_groups=mesh['group'=16,'dp'=8,'space'=2] {'group'}, use_global_device_ids=true, to_apply=%add.7 | all-reduce | flops 32 | bytes 256
  34.7 0.6 fusion.106
  35.3 4.3 %copy.34 = bf16[3,3,3,256,256]{3,4,2,1,0:T(8,128)(2,1)S(1)} copy(bf16[3,3,3,256,256]{4,3,2,1,0:T(8,128)(2,1)} %bitcast.369) | data formatting | bytes 7077888 | tf_op jit(solution)/shard_map/reshape | solution.py:177
  39.8 1.1 constant_dynamic-update-slice_fusion.1
  40.9 1.1 constant_dynamic-update-slice_fusion
  42.0 1.1 constant_dynamic-update-slice_fusion.3
  43.1 1.1 constant_dynamic-update-slice_fusion.2
  45.0 0.9 pad_slice_fusion.3
  46.3 1.6 copy-done
  51.5 0.6 fusion.50
  52.1 0.6 fusion.47
  53.1 1.0 fusion.92
  54.1 4.7 %collective-permute-start.3 = (bf16[1,2,8,64,256]{4,3,2,1,0:T(8,128)(2,1)S(1)}, bf16[1,2,8,64,256]{4,3,2,1,0:T(8,128)(2,1)S(1)}, u32[]{:S(2)}, u32[]{:S(2)}) collective-permute-start(bf16[1,2,8,64,256]{4,3,2,1,0:T(8,128)(2,1)S(1)} %get-tuple-element.39), channel_id=1, source_target_pairs={{16,0},{32,16},{48,32},{64,48},{80,64},{96,80},{112,96},{128,112},... | collective-permute-start | bytes 1572872 | tf_op jit(solution)/shard_map/ppermute | solution.py:10
  58.8 3.6 %collective-permute-start.6 = (bf16[1,2,8,64,256]{4,3,2,1,0:T(8,128)(2,1)S(1)}, bf16[1,2,8,64,256]{4,3,2,1,0:T(8,128)(2,1)S(1)}, u32[]{:S(2)}, u32[]{:S(2)}) collective-permute-start(bf16[1,2,8,64,256]{4,3,2,1,0:T(8,128)(2,1)S(1)} %get-tuple-element.39), channel_id=1, source_target_pairs={{0,1},{1,0},{2,3},{3,2},{4,5},{5,4},{6,7},{7,6},{8,9},{9,8},{10,11... | collective-permute-start | bytes 1572872 | tf_op jit(solution)/shard_map/ppermute | solution.py:163
  62.6 1.3 pad_slice_fusion.1
  63.9 0.7 pad_maximum_fusion.2
  64.6 2.3 %fusion.114 = (bf16[2,2,8,64,384]{4,3,2,1,0:T(8,128)(2,1)S(1)}, bf16[2,2,8,64,384]{4,3,2,1,0:T(8,128)(2,1)S(1)}, bf16[2,2,8,64,384]{4,3,2,1,0:T(8,128)(2,1)S(1)}...) fusion(bf16[2,4,10,64,384]{4,3,2,1,0:T(8,128)(2,1)S(1)} %pad_ma, ...), kind=kLoop, calls=%fused_computation.218 | loop fusion | bytes 28311552 | tf_op jit(solution)/shard_map/slice | solution.py:168
  67.0 1.1 fusion.102
  68.1 4.8 %collective-permute-start.5 = (bf16[1,4,1,64,256]{4,3,2,1,0:T(8,128)(2,1)S(1)}, bf16[1,4,1,64,256]{4,3,2,1,0:T(8,128)(2,1)S(1)}, u32[]{:S(2)}, u32[]{:S(2)}) collective-permute-start(bf16[1,4,1,64,256]{4,3,2,1,0:T(8,128)(2,1)S(1)} %get-tuple-element.24), channel_id=1, source_target_pairs={{1,0},{3,2},{5,4},{7,6},{9,8},{11,10},{13,12},{15,14},{17,16},{19,... | collective-permute-start | bytes 393224 | tf_op jit(solution)/shard_map/ppermute | solution.py:20
  72.8 1.3 collective-permute-start.4
  74.5 0.6 fusion.89
  75.1 0.6 fusion.86
  75.7 0.6 fusion.83
  76.5 1.4 collective-permute-start.13
  77.9 0.6 fusion.80
  78.5 0.6 fusion.77
  79.1 0.6 fusion.74
  79.8 0.7 collective-permute-start.10
  80.6 0.6 fusion.71
  81.2 0.6 fusion.68
  81.8 0.6 fusion.65
  82.5 1.9 %collective-permute-start.7 = (f32[9,64,256]{2,1,0:T(8,128)S(1)}, f32[9,64,256]{2,1,0:T(8,128)S(1)}, u32[]{:S(2)}, u32[]{:S(2)}) collective-permute-start(f32[9,64,256]{2,1,0:T(8,128)S(1)} %constant_dynamic-slice_fusion.12), channel_id=1, source_target_pairs={{0,2},{2,0},{4,6},{6,4},{8,10},{10,8},{12,14},{14,12},{1,3},{3,1},... | collective-permute-start | bytes 1769480 | tf_op jit(solution)/shard_map/ppermute | solution.py:30
  84.5 0.8 select_maximum_fusion
  85.3 0.9 fusion.115
  87.8 0.6 fusion.61
  89.1 1.2 collective-permute-done.13
  90.4 1.7 %collective-permute-start.14 = (f32[9,32,256]{2,1,0:T(8,128)S(1)}, f32[9,32,256]{2,1,0:T(8,128)S(1)}, u32[]{:S(2)}, u32[]{:S(2)}) collective-permute-start(f32[9,32,256]{2,1,0:T(8,128)S(1)} %constant_dynamic-slice_fusion.5), channel_id=1, source_target_pairs={{0,2},{2,0},{4,6},{6,4},{8,10},{10,8},{12,14},{14,12},{1,3},{3,1},... | collective-permute-start | bytes 884744 | tf_op jit(solution)/shard_map/ppermute | solution.py:30
  92.1 1.3 collective-permute-done.10
  93.8 2.6 %collective-permute-done.7 = f32[9,64,256]{2,1,0:T(8,128)S(1)} collective-permute-done((f32[9,64,256]{2,1,0:T(8,128)S(1)}, f32[9,64,256]{2,1,0:T(8,128)S(1)}, u32[]{:S(2)}, u32[]{:S(2)}) %collective-permute-start.7) | collective-permute-done | bytes 589856 | tf_op jit(solution)/shard_map/ppermute | solution.py:30
  96.5 0.9 collective-permute-start.8
  97.5 5.3 %collective-permute-done.14 = f32[9,32,256]{2,1,0:T(8,128)S(1)} collective-permute-done((f32[9,32,256]{2,1,0:T(8,128)S(1)}, f32[9,32,256]{2,1,0:T(8,128)S(1)}, u32[]{:S(2)}, u32[]{:S(2)}) %collective-permute-start.14) | collective-permute-done | bytes 294944 | tf_op jit(solution)/shard_map/ppermute | solution.py:30
  102.8 0.9 collective-permute-start.15
  103.8 1.4 collective-permute-start.12
  105.5 3.3 %collective-permute-done.15 = f32[9,16,256]{2,1,0:T(8,128)S(1)} collective-permute-done((f32[9,16,256]{2,1,0:T(8,128)S(1)}, f32[9,16,256]{2,1,0:T(8,128)S(1)}, u32[]{:S(2)}, u32[]{:S(2)}) %collective-permute-start.15) | collective-permute-done | bytes 147488 | tf_op jit(solution)/shard_map/ppermute | solution.py:30
  108.8 0.8 collective-permute-done.9
  109.7 3.4 %collective-permute-start.16 = (f32[3,9,8,256]{3,2,1,0:T(8,128)S(1)}, f32[3,9,8,256]{3,2,1,0:T(8,128)S(1)}, u32[]{:S(2)}, u32[]{:S(2)}) collective-permute-start(f32[3,9,8,256]{3,2,1,0:T(8,128)S(1)} %constant_dynamic-slice_fusion.3), channel_id=1, source_target_pairs={{0,32},{16,48},{32,0},{48,16},{64,96},{80,112},{96,64},{112,80},{1... | collective-permute-start | bytes 663560 | tf_op jit(solution)/shard_map/ppermute | solution.py:30
  113.7 2.7 %collective-permute-done.16 = f32[3,9,8,256]{3,2,1,0:T(8,128)S(1)} collective-permute-done((f32[3,9,8,256]{3,2,1,0:T(8,128)S(1)}, f32[3,9,8,256]{3,2,1,0:T(8,128)S(1)}, u32[]{:S(2)}, u32[]{:S(2)}) %collective-permute-start.16) | collective-permute-done | bytes 221216 | tf_op jit(solution)/shard_map/ppermute | solution.py:30
  116.5 3.3 %collective-permute-start.17 = (f32[3,9,4,256]{3,2,1,0:T(4,128)S(1)}, f32[3,9,4,256]{3,2,1,0:T(4,128)S(1)}, u32[]{:S(2)}, u32[]{:S(2)}) collective-permute-start(f32[3,9,4,256]{3,2,1,0:T(4,128)S(1)} %constant_dynamic-slice_fusion.2), channel_id=1, source_target_pairs={{0,128},{16,144},{32,160},{48,176},{64,192},{80,208},{96,224},{112... | collective-permute-start | bytes 331784 | tf_op jit(solution)/shard_map/ppermute | solution.py:30
  119.8 0.6 fusion.58
  120.4 1.8 %collective-permute-done.17 = f32[3,9,4,256]{3,2,1,0:T(4,128)S(1)} collective-permute-done((f32[3,9,4,256]{3,2,1,0:T(4,128)S(1)}, f32[3,9,4,256]{3,2,1,0:T(4,128)S(1)}, u32[]{:S(2)}, u32[]{:S(2)}) %collective-permute-start.17) | collective-permute-done | bytes 110624 | tf_op jit(solution)/shard_map/ppermute | solution.py:30
  122.3 3.1 %collective-permute-start.18 = (f32[3,9,2,256]{3,2,1,0:T(2,128)S(1)}, f32[3,9,2,256]{3,2,1,0:T(2,128)S(1)}, u32[]{:S(2)}, u32[]{:S(2)}) collective-permute-start(f32[3,9,2,256]{3,2,1,0:T(2,128)S(1)} %constant_dynamic-slice_fusion.1), channel_id=1, source_target_pairs={{0,4},{2,6},{4,0},{6,2},{8,12},{10,14},{12,8},{14,10},{1,5},{3,7},... | collective-permute-start | bytes 165896 | tf_op jit(solution)/shard_map/ppermute | solution.py:30
  126.0 1.0 collective-permute-done.18
  127.0 6.4 %collective-permute-start.19 = (f32[3,9,1,256]{3,2,1,0:T(1,128)S(1)}, f32[3,9,1,256]{3,2,1,0:T(1,128)S(1)}, u32[]{:S(2)}, u32[]{:S(2)}) collective-permute-start(f32[3,9,1,256]{3,2,1,0:T(1,128)S(1)} %constant_dynamic-slice_fusion), channel_id=1, source_target_pairs={{0,8},{2,10},{4,12},{6,14},{8,0},{10,2},{12,4},{14,6},{1,9},{3,11}... | collective-permute-start | bytes 82952 | tf_op jit(solution)/shard_map/ppermute | solution.py:30
  134.0 0.7 collective-permute-done.19
  134.7 12.6 %collective-permute-start.22 = (f32[9,1,256]{2,1,0:T(1,128)S(1)}, f32[9,1,256]{2,1,0:T(1,128)S(1)}, u32[]{:S(2)}, u32[]{:S(2)}) collective-permute-start(f32[9,1,256]{2,1,0:T(1,128)S(1)} %get-tuple-element.26), channel_id=1, source_target_pairs={{0,0},{1,128},{2,32},{3,160},{4,2},{5,130},{6,34},{7,162},{8,1},{9... | collective-permute-start | bytes 27656 | tf_op jit(solution)/shard_map/ppermute | solution.py:86
  147.3 11.6 %collective-permute-start.21 = (f32[9,1,256]{2,0,1:T(8,128)S(1)}, f32[9,1,256]{2,0,1:T(8,128)S(1)}, u32[]{:S(2)}, u32[]{:S(2)}) collective-permute-start(f32[9,1,256]{2,0,1:T(8,128)S(1)} %bitcast.388), channel_id=1, source_target_pairs={{0,0},{1,128},{2,16},{3,144},{4,2},{5,130},{6,18},{7,146},{8,1},{9... | collective-permute-start | bytes 27656 | tf_op jit(solution)/shard_map/ppermute | solution.py:86
  159.0 1.9 %collective-permute-start.20 = (f32[9,1,256]{2,0,1:T(8,128)S(1)}, f32[9,1,256]{2,0,1:T(8,128)S(1)}, u32[]{:S(2)}, u32[]{:S(2)}) collective-permute-start(f32[9,1,256]{2,0,1:T(8,128)S(1)} %bitcast.389), channel_id=1, source_target_pairs={{0,0},{1,128},{2,64},{3,192},{4,2},{5,130},{6,66},{7,194},{8,1},{9... | collective-permute-start | bytes 27656 | tf_op jit(solution)/shard_map/ppermute | solution.py:86
  160.9 1.4 fusion.64
  162.3 6.2 %collective-permute-done.20 = f32[9,1,256]{2,0,1:T(8,128)S(1)} collective-permute-done((f32[9,1,256]{2,0,1:T(8,128)S(1)}, f32[9,1,256]{2,0,1:T(8,128)S(1)}, u32[]{:S(2)}, u32[]{:S(2)}) %collective-permute-start.20) | collective-permute-done | bytes 9248 | tf_op jit(solution)/shard_map/ppermute | solution.py:86
  168.6 0.6 pad_maximum_fusion.10
  (92 shorter events, 12.2 us)
Async XLA Ops:
  0.6 41.3 %collective-permute-start.1 = (bf16[1,2,8,64,256]{4,3,2,1,0:T(8,128)(2,1)}, bf16[1,2,8,64,256]{4,3,2,1,0:T(8,128)(2,1)}, u32[]{:S(2)}, u32[]{:S(2)}) collective-permute-start(bf16[1,2,8,64,256]{4,3,2,1,0:T(8,128)(2,1)} %param.4), channel_id=1, source_target_pairs={{0,17},{1,16},{16,33},{17,32},{32,49},{33,48},{48,65},{49,64},{64,... | collective-permute-start | bytes 1572872 | tf_op jit(solution)/shard_map/ppermute | solution.py:123
  4.3 38.7 %collective-permute-start.2 = (bf16[1,2,8,64,256]{4,3,2,1,0:T(8,128)(2,1)}, bf16[1,2,8,64,256]{4,3,2,1,0:T(8,128)(2,1)}, u32[]{:S(2)}, u32[]{:S(2)}) collective-permute-start(bf16[1,2,8,64,256]{4,3,2,1,0:T(8,128)(2,1)} %param.4), channel_id=1, source_target_pairs={{0,1},{1,0},{2,3},{3,2},{4,5},{5,4},{6,7},{7,6},{8,9},{9,8},{10,11... | collective-permute-start | bytes 1572872 | tf_op jit(solution)/shard_map/ppermute | solution.py:120
  4.4 35.3 %collective-permute-start = (bf16[1,2,8,64,256]{4,3,2,1,0:T(8,128)(2,1)}, bf16[1,2,8,64,256]{4,3,2,1,0:T(8,128)(2,1)}, u32[]{:S(2)}, u32[]{:S(2)}) collective-permute-start(bf16[1,2,8,64,256]{4,3,2,1,0:T(8,128)(2,1)} %param.4), channel_id=1, source_target_pairs={{0,16},{16,32},{32,48},{48,64},{64,80},{80,96},{96,112},{112,128},... | collective-permute-start | bytes 1572872 | tf_op jit(solution)/shard_map/ppermute | solution.py:10
  45.9 2.0 %copy-start = (bf16[6912,256]{1,0:T(8,128)(2,1)S(1)}, bf16[6912,256]{1,0:T(8,128)(2,1)}, u32[]{:S(2)}) copy-start(bf16[6912,256]{1,0:T(8,128)(2,1)} %param.6) | copy-start | bytes 10616836
  52.1 1.0 copy-start.5
  54.1 13.9 %collective-permute-start.3 = (bf16[1,2,8,64,256]{4,3,2,1,0:T(8,128)(2,1)S(1)}, bf16[1,2,8,64,256]{4,3,2,1,0:T(8,128)(2,1)S(1)}, u32[]{:S(2)}, u32[]{:S(2)}) collective-permute-start(bf16[1,2,8,64,256]{4,3,2,1,0:T(8,128)(2,1)S(1)} %get-tuple-element.39), channel_id=1, source_target_pairs={{16,0},{32,16},{48,32},{64,48},{80,64},{96,80},{112,96},{128,112},... | collective-permute-start | bytes 1572872 | tf_op jit(solution)/shard_map/ppermute | solution.py:10
  58.8 15.4 %collective-permute-start.6 = (bf16[1,2,8,64,256]{4,3,2,1,0:T(8,128)(2,1)S(1)}, bf16[1,2,8,64,256]{4,3,2,1,0:T(8,128)(2,1)S(1)}, u32[]{:S(2)}, u32[]{:S(2)}) collective-permute-start(bf16[1,2,8,64,256]{4,3,2,1,0:T(8,128)(2,1)S(1)} %get-tuple-element.39), channel_id=1, source_target_pairs={{0,1},{1,0},{2,3},{3,2},{4,5},{5,4},{6,7},{7,6},{8,9},{9,8},{10,11... | collective-permute-start | bytes 1572872 | tf_op jit(solution)/shard_map/ppermute | solution.py:163
  66.9 7.2 %copy-start.2 = (bf16[2]{0:T(256)(128)(2,1)S(1)}, bf16[2]{0:T(256)(128)(2,1)}, u32[]{:S(2)}) copy-start(bf16[2]{0:T(256)(128)(2,1)} %get-tuple-element.31) | copy-start | bytes 16
  66.9 7.2 %copy-start.3 = (bf16[2]{0:T(256)(128)(2,1)S(1)}, bf16[2]{0:T(256)(128)(2,1)}, u32[]{:S(2)}) copy-start(bf16[2]{0:T(256)(128)(2,1)} %get-tuple-element.33) | copy-start | bytes 16
  67.0 7.2 %copy-start.4 = (bf16[2]{0:T(256)(128)(2,1)S(1)}, bf16[2]{0:T(256)(128)(2,1)}, u32[]{:S(2)}) copy-start(bf16[2]{0:T(256)(128)(2,1)} %get-tuple-element.34) | copy-start | bytes 16
  68.1 16.4 %collective-permute-start.5 = (bf16[1,4,1,64,256]{4,3,2,1,0:T(8,128)(2,1)S(1)}, bf16[1,4,1,64,256]{4,3,2,1,0:T(8,128)(2,1)S(1)}, u32[]{:S(2)}, u32[]{:S(2)}) collective-permute-start(bf16[1,4,1,64,256]{4,3,2,1,0:T(8,128)(2,1)S(1)} %get-tuple-element.24), channel_id=1, source_target_pairs={{1,0},{3,2},{5,4},{7,6},{9,8},{11,10},{13,12},{15,14},{17,16},{19,... | collective-permute-start | bytes 393224 | tf_op jit(solution)/shard_map/ppermute | solution.py:20
  72.8 11.6 %collective-permute-start.4 = (bf16[1,4,1,64,256]{4,3,2,1,0:T(8,128)(2,1)S(1)}, bf16[1,4,1,64,256]{4,3,2,1,0:T(8,128)(2,1)S(1)}, u32[]{:S(2)}, u32[]{:S(2)}) collective-permute-start(bf16[1,4,1,64,256]{4,3,2,1,0:T(8,128)(2,1)S(1)} %get-tuple-element.23), channel_id=1, source_target_pairs={{0,1},{2,3},{4,5},{6,7},{8,9},{10,11},{12,13},{14,15},{16,17},{18,... | collective-permute-start | bytes 393224 | tf_op jit(solution)/shard_map/ppermute | solution.py:17
  76.5 13.8 %collective-permute-start.13 = (f32[9,64,256]{2,1,0:T(8,128)S(1)}, f32[9,64,256]{2,1,0:T(8,128)S(1)}, u32[]{:S(2)}, u32[]{:S(2)}) collective-permute-start(f32[9,64,256]{2,1,0:T(8,128)S(1)} %constant_dynamic-slice_fusion.6), channel_id=1, source_target_pairs={{0,64},{16,80},{32,96},{48,112},{64,0},{80,16},{96,32},{112,48},{1... | collective-permute-start | bytes 1769480 | tf_op jit(solution)/shard_map/ppermute | solution.py:30
  79.8 13.6 %collective-permute-start.10 = (f32[9,64,256]{2,1,0:T(8,128)S(1)}, f32[9,64,256]{2,1,0:T(8,128)S(1)}, u32[]{:S(2)}, u32[]{:S(2)}) collective-permute-start(f32[9,64,256]{2,1,0:T(8,128)S(1)} %constant_dynamic-slice_fusion.9), channel_id=1, source_target_pairs={{0,16},{16,0},{32,48},{48,32},{64,80},{80,64},{96,112},{112,96},{1... | collective-permute-start | bytes 1769480 | tf_op jit(solution)/shard_map/ppermute | solution.py:30
  82.5 13.9 %collective-permute-start.7 = (f32[9,64,256]{2,1,0:T(8,128)S(1)}, f32[9,64,256]{2,1,0:T(8,128)S(1)}, u32[]{:S(2)}, u32[]{:S(2)}) collective-permute-start(f32[9,64,256]{2,1,0:T(8,128)S(1)} %constant_dynamic-slice_fusion.12), channel_id=1, source_target_pairs={{0,2},{2,0},{4,6},{6,4},{8,10},{10,8},{12,14},{14,12},{1,3},{3,1},... | collective-permute-start | bytes 1769480 | tf_op jit(solution)/shard_map/ppermute | solution.py:30
  87.2 0.6 copy-start.1
  90.4 12.3 %collective-permute-start.14 = (f32[9,32,256]{2,1,0:T(8,128)S(1)}, f32[9,32,256]{2,1,0:T(8,128)S(1)}, u32[]{:S(2)}, u32[]{:S(2)}) collective-permute-start(f32[9,32,256]{2,1,0:T(8,128)S(1)} %constant_dynamic-slice_fusion.5), channel_id=1, source_target_pairs={{0,2},{2,0},{4,6},{6,4},{8,10},{10,8},{12,14},{14,12},{1,3},{3,1},... | collective-permute-start | bytes 884744 | tf_op jit(solution)/shard_map/ppermute | solution.py:30
  93.5 10.2 %collective-permute-start.11 = (f32[9,32,256]{2,1,0:T(8,128)S(1)}, f32[9,32,256]{2,1,0:T(8,128)S(1)}, u32[]{:S(2)}, u32[]{:S(2)}) collective-permute-start(f32[9,32,256]{2,1,0:T(8,128)S(1)} %constant_dynamic-slice_fusion.8), channel_id=1, source_target_pairs={{0,64},{16,80},{32,96},{48,112},{64,0},{80,16},{96,32},{112,48},{1... | collective-permute-start | bytes 884744 | tf_op jit(solution)/shard_map/ppermute | solution.py:30
  96.5 8.7 %collective-permute-start.8 = (f32[9,32,256]{2,1,0:T(8,128)S(1)}, f32[9,32,256]{2,1,0:T(8,128)S(1)}, u32[]{:S(2)}, u32[]{:S(2)}) collective-permute-start(f32[9,32,256]{2,1,0:T(8,128)S(1)} %constant_dynamic-slice_fusion.11), channel_id=1, source_target_pairs={{0,16},{16,0},{32,48},{48,32},{64,80},{80,64},{96,112},{112,96},{1... | collective-permute-start | bytes 884744 | tf_op jit(solution)/shard_map/ppermute | solution.py:30
  102.8 6.0 %collective-permute-start.15 = (f32[9,16,256]{2,1,0:T(8,128)S(1)}, f32[9,16,256]{2,1,0:T(8,128)S(1)}, u32[]{:S(2)}, u32[]{:S(2)}) collective-permute-start(f32[9,16,256]{2,1,0:T(8,128)S(1)} %constant_dynamic-slice_fusion.4), channel_id=1, source_target_pairs={{0,16},{16,0},{32,48},{48,32},{64,80},{80,64},{96,112},{112,96},{1... | collective-permute-start | bytes 442376 | tf_op jit(solution)/shard_map/ppermute | solution.py:30
  103.8 5.0 %collective-permute-start.12 = (f32[9,16,256]{2,1,0:T(8,128)S(1)}, f32[9,16,256]{2,1,0:T(8,128)S(1)}, u32[]{:S(2)}, u32[]{:S(2)}) collective-permute-start(f32[9,16,256]{2,1,0:T(8,128)S(1)} %constant_dynamic-slice_fusion.7), channel_id=1, source_target_pairs={{0,2},{2,0},{4,6},{6,4},{8,10},{10,8},{12,14},{14,12},{1,3},{3,1},... | collective-permute-start | bytes 442376 | tf_op jit(solution)/shard_map/ppermute | solution.py:30
  105.3 4.4 %collective-permute-start.9 = (f32[9,16,256]{2,1,0:T(8,128)S(1)}, f32[9,16,256]{2,1,0:T(8,128)S(1)}, u32[]{:S(2)}, u32[]{:S(2)}) collective-permute-start(f32[9,16,256]{2,1,0:T(8,128)S(1)} %constant_dynamic-slice_fusion.10), channel_id=1, source_target_pairs={{0,64},{16,80},{32,96},{48,112},{64,0},{80,16},{96,32},{112,48},{1... | collective-permute-start | bytes 442376 | tf_op jit(solution)/shard_map/ppermute | solution.py:30
  109.7 6.7 %collective-permute-start.16 = (f32[3,9,8,256]{3,2,1,0:T(8,128)S(1)}, f32[3,9,8,256]{3,2,1,0:T(8,128)S(1)}, u32[]{:S(2)}, u32[]{:S(2)}) collective-permute-start(f32[3,9,8,256]{3,2,1,0:T(8,128)S(1)} %constant_dynamic-slice_fusion.3), channel_id=1, source_target_pairs={{0,32},{16,48},{32,0},{48,16},{64,96},{80,112},{96,64},{112,80},{1... | collective-permute-start | bytes 663560 | tf_op jit(solution)/shard_map/ppermute | solution.py:30
  116.5 5.7 %collective-permute-start.17 = (f32[3,9,4,256]{3,2,1,0:T(4,128)S(1)}, f32[3,9,4,256]{3,2,1,0:T(4,128)S(1)}, u32[]{:S(2)}, u32[]{:S(2)}) collective-permute-start(f32[3,9,4,256]{3,2,1,0:T(4,128)S(1)} %constant_dynamic-slice_fusion.2), channel_id=1, source_target_pairs={{0,128},{16,144},{32,160},{48,176},{64,192},{80,208},{96,224},{112... | collective-permute-start | bytes 331784 | tf_op jit(solution)/shard_map/ppermute | solution.py:30
  122.3 4.6 %collective-permute-start.18 = (f32[3,9,2,256]{3,2,1,0:T(2,128)S(1)}, f32[3,9,2,256]{3,2,1,0:T(2,128)S(1)}, u32[]{:S(2)}, u32[]{:S(2)}) collective-permute-start(f32[3,9,2,256]{3,2,1,0:T(2,128)S(1)} %constant_dynamic-slice_fusion.1), channel_id=1, source_target_pairs={{0,4},{2,6},{4,0},{6,2},{8,12},{10,14},{12,8},{14,10},{1,5},{3,7},... | collective-permute-start | bytes 165896 | tf_op jit(solution)/shard_map/ppermute | solution.py:30
  127.0 7.6 %collective-permute-start.19 = (f32[3,9,1,256]{3,2,1,0:T(1,128)S(1)}, f32[3,9,1,256]{3,2,1,0:T(1,128)S(1)}, u32[]{:S(2)}, u32[]{:S(2)}) collective-permute-start(f32[3,9,1,256]{3,2,1,0:T(1,128)S(1)} %constant_dynamic-slice_fusion), channel_id=1, source_target_pairs={{0,8},{2,10},{4,12},{6,14},{8,0},{10,2},{12,4},{14,6},{1,9},{3,11}... | collective-permute-start | bytes 82952 | tf_op jit(solution)/shard_map/ppermute | solution.py:30
  134.7 27.7 %collective-permute-start.22 = (f32[9,1,256]{2,1,0:T(1,128)S(1)}, f32[9,1,256]{2,1,0:T(1,128)S(1)}, u32[]{:S(2)}, u32[]{:S(2)}) collective-permute-start(f32[9,1,256]{2,1,0:T(1,128)S(1)} %get-tuple-element.26), channel_id=1, source_target_pairs={{0,0},{1,128},{2,32},{3,160},{4,2},{5,130},{6,34},{7,162},{8,1},{9... | collective-permute-start | bytes 27656 | tf_op jit(solution)/shard_map/ppermute | solution.py:86
  147.3 15.0 %collective-permute-start.21 = (f32[9,1,256]{2,0,1:T(8,128)S(1)}, f32[9,1,256]{2,0,1:T(8,128)S(1)}, u32[]{:S(2)}, u32[]{:S(2)}) collective-permute-start(f32[9,1,256]{2,0,1:T(8,128)S(1)} %bitcast.388), channel_id=1, source_target_pairs={{0,0},{1,128},{2,16},{3,144},{4,2},{5,130},{6,18},{7,146},{8,1},{9... | collective-permute-start | bytes 27656 | tf_op jit(solution)/shard_map/ppermute | solution.py:86
  159.0 9.6 %collective-permute-start.20 = (f32[9,1,256]{2,0,1:T(8,128)S(1)}, f32[9,1,256]{2,0,1:T(8,128)S(1)}, u32[]{:S(2)}, u32[]{:S(2)}) collective-permute-start(f32[9,1,256]{2,0,1:T(8,128)S(1)} %bitcast.389), channel_id=1, source_target_pairs={{0,0},{1,128},{2,64},{3,192},{4,2},{5,130},{6,66},{7,194},{8,1},{9... | collective-permute-start | bytes 27656 | tf_op jit(solution)/shard_map/ppermute | solution.py:86

commit v5 on v4

--- a/solution.py
+++ b/solution.py
@@ -88,7 +88,11 @@
 
 
 def clip_tables(clip_id, frames):
-    ids = lax.all_gather(clip_id, "group", axis=1, tiled=True)
+    lanes = lax.broadcasted_iota(jnp.int32, clip_id.shape + (128,), 2)
+    wide = (clip_id[:, :, None] * 1024 + lanes).astype(jnp.float32)
+    ids = lax.all_gather(wide, "group", axis=1, tiled=True)
+    ids = jnp.sum(ids, axis=2).astype(jnp.int32)
+    ids = (ids - 127 * 64) // (128 * 1024)
     total = ids.shape[1]
     index = jnp.arange(total, dtype=jnp.int32)[None, :]
     prev = jnp.concatenate([jnp.full_like(ids[:, :1], -1), ids[:, :-1]], axis=1)

time: 171 us -> 176 us (1.029)
  blocking collectives: 23.7 us -> 32.9 us
  starting transfers between devices: 73 us -> 70.3 us
  local copies, waits for them, and re-layouts: 18.9 us -> 16.9 us
    all_gather x0 -> x1, blocking collectives: none -> 32.9 us  [clip_tables(): ids = lax.all_gather(wide, 'group', axis=1, tiled=True)]
    unnamed x1 -> x0, blocking collectives: 23.7 us -> none
    ppermute x2, starting transfers between devices: 7.8 us -> 5.58 us  [passed_along(): return lax.ppermute(value, axis, pairs)]
    unnamed x20 -> x17, local copies, waits for them, and re-layouts: 6.27 us -> 4.24 us
  transfers between devices with their start and end apart: 23 -> 23, of which waited for: 11 -> 12; matrix products, arithmetic and copies ran while one was open for 19% -> 18% of each run, Pallas kernels for 0% -> 0%
where the time goes in v5:
time: 176 us; the launch traced here: 174 us
  starting transfers between devices  70.3 us (40%)
  blocking collectives  32.9 us (19%)
  waiting for transfers between devices  26.9 us (15%)
  matrix products  17.3 us (10%)
  local copies, waits for them, and re-layouts  16.9 us (10%)
  other arithmetic  8.25 us (5%)
    all_gather x1, blocking collectives, clip_tables(): ids = lax.all_gather(wide, 'group', axis=1, tiled=True)  32.9 us
    ppermute x3, starting transfers between devices, reduce_weight_grad(): parts.append(lax.ppermute(joined[n], names, pairs).reshape(per, outs))  25.7 us
    ppermute x13, starting transfers between devices, halve(): return keep + lax.ppermute(give, axis, pairs)  24 us
    ppermute x13, waiting for transfers between devices, halve(): return keep + lax.ppermute(give, axis, pairs)  20.6 us
    ppermute x3, waiting for transfers between devices, reduce_weight_grad(): parts.append(lax.ppermute(joined[n], names, pairs).reshape(per, outs))  6.23 us
    dot_general x9, matrix products, local(): jnp.einsum('sfhwk,kc->sfhwc', block, back[k, a], preferred_element_type=j...  6.15 us
    dot_general x9, matrix products, local(): jnp.einsum('sfhwk,kc->sfhwc', block, taps[k, a], preferred_element_type=j...  5.66 us
    ppermute x2, starting transfers between devices, passed_along(): return lax.ppermute(value, axis, pairs)  5.58 us
  transfers between devices with their start and end apart: 23, of which 12 were waited for; matrix products, arithmetic and copies ran while one was open for 18% of the time, Pallas kernels for 0%

profile of v5, /device:TPU:25, one launch (start us, length us, event | category | flops | bytes accessed | tf_op | source)
XLA Modules:
  0.0 174.1 jit_solution(9709006271430047698)
XLA Ops:
  0.6 3.7 %collective-permute-start.1 = (bf16[1,2,8,64,256]{4,3,2,1,0:T(8,128)(2,1)}, bf16[1,2,8,64,256]{4,3,2,1,0:T(8,128)(2,1)}, u32[]{:S(2)}, u32[]{:S(2)}) collective-permute-start(bf16[1,2,8,64,256]{4,3,2,1,0:T(8,128)(2,1)} %param.4), channel_id=1, source_target_pairs={{0,17},{1,16},{16,33},{17,32},{32,49},{33,48},{48,65},{49,64},{64,... | collective-permute-start | bytes 1572872 | tf_op jit(solution)/shard_map/ppermute | solution.py:127
  4.4 3.1 %collective-permute-start = (bf16[1,2,8,64,256]{4,3,2,1,0:T(8,128)(2,1)}, bf16[1,2,8,64,256]{4,3,2,1,0:T(8,128)(2,1)}, u32[]{:S(2)}, u32[]{:S(2)}) collective-permute-start(bf16[1,2,8,64,256]{4,3,2,1,0:T(8,128)(2,1)} %param.4), channel_id=1, source_target_pairs={{0,16},{16,32},{32,48},{48,64},{64,80},{80,96},{96,112},{112,128},... | collective-permute-start | bytes 1572872 | tf_op jit(solution)/shard_map/ppermute | solution.py:10
  7.6 0.7 multiply_bitcast_fusion
  8.3 32.9 %all_gather.3 = f32[1,32,128]{2,0,1:T(1,128)S(1)} all-gather(f32[1,2,128]{2,0,1:T(1,128)S(1)} %add_convert_fusion.1), channel_id=1, replica_groups=mesh['group'=16,'dp'=8,'space'=2] {'group'}, dimensions={1}, use_global_device_ids=true | all-gather | bytes 17408 | tf_op jit(solution)/shard_map/all_gather | solution.py:93
  42.3 0.6 fusion.106
  42.9 4.3 %copy.34 = bf16[3,3,3,256,256]{3,4,2,1,0:T(8,128)(2,1)S(1)} copy(bf16[3,3,3,256,256]{4,3,2,1,0:T(8,128)(2,1)} %bitcast.376) | data formatting | bytes 7077888 | tf_op jit(solution)/shard_map/reshape | solution.py:181
  47.4 1.1 constant_dynamic-update-slice_fusion.1
  48.5 1.1 constant_dynamic-update-slice_fusion
  49.5 1.1 constant_dynamic-update-slice_fusion.3
  50.6 1.1 constant_dynamic-update-slice_fusion.2
  52.6 0.9 pad_slice_fusion.3
  53.9 1.6 copy-done
  56.7 0.6 fusion.13
  58.5 0.6 fusion.17
  59.1 0.6 fusion.50
  59.7 0.6 fusion.47
  60.7 1.0 fusion.92
  61.7 2.5 %collective-permute-start.3 = (bf16[1,2,8,64,256]{4,3,2,1,0:T(8,128)(2,1)S(1)}, bf16[1,2,8,64,256]{4,3,2,1,0:T(8,128)(2,1)S(1)}, u32[]{:S(2)}, u32[]{:S(2)}) collective-permute-start(bf16[1,2,8,64,256]{4,3,2,1,0:T(8,128)(2,1)S(1)} %get-tuple-element.39), channel_id=1, source_target_pairs={{16,0},{32,16},{48,32},{64,48},{80,64},{96,80},{112,96},{128,112},... | collective-permute-start | bytes 1572872 | tf_op jit(solution)/shard_map/ppermute | solution.py:10
  64.2 4.5 %collective-permute-start.6 = (bf16[1,2,8,64,256]{4,3,2,1,0:T(8,128)(2,1)S(1)}, bf16[1,2,8,64,256]{4,3,2,1,0:T(8,128)(2,1)S(1)}, u32[]{:S(2)}, u32[]{:S(2)}) collective-permute-start(bf16[1,2,8,64,256]{4,3,2,1,0:T(8,128)(2,1)S(1)} %get-tuple-element.39), channel_id=1, source_target_pairs={{0,1},{1,0},{2,3},{3,2},{4,5},{5,4},{6,7},{7,6},{8,9},{9,8},{10,11... | collective-permute-start | bytes 1572872 | tf_op jit(solution)/shard_map/ppermute | solution.py:167
  69.0 1.3 pad_slice_fusion.1
  70.3 0.7 pad_maximum_fusion.2
  71.0 2.3 %fusion.114 = (bf16[2,2,8,64,384]{4,3,2,1,0:T(8,128)(2,1)S(1)}, bf16[2,2,8,64,384]{4,3,2,1,0:T(8,128)(2,1)S(1)}, bf16[2,2,8,64,384]{4,3,2,1,0:T(8,128)(2,1)S(1)}...) fusion(bf16[2,4,10,64,384]{4,3,2,1,0:T(8,128)(2,1)S(1)} %pad_ma, ...), kind=kLoop, calls=%fused_computation.224 | loop fusion | bytes 28311552 | tf_op jit(solution)/shard_map/slice | solution.py:172
  73.3 1.1 fusion.102
  74.4 5.4 %collective-permute-start.5 = (bf16[1,4,1,64,256]{4,3,2,1,0:T(8,128)(2,1)S(1)}, bf16[1,4,1,64,256]{4,3,2,1,0:T(8,128)(2,1)S(1)}, u32[]{:S(2)}, u32[]{:S(2)}) collective-permute-start(bf16[1,4,1,64,256]{4,3,2,1,0:T(8,128)(2,1)S(1)} %get-tuple-element.24), channel_id=1, source_target_pairs={{1,0},{3,2},{5,4},{7,6},{9,8},{11,10},{13,12},{15,14},{17,16},{19,... | collective-permute-start | bytes 393224 | tf_op jit(solution)/shard_map/ppermute | solution.py:20
  79.9 1.3 collective-permute-start.4
  81.5 0.6 fusion.89
  82.1 0.6 fusion.86
  82.7 0.6 fusion.83
  83.6 0.6 fusion.80
  84.2 0.6 fusion.77
  84.8 0.6 fusion.74
  85.7 0.6 fusion.71
  86.3 0.6 fusion.68
  86.9 0.6 fusion.65
  87.7 1.9 %collective-permute-start.7 = (f32[9,64,256]{2,1,0:T(8,128)S(1)}, f32[9,64,256]{2,1,0:T(8,128)S(1)}, u32[]{:S(2)}, u32[]{:S(2)}) collective-permute-start(f32[9,64,256]{2,1,0:T(8,128)S(1)} %constant_dynamic-slice_fusion.12), channel_id=1, source_target_pairs={{0,2},{2,0},{4,6},{6,4},{8,10},{10,8},{12,14},{14,12},{1,3},{3,1},... | collective-permute-start | bytes 1769480 | tf_op jit(solution)/shard_map/ppermute | solution.py:30
  89.6 0.8 select_maximum_fusion
  90.4 0.9 fusion.115
  93.0 0.6 fusion.61
  94.2 3.1 %collective-permute-done.13 = f32[9,64,256]{2,1,0:T(8,128)S(1)} collective-permute-done((f32[9,64,256]{2,1,0:T(8,128)S(1)}, f32[9,64,256]{2,1,0:T(8,128)S(1)}, u32[]{:S(2)}, u32[]{:S(2)}) %collective-permute-start.13) | collective-permute-done | bytes 589856 | tf_op jit(solution)/shard_map/ppermute | solution.py:30
  97.4 1.7 collective-permute-start.14
  99.5 1.3 collective-permute-start.11
  100.8 1.0 collective-permute-done.7
  101.9 1.6 collective-permute-start.8
  103.4 4.7 %collective-permute-done.14 = f32[9,32,256]{2,1,0:T(8,128)S(1)} collective-permute-done((f32[9,32,256]{2,1,0:T(8,128)S(1)}, f32[9,32,256]{2,1,0:T(8,128)S(1)}, u32[]{:S(2)}, u32[]{:S(2)}) %collective-permute-start.14) | collective-permute-done | bytes 294944 | tf_op jit(solution)/shard_map/ppermute | solution.py:30
  108.2 1.6 collective-permute-start.15
  109.8 1.4 collective-permute-start.12
  111.2 1.2 collective-permute-start.9
  112.5 1.4 collective-permute-done.15
  114.2 1.4 collective-permute-done.9
  115.7 2.7 %collective-permute-start.16 = (f32[3,9,8,256]{3,2,1,0:T(8,128)S(1)}, f32[3,9,8,256]{3,2,1,0:T(8,128)S(1)}, u32[]{:S(2)}, u32[]{:S(2)}) collective-permute-start(f32[3,9,8,256]{3,2,1,0:T(8,128)S(1)} %constant_dynamic-slice_fusion.3), channel_id=1, source_target_pairs={{0,32},{16,48},{32,0},{48,16},{64,96},{80,112},{96,64},{112,80},{1... | collective-permute-start | bytes 663560 | tf_op jit(solution)/shard_map/ppermute | solution.py:30
  119.0 3.0 %collective-permute-done.16 = f32[3,9,8,256]{3,2,1,0:T(8,128)S(1)} collective-permute-done((f32[3,9,8,256]{3,2,1,0:T(8,128)S(1)}, f32[3,9,8,256]{3,2,1,0:T(8,128)S(1)}, u32[]{:S(2)}, u32[]{:S(2)}) %collective-permute-start.16) | collective-permute-done | bytes 221216 | tf_op jit(solution)/shard_map/ppermute | solution.py:30
  122.2 2.2 %collective-permute-start.17 = (f32[3,9,4,256]{3,2,1,0:T(4,128)S(1)}, f32[3,9,4,256]{3,2,1,0:T(4,128)S(1)}, u32[]{:S(2)}, u32[]{:S(2)}) collective-permute-start(f32[3,9,4,256]{3,2,1,0:T(4,128)S(1)} %constant_dynamic-slice_fusion.2), channel_id=1, source_target_pairs={{0,128},{16,144},{32,160},{48,176},{64,192},{80,208},{96,224},{112... | collective-permute-start | bytes 331784 | tf_op jit(solution)/shard_map/ppermute | solution.py:30
  124.3 0.6 fusion.58
  125.0 2.7 %collective-permute-done.17 = f32[3,9,4,256]{3,2,1,0:T(4,128)S(1)} collective-permute-done((f32[3,9,4,256]{3,2,1,0:T(4,128)S(1)}, f32[3,9,4,256]{3,2,1,0:T(4,128)S(1)}, u32[]{:S(2)}, u32[]{:S(2)}) %collective-permute-start.17) | collective-permute-done | bytes 110624 | tf_op jit(solution)/shard_map/ppermute | solution.py:30
  127.7 3.1 %collective-permute-start.18 = (f32[3,9,2,256]{3,2,1,0:T(2,128)S(1)}, f32[3,9,2,256]{3,2,1,0:T(2,128)S(1)}, u32[]{:S(2)}, u32[]{:S(2)}) collective-permute-start(f32[3,9,2,256]{3,2,1,0:T(2,128)S(1)} %constant_dynamic-slice_fusion.1), channel_id=1, source_target_pairs={{0,4},{2,6},{4,0},{6,2},{8,12},{10,14},{12,8},{14,10},{1,5},{3,7},... | collective-permute-start | bytes 165896 | tf_op jit(solution)/shard_map/ppermute | solution.py:30
  131.4 1.8 %collective-permute-done.18 = f32[3,9,2,256]{3,2,1,0:T(2,128)S(1)} collective-permute-done((f32[3,9,2,256]{3,2,1,0:T(2,128)S(1)}, f32[3,9,2,256]{3,2,1,0:T(2,128)S(1)}, u32[]{:S(2)}, u32[]{:S(2)}) %collective-permute-start.18) | collective-permute-done | bytes 55328 | tf_op jit(solution)/shard_map/ppermute | solution.py:30
  133.3 5.2 %collective-permute-start.19 = (f32[3,9,1,256]{3,2,1,0:T(1,128)S(1)}, f32[3,9,1,256]{3,2,1,0:T(1,128)S(1)}, u32[]{:S(2)}, u32[]{:S(2)}) collective-permute-start(f32[3,9,1,256]{3,2,1,0:T(1,128)S(1)} %constant_dynamic-slice_fusion), channel_id=1, source_target_pairs={{0,8},{2,10},{4,12},{6,14},{8,0},{10,2},{12,4},{14,6},{1,9},{3,11}... | collective-permute-start | bytes 82952 | tf_op jit(solution)/shard_map/ppermute | solution.py:30
  139.1 0.9 collective-permute-done.19
  140.1 12.9 %collective-permute-start.22 = (f32[9,1,256]{2,1,0:T(1,128)S(1)}, f32[9,1,256]{2,1,0:T(1,128)S(1)}, u32[]{:S(2)}, u32[]{:S(2)}) collective-permute-start(f32[9,1,256]{2,1,0:T(1,128)S(1)} %get-tuple-element.26), channel_id=1, source_target_pairs={{0,0},{1,128},{2,32},{3,160},{4,2},{5,130},{6,34},{7,162},{8,1},{9... | collective-permute-start | bytes 27656 | tf_op jit(solution)/shard_map/ppermute | solution.py:86
  153.0 10.8 %collective-permute-start.21 = (f32[9,1,256]{2,0,1:T(8,128)S(1)}, f32[9,1,256]{2,0,1:T(8,128)S(1)}, u32[]{:S(2)}, u32[]{:S(2)}) collective-permute-start(f32[9,1,256]{2,0,1:T(8,128)S(1)} %bitcast.395), channel_id=1, source_target_pairs={{0,0},{1,128},{2,16},{3,144},{4,2},{5,130},{6,18},{7,146},{8,1},{9... | collective-permute-start | bytes 27656 | tf_op jit(solution)/shard_map/ppermute | solution.py:86
  163.8 1.9 %collective-permute-start.20 = (f32[9,1,256]{2,0,1:T(8,128)S(1)}, f32[9,1,256]{2,0,1:T(8,128)S(1)}, u32[]{:S(2)}, u32[]{:S(2)}) collective-permute-start(f32[9,1,256]{2,0,1:T(8,128)S(1)} %bitcast.396), channel_id=1, source_target_pairs={{0,0},{1,128},{2,64},{3,192},{4,2},{5,130},{6,66},{7,194},{8,1},{9... | collective-permute-start | bytes 27656 | tf_op jit(solution)/shard_map/ppermute | solution.py:86
  165.8 1.4 fusion.64
  167.2 6.2 %collective-permute-done.20 = f32[9,1,256]{2,0,1:T(8,128)S(1)} collective-permute-done((f32[9,1,256]{2,0,1:T(8,128)S(1)}, f32[9,1,256]{2,0,1:T(8,128)S(1)}, u32[]{:S(2)}, u32[]{:S(2)}) %collective-permute-start.20) | collective-permute-done | bytes 9248 | tf_op jit(solution)/shard_map/ppermute | solution.py:86
  173.4 0.6 pad_maximum_fusion.10
  (93 shorter events, 11.7 us)
Async XLA Ops:
  0.6 48.9 %collective-permute-start.1 = (bf16[1,2,8,64,256]{4,3,2,1,0:T(8,128)(2,1)}, bf16[1,2,8,64,256]{4,3,2,1,0:T(8,128)(2,1)}, u32[]{:S(2)}, u32[]{:S(2)}) collective-permute-start(bf16[1,2,8,64,256]{4,3,2,1,0:T(8,128)(2,1)} %param.4), channel_id=1, source_target_pairs={{0,17},{1,16},{16,33},{17,32},{32,49},{33,48},{48,65},{49,64},{64,... | collective-permute-start | bytes 1572872 | tf_op jit(solution)/shard_map/ppermute | solution.py:127
  4.3 46.3 %collective-permute-start.2 = (bf16[1,2,8,64,256]{4,3,2,1,0:T(8,128)(2,1)}, bf16[1,2,8,64,256]{4,3,2,1,0:T(8,128)(2,1)}, u32[]{:S(2)}, u32[]{:S(2)}) collective-permute-start(bf16[1,2,8,64,256]{4,3,2,1,0:T(8,128)(2,1)} %param.4), channel_id=1, source_target_pairs={{0,1},{1,0},{2,3},{3,2},{4,5},{5,4},{6,7},{7,6},{8,9},{9,8},{10,11... | collective-permute-start | bytes 1572872 | tf_op jit(solution)/shard_map/ppermute | solution.py:124
  4.4 42.9 %collective-permute-start = (bf16[1,2,8,64,256]{4,3,2,1,0:T(8,128)(2,1)}, bf16[1,2,8,64,256]{4,3,2,1,0:T(8,128)(2,1)}, u32[]{:S(2)}, u32[]{:S(2)}) collective-permute-start(bf16[1,2,8,64,256]{4,3,2,1,0:T(8,128)(2,1)} %param.4), channel_id=1, source_target_pairs={{0,16},{16,32},{32,48},{48,64},{64,80},{80,96},{96,112},{112,128},... | collective-permute-start | bytes 1572872 | tf_op jit(solution)/shard_map/ppermute | solution.py:10
  53.5 2.0 %copy-start = (bf16[6912,256]{1,0:T(8,128)(2,1)S(1)}, bf16[6912,256]{1,0:T(8,128)(2,1)}, u32[]{:S(2)}) copy-start(bf16[6912,256]{1,0:T(8,128)(2,1)} %param.6) | copy-start | bytes 10616836
  59.7 1.0 copy-start.5
  61.7 12.7 %collective-permute-start.3 = (bf16[1,2,8,64,256]{4,3,2,1,0:T(8,128)(2,1)S(1)}, bf16[1,2,8,64,256]{4,3,2,1,0:T(8,128)(2,1)S(1)}, u32[]{:S(2)}, u32[]{:S(2)}) collective-permute-start(bf16[1,2,8,64,256]{4,3,2,1,0:T(8,128)(2,1)S(1)} %get-tuple-element.39), channel_id=1, source_target_pairs={{16,0},{32,16},{48,32},{64,48},{80,64},{96,80},{112,96},{128,112},... | collective-permute-start | bytes 1572872 | tf_op jit(solution)/shard_map/ppermute | solution.py:10
  64.2 17.0 %collective-permute-start.6 = (bf16[1,2,8,64,256]{4,3,2,1,0:T(8,128)(2,1)S(1)}, bf16[1,2,8,64,256]{4,3,2,1,0:T(8,128)(2,1)S(1)}, u32[]{:S(2)}, u32[]{:S(2)}) collective-permute-start(bf16[1,2,8,64,256]{4,3,2,1,0:T(8,128)(2,1)S(1)} %get-tuple-element.39), channel_id=1, source_target_pairs={{0,1},{1,0},{2,3},{3,2},{4,5},{5,4},{6,7},{7,6},{8,9},{9,8},{10,11... | collective-permute-start | bytes 1572872 | tf_op jit(solution)/shard_map/ppermute | solution.py:167
  73.3 7.9 %copy-start.2 = (bf16[2]{0:T(256)(128)(2,1)S(1)}, bf16[2]{0:T(256)(128)(2,1)}, u32[]{:S(2)}) copy-start(bf16[2]{0:T(256)(128)(2,1)} %get-tuple-element.31) | copy-start | bytes 16
  73.3 7.9 %copy-start.3 = (bf16[2]{0:T(256)(128)(2,1)S(1)}, bf16[2]{0:T(256)(128)(2,1)}, u32[]{:S(2)}) copy-start(bf16[2]{0:T(256)(128)(2,1)} %get-tuple-element.33) | copy-start | bytes 16
  73.3 7.9 %copy-start.4 = (bf16[2]{0:T(256)(128)(2,1)S(1)}, bf16[2]{0:T(256)(128)(2,1)}, u32[]{:S(2)}) copy-start(bf16[2]{0:T(256)(128)(2,1)} %get-tuple-element.34) | copy-start | bytes 16
  74.4 15.2 %collective-permute-start.5 = (bf16[1,4,1,64,256]{4,3,2,1,0:T(8,128)(2,1)S(1)}, bf16[1,4,1,64,256]{4,3,2,1,0:T(8,128)(2,1)S(1)}, u32[]{:S(2)}, u32[]{:S(2)}) collective-permute-start(bf16[1,4,1,64,256]{4,3,2,1,0:T(8,128)(2,1)S(1)} %get-tuple-element.24), channel_id=1, source_target_pairs={{1,0},{3,2},{5,4},{7,6},{9,8},{11,10},{13,12},{15,14},{17,16},{19,... | collective-permute-start | bytes 393224 | tf_op jit(solution)/shard_map/ppermute | solution.py:20
  79.9 9.7 %collective-permute-start.4 = (bf16[1,4,1,64,256]{4,3,2,1,0:T(8,128)(2,1)S(1)}, bf16[1,4,1,64,256]{4,3,2,1,0:T(8,128)(2,1)S(1)}, u32[]{:S(2)}, u32[]{:S(2)}) collective-permute-start(bf16[1,4,1,64,256]{4,3,2,1,0:T(8,128)(2,1)S(1)} %get-tuple-element.23), channel_id=1, source_target_pairs={{0,1},{2,3},{4,5},{6,7},{8,9},{10,11},{12,13},{14,15},{16,17},{18,... | collective-permute-start | bytes 393224 | tf_op jit(solution)/shard_map/ppermute | solution.py:17
  83.5 13.8 %collective-permute-start.13 = (f32[9,64,256]{2,1,0:T(8,128)S(1)}, f32[9,64,256]{2,1,0:T(8,128)S(1)}, u32[]{:S(2)}, u32[]{:S(2)}) collective-permute-start(f32[9,64,256]{2,1,0:T(8,128)S(1)} %constant_dynamic-slice_fusion.6), channel_id=1, source_target_pairs={{0,64},{16,80},{32,96},{48,112},{64,0},{80,16},{96,32},{112,48},{1... | collective-permute-start | bytes 1769480 | tf_op jit(solution)/shard_map/ppermute | solution.py:30
  85.6 13.8 %collective-permute-start.10 = (f32[9,64,256]{2,1,0:T(8,128)S(1)}, f32[9,64,256]{2,1,0:T(8,128)S(1)}, u32[]{:S(2)}, u32[]{:S(2)}) collective-permute-start(f32[9,64,256]{2,1,0:T(8,128)S(1)} %constant_dynamic-slice_fusion.9), channel_id=1, source_target_pairs={{0,16},{16,0},{32,48},{48,32},{64,80},{80,64},{96,112},{112,96},{1... | collective-permute-start | bytes 1769480 | tf_op jit(solution)/shard_map/ppermute | solution.py:30
  87.7 14.1 %collective-permute-start.7 = (f32[9,64,256]{2,1,0:T(8,128)S(1)}, f32[9,64,256]{2,1,0:T(8,128)S(1)}, u32[]{:S(2)}, u32[]{:S(2)}) collective-permute-start(f32[9,64,256]{2,1,0:T(8,128)S(1)} %constant_dynamic-slice_fusion.12), channel_id=1, source_target_pairs={{0,2},{2,0},{4,6},{6,4},{8,10},{10,8},{12,14},{14,12},{1,3},{3,1},... | collective-permute-start | bytes 1769480 | tf_op jit(solution)/shard_map/ppermute | solution.py:30
  92.3 0.6 copy-start.1
  97.4 10.6 %collective-permute-start.14 = (f32[9,32,256]{2,1,0:T(8,128)S(1)}, f32[9,32,256]{2,1,0:T(8,128)S(1)}, u32[]{:S(2)}, u32[]{:S(2)}) collective-permute-start(f32[9,32,256]{2,1,0:T(8,128)S(1)} %constant_dynamic-slice_fusion.5), channel_id=1, source_target_pairs={{0,2},{2,0},{4,6},{6,4},{8,10},{10,8},{12,14},{14,12},{1,3},{3,1},... | collective-permute-start | bytes 884744 | tf_op jit(solution)/shard_map/ppermute | solution.py:30
  99.5 10.2 %collective-permute-start.11 = (f32[9,32,256]{2,1,0:T(8,128)S(1)}, f32[9,32,256]{2,1,0:T(8,128)S(1)}, u32[]{:S(2)}, u32[]{:S(2)}) collective-permute-start(f32[9,32,256]{2,1,0:T(8,128)S(1)} %constant_dynamic-slice_fusion.8), channel_id=1, source_target_pairs={{0,64},{16,80},{32,96},{48,112},{64,0},{80,16},{96,32},{112,48},{1... | collective-permute-start | bytes 884744 | tf_op jit(solution)/shard_map/ppermute | solution.py:30
  101.9 9.3 %collective-permute-start.8 = (f32[9,32,256]{2,1,0:T(8,128)S(1)}, f32[9,32,256]{2,1,0:T(8,128)S(1)}, u32[]{:S(2)}, u32[]{:S(2)}) collective-permute-start(f32[9,32,256]{2,1,0:T(8,128)S(1)} %constant_dynamic-slice_fusion.11), channel_id=1, source_target_pairs={{0,16},{16,0},{32,48},{48,32},{64,80},{80,64},{96,112},{112,96},{1... | collective-permute-start | bytes 884744 | tf_op jit(solution)/shard_map/ppermute | solution.py:30
  108.2 5.7 %collective-permute-start.15 = (f32[9,16,256]{2,1,0:T(8,128)S(1)}, f32[9,16,256]{2,1,0:T(8,128)S(1)}, u32[]{:S(2)}, u32[]{:S(2)}) collective-permute-start(f32[9,16,256]{2,1,0:T(8,128)S(1)} %constant_dynamic-slice_fusion.4), channel_id=1, source_target_pairs={{0,16},{16,0},{32,48},{48,32},{64,80},{80,64},{96,112},{112,96},{1... | collective-permute-start | bytes 442376 | tf_op jit(solution)/shard_map/ppermute | solution.py:30
  109.8 4.4 %collective-permute-start.12 = (f32[9,16,256]{2,1,0:T(8,128)S(1)}, f32[9,16,256]{2,1,0:T(8,128)S(1)}, u32[]{:S(2)}, u32[]{:S(2)}) collective-permute-start(f32[9,16,256]{2,1,0:T(8,128)S(1)} %constant_dynamic-slice_fusion.7), channel_id=1, source_target_pairs={{0,2},{2,0},{4,6},{6,4},{8,10},{10,8},{12,14},{14,12},{1,3},{3,1},... | collective-permute-start | bytes 442376 | tf_op jit(solution)/shard_map/ppermute | solution.py:30
  111.2 4.4 %collective-permute-start.9 = (f32[9,16,256]{2,1,0:T(8,128)S(1)}, f32[9,16,256]{2,1,0:T(8,128)S(1)}, u32[]{:S(2)}, u32[]{:S(2)}) collective-permute-start(f32[9,16,256]{2,1,0:T(8,128)S(1)} %constant_dynamic-slice_fusion.10), channel_id=1, source_target_pairs={{0,64},{16,80},{32,96},{48,112},{64,0},{80,16},{96,32},{112,48},{1... | collective-permute-start | bytes 442376 | tf_op jit(solution)/shard_map/ppermute | solution.py:30
  115.7 6.4 %collective-permute-start.16 = (f32[3,9,8,256]{3,2,1,0:T(8,128)S(1)}, f32[3,9,8,256]{3,2,1,0:T(8,128)S(1)}, u32[]{:S(2)}, u32[]{:S(2)}) collective-permute-start(f32[3,9,8,256]{3,2,1,0:T(8,128)S(1)} %constant_dynamic-slice_fusion.3), channel_id=1, source_target_pairs={{0,32},{16,48},{32,0},{48,16},{64,96},{80,112},{96,64},{112,80},{1... | collective-permute-start | bytes 663560 | tf_op jit(solution)/shard_map/ppermute | solution.py:30
  122.2 5.5 %collective-permute-start.17 = (f32[3,9,4,256]{3,2,1,0:T(4,128)S(1)}, f32[3,9,4,256]{3,2,1,0:T(4,128)S(1)}, u32[]{:S(2)}, u32[]{:S(2)}) collective-permute-start(f32[3,9,4,256]{3,2,1,0:T(4,128)S(1)} %constant_dynamic-slice_fusion.2), channel_id=1, source_target_pairs={{0,128},{16,144},{32,160},{48,176},{64,192},{80,208},{96,224},{112... | collective-permute-start | bytes 331784 | tf_op jit(solution)/shard_map/ppermute | solution.py:30
  127.7 5.5 %collective-permute-start.18 = (f32[3,9,2,256]{3,2,1,0:T(2,128)S(1)}, f32[3,9,2,256]{3,2,1,0:T(2,128)S(1)}, u32[]{:S(2)}, u32[]{:S(2)}) collective-permute-start(f32[3,9,2,256]{3,2,1,0:T(2,128)S(1)} %constant_dynamic-slice_fusion.1), channel_id=1, source_target_pairs={{0,4},{2,6},{4,0},{6,2},{8,12},{10,14},{12,8},{14,10},{1,5},{3,7},... | collective-permute-start | bytes 165896 | tf_op jit(solution)/shard_map/ppermute | solution.py:30
  133.3 6.7 %collective-permute-start.19 = (f32[3,9,1,256]{3,2,1,0:T(1,128)S(1)}, f32[3,9,1,256]{3,2,1,0:T(1,128)S(1)}, u32[]{:S(2)}, u32[]{:S(2)}) collective-permute-start(f32[3,9,1,256]{3,2,1,0:T(1,128)S(1)} %constant_dynamic-slice_fusion), channel_id=1, source_target_pairs={{0,8},{2,10},{4,12},{6,14},{8,0},{10,2},{12,4},{14,6},{1,9},{3,11}... | collective-permute-start | bytes 82952 | tf_op jit(solution)/shard_map/ppermute | solution.py:30
  140.1 27.1 %collective-permute-start.22 = (f32[9,1,256]{2,1,0:T(1,128)S(1)}, f32[9,1,256]{2,1,0:T(1,128)S(1)}, u32[]{:S(2)}, u32[]{:S(2)}) collective-permute-start(f32[9,1,256]{2,1,0:T(1,128)S(1)} %get-tuple-element.26), channel_id=1, source_target_pairs={{0,0},{1,128},{2,32},{3,160},{4,2},{5,130},{6,34},{7,162},{8,1},{9... | collective-permute-start | bytes 27656 | tf_op jit(solution)/shard_map/ppermute | solution.py:86
  153.0 14.2 %collective-permute-start.21 = (f32[9,1,256]{2,0,1:T(8,128)S(1)}, f32[9,1,256]{2,0,1:T(8,128)S(1)}, u32[]{:S(2)}, u32[]{:S(2)}) collective-permute-start(f32[9,1,256]{2,0,1:T(8,128)S(1)} %bitcast.395), channel_id=1, source_target_pairs={{0,0},{1,128},{2,16},{3,144},{4,2},{5,130},{6,18},{7,146},{8,1},{9... | collective-permute-start | bytes 27656 | tf_op jit(solution)/shard_map/ppermute | solution.py:86
  163.8 9.6 %collective-permute-start.20 = (f32[9,1,256]{2,0,1:T(8,128)S(1)}, f32[9,1,256]{2,0,1:T(8,128)S(1)}, u32[]{:S(2)}, u32[]{:S(2)}) collective-permute-start(f32[9,1,256]{2,0,1:T(8,128)S(1)} %bitcast.396), channel_id=1, source_target_pairs={{0,0},{1,128},{2,64},{3,192},{4,2},{5,130},{6,66},{7,194},{8,1},{9... | collective-permute-start | bytes 27656 | tf_op jit(solution)/shard_map/ppermute | solution.py:86

commit v6 on v4

--- a/solution.py
+++ b/solution.py
@@ -153,14 +153,16 @@
     delta = (cotangent.astype(jnp.float32) * sigma * (1.0 + pre * (1.0 - sigma))).astype(
         jnp.bfloat16
     )
-    ahead = passed_along(lax.slice_in_dim(delta, 0, 2, axis=1), "group", -1)
-    gwide = row_halo(jnp.concatenate([delta, ahead], axis=1), "space", 2)
+    delta_other = lax.ppermute(delta, "space", swap)
+    delta_late, _ = lax.optimization_barrier((delta, delta_other))
+    ahead = passed_along(lax.slice_in_dim(delta_late, 0, 2, axis=1), "group", -1)
+    gwide = row_halo(jnp.concatenate([delta_late, ahead], axis=1), "space", 2)
     half = chans // 2
     both = jnp.concatenate([shifted, shifted_other], axis=0)
     both = lax.dynamic_slice_in_dim(both, lax.axis_index("space") * half, half, axis=4)
     both = jnp.pad(both, ((0, 0), (0, 0), (0, 0), (1, 1), (0, 0)))
     bstack = jnp.concatenate([both[:, :, :, b : b + cols] for b in range(3)], axis=4)
-    bdelta = jnp.concatenate([delta, lax.ppermute(delta, "space", swap)], axis=0)
+    bdelta = jnp.concatenate([delta, delta_other], axis=0)
     terms = []
     for k in range(3):
         masked = bdelta * same_fwd[k].astype(jnp.bfloat16)[:, :, None, None, None]

time: 171 us -> 168 us (0.982)
  starting transfers between devices: 73 us -> 70 us
    ppermute x13, waiting for transfers between devices: 20.7 us -> 17.7 us  [halve(): return keep + lax.ppermute(give, axis, pairs)]
    ppermute x1, starting transfers between devices: 4.77 us -> 2.74 us  [row_halo(): high = lax.ppermute(lax.slice_in_dim(block, 0, 1, axis=dim), axis, backward)]
    ppermute x2, waiting for transfers between devices: 0.01 us -> 1.81 us  [passed_along(): return lax.ppermute(value, axis, pairs)]
    unnamed x20 -> x21, local copies, waits for them, and re-layouts: 6.27 us -> 6.31 us
  transfers between devices with their start and end apart: 23 -> 23, of which waited for: 11 -> 12; matrix products, arithmetic and copies ran while one was open for 19% -> 18% of each run, Pallas kernels for 0% -> 0%
where the time goes in v6:
time: 168 us; the launch traced here: 165 us
  starting transfers between devices  70 us (42%)
  waiting for transfers between devices  25.7 us (15%)
  blocking collectives  23.7 us (14%)
  local copies, waits for them, and re-layouts  19 us (11%)
  matrix products  17.3 us (10%)
  other arithmetic  7.06 us (4%)
  between operations  2.24 us (1%)
    ppermute x13, starting transfers between devices, halve(): return keep + lax.ppermute(give, axis, pairs)  26.9 us
    ppermute x3, starting transfers between devices, reduce_weight_grad(): parts.append(lax.ppermute(joined[n], names, pairs).reshape(per, outs))  24.5 us
    unnamed x1, blocking collectives  23.7 us
    ppermute x13, waiting for transfers between devices, halve(): return keep + lax.ppermute(give, axis, pairs)  17.7 us
    ppermute x2, starting transfers between devices, passed_along(): return lax.ppermute(value, axis, pairs)  8.66 us
    unnamed x21, local copies, waits for them, and re-layouts  6.31 us
    ppermute x3, waiting for transfers between devices, reduce_weight_grad(): parts.append(lax.ppermute(joined[n], names, pairs).reshape(per, outs))  6.23 us
    dot_general x9, matrix products, local(): jnp.einsum('sfhwk,kc->sfhwc', block, back[k, a], preferred_element_type=j...  6.15 us
  transfers between devices with their start and end apart: 23, of which 12 were waited for; matrix products, arithmetic and copies ran while one was open for 18% of the time, Pallas kernels for 0%

profile of v6, /device:TPU:25, one launch (start us, length us, event | category | flops | bytes accessed | tf_op | source)
XLA Modules:
  0.0 165.1 jit_solution(17488067867233098561)
XLA Ops:
  0.6 3.7 %collective-permute-start.1 = (bf16[1,2,8,64,256]{4,3,2,1,0:T(8,128)(2,1)}, bf16[1,2,8,64,256]{4,3,2,1,0:T(8,128)(2,1)}, u32[]{:S(2)}, u32[]{:S(2)}) collective-permute-start(bf16[1,2,8,64,256]{4,3,2,1,0:T(8,128)(2,1)} %param.4), channel_id=1, source_target_pairs={{0,17},{1,16},{16,33},{17,32},{32,49},{33,48},{48,65},{49,64},{64,... | collective-permute-start | bytes 1572872 | tf_op jit(solution)/shard_map/ppermute | solution.py:123
  4.4 3.1 %collective-permute-start = (bf16[1,2,8,64,256]{4,3,2,1,0:T(8,128)(2,1)}, bf16[1,2,8,64,256]{4,3,2,1,0:T(8,128)(2,1)}, u32[]{:S(2)}, u32[]{:S(2)}) collective-permute-start(bf16[1,2,8,64,256]{4,3,2,1,0:T(8,128)(2,1)} %param.4), channel_id=1, source_target_pairs={{0,16},{16,32},{32,48},{48,64},{64,80},{80,96},{96,112},{112,128},... | collective-permute-start | bytes 1572872 | tf_op jit(solution)/shard_map/ppermute | solution.py:10
  7.6 1.3 dynamic-slice
  9.5 0.8 bitcast_dynamic-update-slice_fusion
  10.3 23.7 %all-reduce.7 = s32[32]{0:T(128)S(1)} all-reduce(s32[32]{0:T(128)S(1)} %bitcast_dynamic-update-slice_fusion), channel_id=1, replica_groups=mesh['group'=16,'dp'=8,'space'=2] {'group'}, use_global_device_ids=true, to_apply=%add.7 | all-reduce | flops 32 | bytes 256
  35.3 4.3 %copy.34 = bf16[3,3,3,256,256]{3,4,2,1,0:T(8,128)(2,1)S(1)} copy(bf16[3,3,3,256,256]{4,3,2,1,0:T(8,128)(2,1)} %bitcast.369) | data formatting | bytes 7077888 | tf_op jit(solution)/shard_map/reshape | solution.py:179
  39.8 1.1 constant_dynamic-update-slice_fusion.1
  40.9 1.1 constant_dynamic-update-slice_fusion
  42.0 1.1 constant_dynamic-update-slice_fusion.3
  43.1 1.1 constant_dynamic-update-slice_fusion.2
  45.0 0.9 pad_slice_fusion.3
  46.3 1.6 copy-done
  51.5 0.6 fusion.52
  52.1 0.6 fusion.49
  53.1 1.0 fusion.94
  54.1 1.1 fusion.104
  55.2 2.2 %collective-permute-start.3 = (bf16[1,2,8,64,256]{4,3,2,1,0:T(8,128)(2,1)S(1)}, bf16[1,2,8,64,256]{4,3,2,1,0:T(8,128)(2,1)S(1)}, u32[]{:S(2)}, u32[]{:S(2)}) collective-permute-start(bf16[1,2,8,64,256]{4,3,2,1,0:T(8,128)(2,1)S(1)} %get-tuple-element.4), channel_id=1, source_target_pairs={{0,1},{1,0},{2,3},{3,2},{4,5},{5,4},{6,7},{7,6},{8,9},{9,8},{10,11... | collective-permute-start | bytes 1572872 | tf_op jit(solution)/shard_map/ppermute | solution.py:156
  57.6 1.3 pad_slice_fusion.1
  58.9 0.6 pad_maximum_fusion.2
  59.6 2.3 %fusion.116 = (bf16[2,2,8,64,384]{4,3,2,1,0:T(8,128)(2,1)S(1)}, bf16[2,2,8,64,384]{4,3,2,1,0:T(8,128)(2,1)S(1)}, bf16[2,2,8,64,384]{4,3,2,1,0:T(8,128)(2,1)S(1)}...) fusion(bf16[2,4,10,64,384]{4,3,2,1,0:T(8,128)(2,1)S(1)} %pad_ma, ...), kind=kLoop, calls=%fused_computation.218 | loop fusion | bytes 28311552 | tf_op jit(solution)/shard_map/slice | solution.py:170
  61.9 5.5 %collective-permute-start.4 = (bf16[1,2,8,64,256]{4,3,2,1,0:T(8,128)(2,1)S(1)}, bf16[1,2,8,64,256]{4,3,2,1,0:T(8,128)(2,1)S(1)}, u32[]{:S(2)}, u32[]{:S(2)}) collective-permute-start(bf16[1,2,8,64,256]{4,3,2,1,0:T(8,128)(2,1)S(1)} %get-tuple-element.4), channel_id=1, source_target_pairs={{16,0},{32,16},{48,32},{64,48},{80,64},{96,80},{112,96},{128,112},... | collective-permute-start | bytes 1572872 | tf_op jit(solution)/shard_map/ppermute | solution.py:10
  67.8 0.6 fusion.91
  68.4 0.6 fusion.88
  69.0 0.6 fusion.85
  69.8 1.4 collective-permute-start.13
  71.2 0.6 fusion.82
  71.8 0.6 fusion.79
  72.4 0.6 fusion.76
  73.2 0.6 fusion.73
  73.9 0.6 fusion.70
  74.5 0.6 fusion.67
  75.2 1.7 %collective-permute-start.7 = (f32[9,64,256]{2,1,0:T(8,128)S(1)}, f32[9,64,256]{2,1,0:T(8,128)S(1)}, u32[]{:S(2)}, u32[]{:S(2)}) collective-permute-start(f32[9,64,256]{2,1,0:T(8,128)S(1)} %constant_dynamic-slice_fusion.12), channel_id=1, source_target_pairs={{0,2},{2,0},{4,6},{6,4},{8,10},{10,8},{12,14},{14,12},{1,3},{3,1},... | collective-permute-start | bytes 1769480 | tf_op jit(solution)/shard_map/ppermute | solution.py:30
  77.0 1.8 %collective-permute-done.4 = bf16[1,2,8,64,256]{4,3,2,1,0:T(8,128)(2,1)S(1)} collective-permute-done((bf16[1,2,8,64,256]{4,3,2,1,0:T(8,128)(2,1)S(1)}, bf16[1,2,8,64,256]{4,3,2,1,0:T(8,128)(2,1)S(1)}, u32[]{:S(2)}, u32[]{:S(2)}) %collective-permute-start.4) | collective-permute-done | bytes 524320 | tf_op jit(solution)/shard_map/ppermute | solution.py:10
  78.9 2.7 %collective-permute-start.6 = (bf16[1,4,1,64,256]{4,3,2,1,0:T(8,128)(2,1)S(1)}, bf16[1,4,1,64,256]{4,3,2,1,0:T(8,128)(2,1)S(1)}, u32[]{:S(2)}, u32[]{:S(2)}) collective-permute-start(bf16[1,4,1,64,256]{4,3,2,1,0:T(8,128)(2,1)S(1)} %get-tuple-element.26), channel_id=1, source_target_pairs={{1,0},{3,2},{5,4},{7,6},{9,8},{11,10},{13,12},{15,14},{17,16},{19,... | collective-permute-start | bytes 393224 | tf_op jit(solution)/shard_map/ppermute | solution.py:20
  81.6 1.3 collective-permute-start.5
  82.9 1.5 collective-permute-done.13
  84.6 1.7 %collective-permute-start.14 = (f32[9,32,256]{2,1,0:T(8,128)S(1)}, f32[9,32,256]{2,1,0:T(8,128)S(1)}, u32[]{:S(2)}, u32[]{:S(2)}) collective-permute-start(f32[9,32,256]{2,1,0:T(8,128)S(1)} %constant_dynamic-slice_fusion.5), channel_id=1, source_target_pairs={{0,2},{2,0},{4,6},{6,4},{8,10},{10,8},{12,14},{14,12},{1,3},{3,1},... | collective-permute-start | bytes 884744 | tf_op jit(solution)/shard_map/ppermute | solution.py:30
  86.3 5.1 %collective-permute-done.10 = f32[9,64,256]{2,1,0:T(8,128)S(1)} collective-permute-done((f32[9,64,256]{2,1,0:T(8,128)S(1)}, f32[9,64,256]{2,1,0:T(8,128)S(1)}, u32[]{:S(2)}, u32[]{:S(2)}) %collective-permute-start.10) | collective-permute-done | bytes 589856 | tf_op jit(solution)/shard_map/ppermute | solution.py:30
  91.6 1.0 collective-permute-start.11
  92.8 0.8 fusion.41
  93.6 0.9 fusion.117
  96.1 0.6 fusion.63
  97.4 1.5 collective-permute-start.15
  98.9 1.0 collective-permute-done.11
  99.9 1.7 %collective-permute-start.12 = (f32[9,16,256]{2,1,0:T(8,128)S(1)}, f32[9,16,256]{2,1,0:T(8,128)S(1)}, u32[]{:S(2)}, u32[]{:S(2)}) collective-permute-start(f32[9,16,256]{2,1,0:T(8,128)S(1)} %constant_dynamic-slice_fusion.7), channel_id=1, source_target_pairs={{0,2},{2,0},{4,6},{6,4},{8,10},{10,8},{12,14},{14,12},{1,3},{3,1},... | collective-permute-start | bytes 442376 | tf_op jit(solution)/shard_map/ppermute | solution.py:30
  101.7 0.8 collective-permute-start.9
  102.5 1.1 collective-permute-done.15
  103.7 0.8 collective-permute-done.12
  104.5 1.6 collective-permute-done.9
  106.2 4.9 %collective-permute-start.16 = (f32[3,9,8,256]{3,2,1,0:T(8,128)S(1)}, f32[3,9,8,256]{3,2,1,0:T(8,128)S(1)}, u32[]{:S(2)}, u32[]{:S(2)}) collective-permute-start(f32[3,9,8,256]{3,2,1,0:T(8,128)S(1)} %constant_dynamic-slice_fusion.3), channel_id=1, source_target_pairs={{0,32},{16,48},{32,0},{48,16},{64,96},{80,112},{96,64},{112,80},{1... | collective-permute-start | bytes 663560 | tf_op jit(solution)/shard_map/ppermute | solution.py:30
  111.7 2.7 %collective-permute-done.16 = f32[3,9,8,256]{3,2,1,0:T(8,128)S(1)} collective-permute-done((f32[3,9,8,256]{3,2,1,0:T(8,128)S(1)}, f32[3,9,8,256]{3,2,1,0:T(8,128)S(1)}, u32[]{:S(2)}, u32[]{:S(2)}) %collective-permute-start.16) | collective-permute-done | bytes 221216 | tf_op jit(solution)/shard_map/ppermute | solution.py:30
  114.5 3.3 %collective-permute-start.17 = (f32[3,9,4,256]{3,2,1,0:T(4,128)S(1)}, f32[3,9,4,256]{3,2,1,0:T(4,128)S(1)}, u32[]{:S(2)}, u32[]{:S(2)}) collective-permute-start(f32[3,9,4,256]{3,2,1,0:T(4,128)S(1)} %constant_dynamic-slice_fusion.2), channel_id=1, source_target_pairs={{0,128},{16,144},{32,160},{48,176},{64,192},{80,208},{96,224},{112... | collective-permute-start | bytes 331784 | tf_op jit(solution)/shard_map/ppermute | solution.py:30
  117.8 0.6 fusion.60
  118.4 1.5 collective-permute-done.17
  120.0 3.1 %collective-permute-start.18 = (f32[3,9,2,256]{3,2,1,0:T(2,128)S(1)}, f32[3,9,2,256]{3,2,1,0:T(2,128)S(1)}, u32[]{:S(2)}, u32[]{:S(2)}) collective-permute-start(f32[3,9,2,256]{3,2,1,0:T(2,128)S(1)} %constant_dynamic-slice_fusion.1), channel_id=1, source_target_pairs={{0,4},{2,6},{4,0},{6,2},{8,12},{10,14},{12,8},{14,10},{1,5},{3,7},... | collective-permute-start | bytes 165896 | tf_op jit(solution)/shard_map/ppermute | solution.py:30
  123.7 1.5 collective-permute-done.18
  125.3 5.5 %collective-permute-start.19 = (f32[3,9,1,256]{3,2,1,0:T(1,128)S(1)}, f32[3,9,1,256]{3,2,1,0:T(1,128)S(1)}, u32[]{:S(2)}, u32[]{:S(2)}) collective-permute-start(f32[3,9,1,256]{3,2,1,0:T(1,128)S(1)} %constant_dynamic-slice_fusion), channel_id=1, source_target_pairs={{0,8},{2,10},{4,12},{6,14},{8,0},{10,2},{12,4},{14,6},{1,9},{3,11}... | collective-permute-start | bytes 82952 | tf_op jit(solution)/shard_map/ppermute | solution.py:30
  131.4 0.8 collective-permute-done.19
  132.2 10.9 %collective-permute-start.22 = (f32[9,1,256]{2,1,0:T(1,128)S(1)}, f32[9,1,256]{2,1,0:T(1,128)S(1)}, u32[]{:S(2)}, u32[]{:S(2)}) collective-permute-start(f32[9,1,256]{2,1,0:T(1,128)S(1)} %get-tuple-element.28), channel_id=1, source_target_pairs={{0,0},{1,128},{2,32},{3,160},{4,2},{5,130},{6,34},{7,162},{8,1},{9... | collective-permute-start | bytes 27656 | tf_op jit(solution)/shard_map/ppermute | solution.py:86
  143.1 11.7 %collective-permute-start.21 = (f32[9,1,256]{2,0,1:T(8,128)S(1)}, f32[9,1,256]{2,0,1:T(8,128)S(1)}, u32[]{:S(2)}, u32[]{:S(2)}) collective-permute-start(f32[9,1,256]{2,0,1:T(8,128)S(1)} %bitcast.388), channel_id=1, source_target_pairs={{0,0},{1,128},{2,16},{3,144},{4,2},{5,130},{6,18},{7,146},{8,1},{9... | collective-permute-start | bytes 27656 | tf_op jit(solution)/shard_map/ppermute | solution.py:86
  154.9 1.9 %collective-permute-start.20 = (f32[9,1,256]{2,0,1:T(8,128)S(1)}, f32[9,1,256]{2,0,1:T(8,128)S(1)}, u32[]{:S(2)}, u32[]{:S(2)}) collective-permute-start(f32[9,1,256]{2,0,1:T(8,128)S(1)} %bitcast.389), channel_id=1, source_target_pairs={{0,0},{1,128},{2,64},{3,192},{4,2},{5,130},{6,66},{7,194},{8,1},{9... | collective-permute-start | bytes 27656 | tf_op jit(solution)/shard_map/ppermute | solution.py:86
  156.8 1.4 fusion.66
  158.2 6.2 %collective-permute-done.20 = f32[9,1,256]{2,0,1:T(8,128)S(1)} collective-permute-done((f32[9,1,256]{2,0,1:T(8,128)S(1)}, f32[9,1,256]{2,0,1:T(8,128)S(1)}, u32[]{:S(2)}, u32[]{:S(2)}) %collective-permute-start.20) | collective-permute-done | bytes 9248 | tf_op jit(solution)/shard_map/ppermute | solution.py:86
  164.5 0.6 pad_maximum_fusion.8
  (94 shorter events, 12.6 us)
Async XLA Ops:
  0.6 41.3 %collective-permute-start.1 = (bf16[1,2,8,64,256]{4,3,2,1,0:T(8,128)(2,1)}, bf16[1,2,8,64,256]{4,3,2,1,0:T(8,128)(2,1)}, u32[]{:S(2)}, u32[]{:S(2)}) collective-permute-start(bf16[1,2,8,64,256]{4,3,2,1,0:T(8,128)(2,1)} %param.4), channel_id=1, source_target_pairs={{0,17},{1,16},{16,33},{17,32},{32,49},{33,48},{48,65},{49,64},{64,... | collective-permute-start | bytes 1572872 | tf_op jit(solution)/shard_map/ppermute | solution.py:123
  4.3 38.7 %collective-permute-start.2 = (bf16[1,2,8,64,256]{4,3,2,1,0:T(8,128)(2,1)}, bf16[1,2,8,64,256]{4,3,2,1,0:T(8,128)(2,1)}, u32[]{:S(2)}, u32[]{:S(2)}) collective-permute-start(bf16[1,2,8,64,256]{4,3,2,1,0:T(8,128)(2,1)} %param.4), channel_id=1, source_target_pairs={{0,1},{1,0},{2,3},{3,2},{4,5},{5,4},{6,7},{7,6},{8,9},{9,8},{10,11... | collective-permute-start | bytes 1572872 | tf_op jit(solution)/shard_map/ppermute | solution.py:120
  4.4 35.3 %collective-permute-start = (bf16[1,2,8,64,256]{4,3,2,1,0:T(8,128)(2,1)}, bf16[1,2,8,64,256]{4,3,2,1,0:T(8,128)(2,1)}, u32[]{:S(2)}, u32[]{:S(2)}) collective-permute-start(bf16[1,2,8,64,256]{4,3,2,1,0:T(8,128)(2,1)} %param.4), channel_id=1, source_target_pairs={{0,16},{16,32},{32,48},{48,64},{64,80},{80,96},{96,112},{112,128},... | collective-permute-start | bytes 1572872 | tf_op jit(solution)/shard_map/ppermute | solution.py:10
  45.9 2.0 %copy-start = (bf16[6912,256]{1,0:T(8,128)(2,1)S(1)}, bf16[6912,256]{1,0:T(8,128)(2,1)}, u32[]{:S(2)}) copy-start(bf16[6912,256]{1,0:T(8,128)(2,1)} %param.6) | copy-start | bytes 10616836
  52.1 1.0 copy-start.5
  55.2 6.7 %collective-permute-start.3 = (bf16[1,2,8,64,256]{4,3,2,1,0:T(8,128)(2,1)S(1)}, bf16[1,2,8,64,256]{4,3,2,1,0:T(8,128)(2,1)S(1)}, u32[]{:S(2)}, u32[]{:S(2)}) collective-permute-start(bf16[1,2,8,64,256]{4,3,2,1,0:T(8,128)(2,1)S(1)} %get-tuple-element.4), channel_id=1, source_target_pairs={{0,1},{1,0},{2,3},{3,2},{4,5},{5,4},{6,7},{7,6},{8,9},{9,8},{10,11... | collective-permute-start | bytes 1572872 | tf_op jit(solution)/shard_map/ppermute | solution.py:156
  59.6 7.9 %copy-start.2 = (bf16[2]{0:T(256)(128)(2,1)S(1)}, bf16[2]{0:T(256)(128)(2,1)}, u32[]{:S(2)}) copy-start(bf16[2]{0:T(256)(128)(2,1)} %get-tuple-element.33) | copy-start | bytes 16
  59.6 7.9 %copy-start.3 = (bf16[2]{0:T(256)(128)(2,1)S(1)}, bf16[2]{0:T(256)(128)(2,1)}, u32[]{:S(2)}) copy-start(bf16[2]{0:T(256)(128)(2,1)} %get-tuple-element.35) | copy-start | bytes 16
  59.6 7.9 %copy-start.4 = (bf16[2]{0:T(256)(128)(2,1)S(1)}, bf16[2]{0:T(256)(128)(2,1)}, u32[]{:S(2)}) copy-start(bf16[2]{0:T(256)(128)(2,1)} %get-tuple-element.36) | copy-start | bytes 16
  61.9 16.9 %collective-permute-start.4 = (bf16[1,2,8,64,256]{4,3,2,1,0:T(8,128)(2,1)S(1)}, bf16[1,2,8,64,256]{4,3,2,1,0:T(8,128)(2,1)S(1)}, u32[]{:S(2)}, u32[]{:S(2)}) collective-permute-start(bf16[1,2,8,64,256]{4,3,2,1,0:T(8,128)(2,1)S(1)} %get-tuple-element.4), channel_id=1, source_target_pairs={{16,0},{32,16},{48,32},{64,48},{80,64},{96,80},{112,96},{128,112},... | collective-permute-start | bytes 1572872 | tf_op jit(solution)/shard_map/ppermute | solution.py:10
  69.8 14.7 %collective-permute-start.13 = (f32[9,64,256]{2,1,0:T(8,128)S(1)}, f32[9,64,256]{2,1,0:T(8,128)S(1)}, u32[]{:S(2)}, u32[]{:S(2)}) collective-permute-start(f32[9,64,256]{2,1,0:T(8,128)S(1)} %constant_dynamic-slice_fusion.6), channel_id=1, source_target_pairs={{0,64},{16,80},{32,96},{48,112},{64,0},{80,16},{96,32},{112,48},{1... | collective-permute-start | bytes 1769480 | tf_op jit(solution)/shard_map/ppermute | solution.py:30
  73.1 18.3 %collective-permute-start.10 = (f32[9,64,256]{2,1,0:T(8,128)S(1)}, f32[9,64,256]{2,1,0:T(8,128)S(1)}, u32[]{:S(2)}, u32[]{:S(2)}) collective-permute-start(f32[9,64,256]{2,1,0:T(8,128)S(1)} %constant_dynamic-slice_fusion.9), channel_id=1, source_target_pairs={{0,16},{16,0},{32,48},{48,32},{64,80},{80,64},{96,112},{112,96},{1... | collective-permute-start | bytes 1769480 | tf_op jit(solution)/shard_map/ppermute | solution.py:30
  75.2 17.3 %collective-permute-start.7 = (f32[9,64,256]{2,1,0:T(8,128)S(1)}, f32[9,64,256]{2,1,0:T(8,128)S(1)}, u32[]{:S(2)}, u32[]{:S(2)}) collective-permute-start(f32[9,64,256]{2,1,0:T(8,128)S(1)} %constant_dynamic-slice_fusion.12), channel_id=1, source_target_pairs={{0,2},{2,0},{4,6},{6,4},{8,10},{10,8},{12,14},{14,12},{1,3},{3,1},... | collective-permute-start | bytes 1769480 | tf_op jit(solution)/shard_map/ppermute | solution.py:30
  78.9 13.9 %collective-permute-start.6 = (bf16[1,4,1,64,256]{4,3,2,1,0:T(8,128)(2,1)S(1)}, bf16[1,4,1,64,256]{4,3,2,1,0:T(8,128)(2,1)S(1)}, u32[]{:S(2)}, u32[]{:S(2)}) collective-permute-start(bf16[1,4,1,64,256]{4,3,2,1,0:T(8,128)(2,1)S(1)} %get-tuple-element.26), channel_id=1, source_target_pairs={{1,0},{3,2},{5,4},{7,6},{9,8},{11,10},{13,12},{15,14},{17,16},{19,... | collective-permute-start | bytes 393224 | tf_op jit(solution)/shard_map/ppermute | solution.py:20
  81.6 11.2 %collective-permute-start.5 = (bf16[1,4,1,64,256]{4,3,2,1,0:T(8,128)(2,1)S(1)}, bf16[1,4,1,64,256]{4,3,2,1,0:T(8,128)(2,1)S(1)}, u32[]{:S(2)}, u32[]{:S(2)}) collective-permute-start(bf16[1,4,1,64,256]{4,3,2,1,0:T(8,128)(2,1)S(1)} %get-tuple-element.25), channel_id=1, source_target_pairs={{0,1},{2,3},{4,5},{6,7},{8,9},{10,11},{12,13},{14,15},{16,17},{18,... | collective-permute-start | bytes 393224 | tf_op jit(solution)/shard_map/ppermute | solution.py:17
  84.6 12.7 %collective-permute-start.14 = (f32[9,32,256]{2,1,0:T(8,128)S(1)}, f32[9,32,256]{2,1,0:T(8,128)S(1)}, u32[]{:S(2)}, u32[]{:S(2)}) collective-permute-start(f32[9,32,256]{2,1,0:T(8,128)S(1)} %constant_dynamic-slice_fusion.5), channel_id=1, source_target_pairs={{0,2},{2,0},{4,6},{6,4},{8,10},{10,8},{12,14},{14,12},{1,3},{3,1},... | collective-permute-start | bytes 884744 | tf_op jit(solution)/shard_map/ppermute | solution.py:30
  91.6 8.3 %collective-permute-start.11 = (f32[9,32,256]{2,1,0:T(8,128)S(1)}, f32[9,32,256]{2,1,0:T(8,128)S(1)}, u32[]{:S(2)}, u32[]{:S(2)}) collective-permute-start(f32[9,32,256]{2,1,0:T(8,128)S(1)} %constant_dynamic-slice_fusion.8), channel_id=1, source_target_pairs={{0,64},{16,80},{32,96},{48,112},{64,0},{80,16},{96,32},{112,48},{1... | collective-permute-start | bytes 884744 | tf_op jit(solution)/shard_map/ppermute | solution.py:30
  92.7 9.0 %collective-permute-start.8 = (f32[9,32,256]{2,1,0:T(8,128)S(1)}, f32[9,32,256]{2,1,0:T(8,128)S(1)}, u32[]{:S(2)}, u32[]{:S(2)}) collective-permute-start(f32[9,32,256]{2,1,0:T(8,128)S(1)} %constant_dynamic-slice_fusion.11), channel_id=1, source_target_pairs={{0,16},{16,0},{32,48},{48,32},{64,80},{80,64},{96,112},{112,96},{1... | collective-permute-start | bytes 884744 | tf_op jit(solution)/shard_map/ppermute | solution.py:30
  95.5 0.6 copy-start.1
  97.4 6.3 %collective-permute-start.15 = (f32[9,16,256]{2,1,0:T(8,128)S(1)}, f32[9,16,256]{2,1,0:T(8,128)S(1)}, u32[]{:S(2)}, u32[]{:S(2)}) collective-permute-start(f32[9,16,256]{2,1,0:T(8,128)S(1)} %constant_dynamic-slice_fusion.4), channel_id=1, source_target_pairs={{0,16},{16,0},{32,48},{48,32},{64,80},{80,64},{96,112},{112,96},{1... | collective-permute-start | bytes 442376 | tf_op jit(solution)/shard_map/ppermute | solution.py:30
  99.9 4.6 %collective-permute-start.12 = (f32[9,16,256]{2,1,0:T(8,128)S(1)}, f32[9,16,256]{2,1,0:T(8,128)S(1)}, u32[]{:S(2)}, u32[]{:S(2)}) collective-permute-start(f32[9,16,256]{2,1,0:T(8,128)S(1)} %constant_dynamic-slice_fusion.7), channel_id=1, source_target_pairs={{0,2},{2,0},{4,6},{6,4},{8,10},{10,8},{12,14},{14,12},{1,3},{3,1},... | collective-permute-start | bytes 442376 | tf_op jit(solution)/shard_map/ppermute | solution.py:30
  101.7 4.4 %collective-permute-start.9 = (f32[9,16,256]{2,1,0:T(8,128)S(1)}, f32[9,16,256]{2,1,0:T(8,128)S(1)}, u32[]{:S(2)}, u32[]{:S(2)}) collective-permute-start(f32[9,16,256]{2,1,0:T(8,128)S(1)} %constant_dynamic-slice_fusion.10), channel_id=1, source_target_pairs={{0,64},{16,80},{32,96},{48,112},{64,0},{80,16},{96,32},{112,48},{1... | collective-permute-start | bytes 442376 | tf_op jit(solution)/shard_map/ppermute | solution.py:30
  106.2 8.2 %collective-permute-start.16 = (f32[3,9,8,256]{3,2,1,0:T(8,128)S(1)}, f32[3,9,8,256]{3,2,1,0:T(8,128)S(1)}, u32[]{:S(2)}, u32[]{:S(2)}) collective-permute-start(f32[3,9,8,256]{3,2,1,0:T(8,128)S(1)} %constant_dynamic-slice_fusion.3), channel_id=1, source_target_pairs={{0,32},{16,48},{32,0},{48,16},{64,96},{80,112},{96,64},{112,80},{1... | collective-permute-start | bytes 663560 | tf_op jit(solution)/shard_map/ppermute | solution.py:30
  114.5 5.5 %collective-permute-start.17 = (f32[3,9,4,256]{3,2,1,0:T(4,128)S(1)}, f32[3,9,4,256]{3,2,1,0:T(4,128)S(1)}, u32[]{:S(2)}, u32[]{:S(2)}) collective-permute-start(f32[3,9,4,256]{3,2,1,0:T(4,128)S(1)} %constant_dynamic-slice_fusion.2), channel_id=1, source_target_pairs={{0,128},{16,144},{32,160},{48,176},{64,192},{80,208},{96,224},{112... | collective-permute-start | bytes 331784 | tf_op jit(solution)/shard_map/ppermute | solution.py:30
  120.0 5.2 %collective-permute-start.18 = (f32[3,9,2,256]{3,2,1,0:T(2,128)S(1)}, f32[3,9,2,256]{3,2,1,0:T(2,128)S(1)}, u32[]{:S(2)}, u32[]{:S(2)}) collective-permute-start(f32[3,9,2,256]{3,2,1,0:T(2,128)S(1)} %constant_dynamic-slice_fusion.1), channel_id=1, source_target_pairs={{0,4},{2,6},{4,0},{6,2},{8,12},{10,14},{12,8},{14,10},{1,5},{3,7},... | collective-permute-start | bytes 165896 | tf_op jit(solution)/shard_map/ppermute | solution.py:30
  125.3 6.9 %collective-permute-start.19 = (f32[3,9,1,256]{3,2,1,0:T(1,128)S(1)}, f32[3,9,1,256]{3,2,1,0:T(1,128)S(1)}, u32[]{:S(2)}, u32[]{:S(2)}) collective-permute-start(f32[3,9,1,256]{3,2,1,0:T(1,128)S(1)} %constant_dynamic-slice_fusion), channel_id=1, source_target_pairs={{0,8},{2,10},{4,12},{6,14},{8,0},{10,2},{12,4},{14,6},{1,9},{3,11}... | collective-permute-start | bytes 82952 | tf_op jit(solution)/shard_map/ppermute | solution.py:30
  132.2 26.0 %collective-permute-start.22 = (f32[9,1,256]{2,1,0:T(1,128)S(1)}, f32[9,1,256]{2,1,0:T(1,128)S(1)}, u32[]{:S(2)}, u32[]{:S(2)}) collective-permute-start(f32[9,1,256]{2,1,0:T(1,128)S(1)} %get-tuple-element.28), channel_id=1, source_target_pairs={{0,0},{1,128},{2,32},{3,160},{4,2},{5,130},{6,34},{7,162},{8,1},{9... | collective-permute-start | bytes 27656 | tf_op jit(solution)/shard_map/ppermute | solution.py:86
  143.1 15.1 %collective-permute-start.21 = (f32[9,1,256]{2,0,1:T(8,128)S(1)}, f32[9,1,256]{2,0,1:T(8,128)S(1)}, u32[]{:S(2)}, u32[]{:S(2)}) collective-permute-start(f32[9,1,256]{2,0,1:T(8,128)S(1)} %bitcast.388), channel_id=1, source_target_pairs={{0,0},{1,128},{2,16},{3,144},{4,2},{5,130},{6,18},{7,146},{8,1},{9... | collective-permute-start | bytes 27656 | tf_op jit(solution)/shard_map/ppermute | solution.py:86
  154.9 9.6 %collective-permute-start.20 = (f32[9,1,256]{2,0,1:T(8,128)S(1)}, f32[9,1,256]{2,0,1:T(8,128)S(1)}, u32[]{:S(2)}, u32[]{:S(2)}) collective-permute-start(f32[9,1,256]{2,0,1:T(8,128)S(1)} %bitcast.389), channel_id=1, source_target_pairs={{0,0},{1,128},{2,64},{3,192},{4,2},{5,130},{6,66},{7,194},{8,1},{9... | collective-permute-start | bytes 27656 | tf_op jit(solution)/shard_map/ppermute | solution.py:86

commit v7 on v6

--- a/solution.py
+++ b/solution.py
@@ -28,6 +28,20 @@
     give = lax.dynamic_slice_in_dim(x, (1 - bit) * size, size, axis=dim)
     pairs = [(i, i ^ flip) for i in range(lax.axis_size(axis))]
     return keep + lax.ppermute(give, axis, pairs)
+
+
+def quarter(x, dim, first, second):
+    axis, high = first
+    low = second[1]
+    size = x.shape[dim] // 4
+    where = lax.axis_index(axis)
+    mine = ((where // high) % 2) * 2 + (where // low) % 2
+    out = lax.dynamic_slice_in_dim(x, mine * size, size, axis=dim)
+    for pattern, flip in ((2, high), (1, low), (3, high + low)):
+        piece = lax.dynamic_slice_in_dim(x, jnp.bitwise_xor(mine, pattern) * size, size, axis=dim)
+        pairs = [(i, i ^ flip) for i in range(lax.axis_size(axis))]
+        out = out + lax.ppermute(piece, axis, pairs)
+    return out
 
 
 def bits_of(n):
@@ -78,8 +92,14 @@
         parts.append(part)
         orders.append(order + rest)
     joined = jnp.stack(parts)
-    for axis, flip in rest:
-        joined = halve(joined, 2, axis, flip)
+    steps = list(rest)
+    while steps:
+        if len(steps) > 1 and steps[0][0] == steps[1][0]:
+            joined = quarter(joined, 2, steps[0], steps[1])
+            steps = steps[2:]
+        else:
+            joined = halve(joined, 2, *steps[0])
+            steps = steps[1:]
     parts = []
     for n, order in enumerate(orders):
         names, pairs = owner_pairs(order, sizes)

time: 168 us -> 161 us (0.958); the launches traced: 165 us -> 160 us
  starting transfers between devices: 70 us -> 63.8 us
    ppermute x13 -> x9, starting transfers between devices: 26.9 us -> 10.1 us  [halve(): return keep + lax.ppermute(give, axis, pairs)]
    ppermute x0 -> x6, starting transfers between devices: none -> 15.7 us  [quarter(): out = out + lax.ppermute(piece, axis, pairs)]
    ppermute x0 -> x6, waiting for transfers between devices: none -> 8.92 us  [quarter(): out = out + lax.ppermute(piece, axis, pairs)]
    ppermute x13 -> x9, waiting for transfers between devices: 17.7 us -> 10.1 us  [halve(): return keep + lax.ppermute(give, axis, pairs)]
    ppermute x3, starting transfers between devices: 24.5 us -> 19.3 us  [reduce_weight_grad(): parts.append(lax.ppermute(joined[n], names, pairs).reshape(per, outs))]
  transfers between devices with their start and end apart: 23 -> 25, of which waited for: 12 -> 10; matrix products, arithmetic and copies ran while one was open for 18% -> 19% of each run, Pallas kernels for 0% -> 0%
where the time goes in v7:
time: 161 us; the launch traced here: 160 us
  starting transfers between devices  63.8 us (40%)
  waiting for transfers between devices  27.1 us (17%)
  blocking collectives  23.7 us (15%)
  local copies, waits for them, and re-layouts  19.2 us (12%)
  matrix products  17.3 us (11%)
  other arithmetic  7.11 us (4%)
  between operations  2.23 us (1%)
    unnamed x1, blocking collectives  23.7 us
    ppermute x3, starting transfers between devices, reduce_weight_grad(): parts.append(lax.ppermute(joined[n], names, pairs).reshape(per, outs))  19.3 us
    ppermute x6, starting transfers between devices, quarter(): out = out + lax.ppermute(piece, axis, pairs)  15.7 us
    ppermute x9, waiting for transfers between devices, halve(): return keep + lax.ppermute(give, axis, pairs)  10.1 us
    ppermute x9, starting transfers between devices, halve(): return keep + lax.ppermute(give, axis, pairs)  10.1 us
    ppermute x6, waiting for transfers between devices, quarter(): out = out + lax.ppermute(piece, axis, pairs)  8.92 us
    ppermute x2, starting transfers between devices, passed_along(): return lax.ppermute(value, axis, pairs)  8.66 us
    unnamed x21, local copies, waits for them, and re-layouts  6.37 us
  transfers between devices with their start and end apart: 25, of which 10 were waited for; matrix products, arithmetic and copies ran while one was open for 19% of the time, Pallas kernels for 0%

profile of v7, /device:TPU:25, one launch (start us, length us, event | category | flops | bytes accessed | tf_op | source)
XLA Modules:
  0.0 160.4 jit_solution(7325467733116790402)
XLA Ops:
  0.6 3.7 %collective-permute-start.1 = (bf16[1,2,8,64,256]{4,3,2,1,0:T(8,128)(2,1)}, bf16[1,2,8,64,256]{4,3,2,1,0:T(8,128)(2,1)}, u32[]{:S(2)}, u32[]{:S(2)}) collective-permute-start(bf16[1,2,8,64,256]{4,3,2,1,0:T(8,128)(2,1)} %param.4), channel_id=1, source_target_pairs={{0,17},{1,16},{16,33},{17,32},{32,49},{33,48},{48,65},{49,64},{64,... | collective-permute-start | bytes 1572872 | tf_op jit(solution)/shard_map/ppermute | solution.py:143
  4.4 3.1 %collective-permute-start = (bf16[1,2,8,64,256]{4,3,2,1,0:T(8,128)(2,1)}, bf16[1,2,8,64,256]{4,3,2,1,0:T(8,128)(2,1)}, u32[]{:S(2)}, u32[]{:S(2)}) collective-permute-start(bf16[1,2,8,64,256]{4,3,2,1,0:T(8,128)(2,1)} %param.4), channel_id=1, source_target_pairs={{0,16},{16,32},{32,48},{48,64},{64,80},{80,96},{96,112},{112,128},... | collective-permute-start | bytes 1572872 | tf_op jit(solution)/shard_map/ppermute | solution.py:10
  7.6 1.3 dynamic-slice
  9.5 0.8 bitcast_dynamic-update-slice_fusion
  10.3 23.7 %all-reduce.7 = s32[32]{0:T(128)S(1)} all-reduce(s32[32]{0:T(128)S(1)} %bitcast_dynamic-update-slice_fusion), channel_id=1, replica_groups=mesh['group'=16,'dp'=8,'space'=2] {'group'}, use_global_device_ids=true, to_apply=%add.7 | all-reduce | flops 32 | bytes 256
  34.7 0.7 fusion.108
  35.4 4.3 %copy.34 = bf16[3,3,3,256,256]{3,4,2,1,0:T(8,128)(2,1)S(1)} copy(bf16[3,3,3,256,256]{4,3,2,1,0:T(8,128)(2,1)} %bitcast.369) | data formatting | bytes 7077888 | tf_op jit(solution)/shard_map/reshape | solution.py:199
  39.8 1.1 constant_dynamic-update-slice_fusion.1
  40.9 1.1 constant_dynamic-update-slice_fusion
  42.0 1.1 constant_dynamic-update-slice_fusion.3
  43.1 1.1 constant_dynamic-update-slice_fusion.2
  45.1 0.9 pad_slice_fusion.3
  46.4 1.6 %copy-done = bf16[6912,256]{1,0:T(8,128)(2,1)S(1)} copy-done((bf16[6912,256]{1,0:T(8,128)(2,1)S(1)}, bf16[6912,256]{1,0:T(8,128)(2,1)}, u32[]{:S(2)}) %copy-start) | copy-done | bytes 3538968
  48.6 0.6 fusion.14
  51.5 0.6 fusion.52
  52.1 0.6 fusion.49
  53.2 1.0 fusion.94
  54.1 1.1 fusion.104
  55.2 2.2 %collective-permute-start.3 = (bf16[1,2,8,64,256]{4,3,2,1,0:T(8,128)(2,1)S(1)}, bf16[1,2,8,64,256]{4,3,2,1,0:T(8,128)(2,1)S(1)}, u32[]{:S(2)}, u32[]{:S(2)}) collective-permute-start(bf16[1,2,8,64,256]{4,3,2,1,0:T(8,128)(2,1)S(1)} %get-tuple-element.4), channel_id=1, source_target_pairs={{0,1},{1,0},{2,3},{3,2},{4,5},{5,4},{6,7},{7,6},{8,9},{9,8},{10,11... | collective-permute-start | bytes 1572872 | tf_op jit(solution)/shard_map/ppermute | solution.py:176
  57.6 1.3 pad_slice_fusion.1
  59.0 0.6 pad_maximum_fusion.2
  59.7 2.3 %fusion.116 = (bf16[2,2,8,64,384]{4,3,2,1,0:T(8,128)(2,1)S(1)}, bf16[2,2,8,64,384]{4,3,2,1,0:T(8,128)(2,1)S(1)}, bf16[2,2,8,64,384]{4,3,2,1,0:T(8,128)(2,1)S(1)}...) fusion(bf16[2,4,10,64,384]{4,3,2,1,0:T(8,128)(2,1)S(1)} %pad_ma, ...), kind=kLoop, calls=%fused_computation.218 | loop fusion | bytes 28311552 | tf_op jit(solution)/shard_map/slice | solution.py:190
  62.0 5.5 %collective-permute-start.4 = (bf16[1,2,8,64,256]{4,3,2,1,0:T(8,128)(2,1)S(1)}, bf16[1,2,8,64,256]{4,3,2,1,0:T(8,128)(2,1)S(1)}, u32[]{:S(2)}, u32[]{:S(2)}) collective-permute-start(bf16[1,2,8,64,256]{4,3,2,1,0:T(8,128)(2,1)S(1)} %get-tuple-element.4), channel_id=1, source_target_pairs={{16,0},{32,16},{48,32},{64,48},{80,64},{96,80},{112,96},{128,112},... | collective-permute-start | bytes 1572872 | tf_op jit(solution)/shard_map/ppermute | solution.py:10
  67.8 0.6 fusion.91
  68.5 0.6 fusion.88
  69.1 0.6 fusion.85
  69.8 1.4 collective-permute-start.13
  71.2 0.6 fusion.82
  71.8 0.6 fusion.79
  72.4 0.6 fusion.76
  73.3 0.6 fusion.73
  73.9 0.6 fusion.70
  74.5 0.6 fusion.67
  75.3 1.7 %collective-permute-start.7 = (f32[9,64,256]{2,1,0:T(8,128)S(1)}, f32[9,64,256]{2,1,0:T(8,128)S(1)}, u32[]{:S(2)}, u32[]{:S(2)}) collective-permute-start(f32[9,64,256]{2,1,0:T(8,128)S(1)} %constant_dynamic-slice_fusion.14), channel_id=1, source_target_pairs={{0,2},{2,0},{4,6},{6,4},{8,10},{10,8},{12,14},{14,12},{1,3},{3,1},... | collective-permute-start | bytes 1769480 | tf_op jit(solution)/shard_map/ppermute | solution.py:30
  77.1 1.8 %collective-permute-done.4 = bf16[1,2,8,64,256]{4,3,2,1,0:T(8,128)(2,1)S(1)} collective-permute-done((bf16[1,2,8,64,256]{4,3,2,1,0:T(8,128)(2,1)S(1)}, bf16[1,2,8,64,256]{4,3,2,1,0:T(8,128)(2,1)S(1)}, u32[]{:S(2)}, u32[]{:S(2)}) %collective-permute-start.4) | collective-permute-done | bytes 524320 | tf_op jit(solution)/shard_map/ppermute | solution.py:10
  78.9 2.7 %collective-permute-start.6 = (bf16[1,4,1,64,256]{4,3,2,1,0:T(8,128)(2,1)S(1)}, bf16[1,4,1,64,256]{4,3,2,1,0:T(8,128)(2,1)S(1)}, u32[]{:S(2)}, u32[]{:S(2)}) collective-permute-start(bf16[1,4,1,64,256]{4,3,2,1,0:T(8,128)(2,1)S(1)} %get-tuple-element.26), channel_id=1, source_target_pairs={{1,0},{3,2},{5,4},{7,6},{9,8},{11,10},{13,12},{15,14},{17,16},{19,... | collective-permute-start | bytes 393224 | tf_op jit(solution)/shard_map/ppermute | solution.py:20
  81.7 1.3 collective-permute-start.5
  83.0 1.5 collective-permute-done.13
  84.6 1.7 %collective-permute-start.14 = (f32[9,32,256]{2,1,0:T(8,128)S(1)}, f32[9,32,256]{2,1,0:T(8,128)S(1)}, u32[]{:S(2)}, u32[]{:S(2)}) collective-permute-start(f32[9,32,256]{2,1,0:T(8,128)S(1)} %constant_dynamic-slice_fusion.7), channel_id=1, source_target_pairs={{0,2},{2,0},{4,6},{6,4},{8,10},{10,8},{12,14},{14,12},{1,3},{3,1},... | collective-permute-start | bytes 884744 | tf_op jit(solution)/shard_map/ppermute | solution.py:30
  86.4 5.1 %collective-permute-done.10 = f32[9,64,256]{2,1,0:T(8,128)S(1)} collective-permute-done((f32[9,64,256]{2,1,0:T(8,128)S(1)}, f32[9,64,256]{2,1,0:T(8,128)S(1)}, u32[]{:S(2)}, u32[]{:S(2)}) %collective-permute-start.10) | collective-permute-done | bytes 589856 | tf_op jit(solution)/shard_map/ppermute | solution.py:30
  91.6 1.0 collective-permute-start.11
  92.9 0.8 fusion.41
  93.7 0.9 fusion.117
  95.5 0.6 fusion.5
  97.4 0.6 fusion.63
  98.0 0.6 fusion.60
  98.8 1.5 collective-permute-start.15
  100.4 1.7 %collective-permute-start.12 = (f32[9,16,256]{2,1,0:T(8,128)S(1)}, f32[9,16,256]{2,1,0:T(8,128)S(1)}, u32[]{:S(2)}, u32[]{:S(2)}) collective-permute-start(f32[9,16,256]{2,1,0:T(8,128)S(1)} %constant_dynamic-slice_fusion.9), channel_id=1, source_target_pairs={{0,2},{2,0},{4,6},{6,4},{8,10},{10,8},{12,14},{14,12},{1,3},{3,1},... | collective-permute-start | bytes 442376 | tf_op jit(solution)/shard_map/ppermute | solution.py:30
  102.2 0.9 collective-permute-start.9
  103.2 1.7 %collective-permute-done.12 = f32[9,16,256]{2,1,0:T(8,128)S(1)} collective-permute-done((f32[9,16,256]{2,1,0:T(8,128)S(1)}, f32[9,16,256]{2,1,0:T(8,128)S(1)}, u32[]{:S(2)}, u32[]{:S(2)}) %collective-permute-start.12) | collective-permute-done | bytes 147488 | tf_op jit(solution)/shard_map/ppermute | solution.py:30
  104.9 1.6 collective-permute-done.9
  106.7 7.5 %collective-permute-start.18 = (f32[3,9,4,256]{3,2,1,0:T(4,128)S(1)}, f32[3,9,4,256]{3,2,1,0:T(4,128)S(1)}, u32[]{:S(2)}, u32[]{:S(2)}) collective-permute-start(f32[3,9,4,256]{3,2,1,0:T(4,128)S(1)} %get-tuple-element.28), channel_id=1, source_target_pairs={{0,160},{16,176},{32,128},{48,144},{64,224},{80,240},{96,192},{112... | collective-permute-start | bytes 331784 | tf_op jit(solution)/shard_map/ppermute | solution.py:43
  115.1 1.2 collective-permute-done.18
  116.3 3.8 %collective-permute-done.17 = f32[3,9,4,256]{3,2,1,0:T(4,128)S(1)} collective-permute-done((f32[3,9,4,256]{3,2,1,0:T(4,128)S(1)}, f32[3,9,4,256]{3,2,1,0:T(4,128)S(1)}, u32[]{:S(2)}, u32[]{:S(2)}) %collective-permute-start.17) | collective-permute-done | bytes 110624 | tf_op jit(solution)/shard_map/ppermute | solution.py:43
  120.3 5.7 %collective-permute-start.21 = (f32[3,9,1,256]{3,2,1,0:T(1,128)S(1)}, f32[3,9,1,256]{3,2,1,0:T(1,128)S(1)}, u32[]{:S(2)}, u32[]{:S(2)}) collective-permute-start(f32[3,9,1,256]{3,2,1,0:T(1,128)S(1)} %get-tuple-element.31), channel_id=1, source_target_pairs={{0,12},{2,14},{4,8},{6,10},{8,4},{10,6},{12,0},{14,2},{1,13},{3,15... | collective-permute-start | bytes 82952 | tf_op jit(solution)/shard_map/ppermute | solution.py:43
  126.0 1.0 collective-permute-start.20
  127.0 1.2 collective-permute-start.19
  128.8 4.0 %collective-permute-done.20 = f32[3,9,1,256]{3,2,1,0:T(1,128)S(1)} collective-permute-done((f32[3,9,1,256]{3,2,1,0:T(1,128)S(1)}, f32[3,9,1,256]{3,2,1,0:T(1,128)S(1)}, u32[]{:S(2)}, u32[]{:S(2)}) %collective-permute-start.20) | collective-permute-done | bytes 27680 | tf_op jit(solution)/shard_map/ppermute | solution.py:43
  132.8 7.3 %collective-permute-start.24 = (f32[9,1,256]{2,1,0:T(1,128)S(1)}, f32[9,1,256]{2,1,0:T(1,128)S(1)}, u32[]{:S(2)}, u32[]{:S(2)}) collective-permute-start(f32[9,1,256]{2,1,0:T(1,128)S(1)} %get-tuple-element.34), channel_id=1, source_target_pairs={{0,0},{1,128},{2,32},{3,160},{4,2},{5,130},{6,34},{7,162},{8,1},{9... | collective-permute-start | bytes 27656 | tf_op jit(solution)/shard_map/ppermute | solution.py:106
  140.1 10.0 %collective-permute-start.23 = (f32[9,1,256]{2,0,1:T(8,128)S(1)}, f32[9,1,256]{2,0,1:T(8,128)S(1)}, u32[]{:S(2)}, u32[]{:S(2)}) collective-permute-start(f32[9,1,256]{2,0,1:T(8,128)S(1)} %bitcast.388), channel_id=1, source_target_pairs={{0,0},{1,128},{2,16},{3,144},{4,2},{5,130},{6,18},{7,146},{8,1},{9... | collective-permute-start | bytes 27656 | tf_op jit(solution)/shard_map/ppermute | solution.py:106
  150.2 1.9 %collective-permute-start.22 = (f32[9,1,256]{2,0,1:T(8,128)S(1)}, f32[9,1,256]{2,0,1:T(8,128)S(1)}, u32[]{:S(2)}, u32[]{:S(2)}) collective-permute-start(f32[9,1,256]{2,0,1:T(8,128)S(1)} %bitcast.389), channel_id=1, source_target_pairs={{0,0},{1,128},{2,64},{3,192},{4,2},{5,130},{6,66},{7,194},{8,1},{9... | collective-permute-start | bytes 27656 | tf_op jit(solution)/shard_map/ppermute | solution.py:106
  152.1 1.4 fusion.66
  153.6 6.2 %collective-permute-done.22 = f32[9,1,256]{2,0,1:T(8,128)S(1)} collective-permute-done((f32[9,1,256]{2,0,1:T(8,128)S(1)}, f32[9,1,256]{2,0,1:T(8,128)S(1)}, u32[]{:S(2)}, u32[]{:S(2)}) %collective-permute-start.22) | collective-permute-done | bytes 9248 | tf_op jit(solution)/shard_map/ppermute | solution.py:106
  159.8 0.6 pad_maximum_fusion.8
  (94 shorter events, 11.5 us)
Async XLA Ops:
  0.6 41.4 %collective-permute-start.1 = (bf16[1,2,8,64,256]{4,3,2,1,0:T(8,128)(2,1)}, bf16[1,2,8,64,256]{4,3,2,1,0:T(8,128)(2,1)}, u32[]{:S(2)}, u32[]{:S(2)}) collective-permute-start(bf16[1,2,8,64,256]{4,3,2,1,0:T(8,128)(2,1)} %param.4), channel_id=1, source_target_pairs={{0,17},{1,16},{16,33},{17,32},{32,49},{33,48},{48,65},{49,64},{64,... | collective-permute-start | bytes 1572872 | tf_op jit(solution)/shard_map/ppermute | solution.py:143
  4.3 38.8 %collective-permute-start.2 = (bf16[1,2,8,64,256]{4,3,2,1,0:T(8,128)(2,1)}, bf16[1,2,8,64,256]{4,3,2,1,0:T(8,128)(2,1)}, u32[]{:S(2)}, u32[]{:S(2)}) collective-permute-start(bf16[1,2,8,64,256]{4,3,2,1,0:T(8,128)(2,1)} %param.4), channel_id=1, source_target_pairs={{0,1},{1,0},{2,3},{3,2},{4,5},{5,4},{6,7},{7,6},{8,9},{9,8},{10,11... | collective-permute-start | bytes 1572872 | tf_op jit(solution)/shard_map/ppermute | solution.py:140
  4.4 35.4 %collective-permute-start = (bf16[1,2,8,64,256]{4,3,2,1,0:T(8,128)(2,1)}, bf16[1,2,8,64,256]{4,3,2,1,0:T(8,128)(2,1)}, u32[]{:S(2)}, u32[]{:S(2)}) collective-permute-start(bf16[1,2,8,64,256]{4,3,2,1,0:T(8,128)(2,1)} %param.4), channel_id=1, source_target_pairs={{0,16},{16,32},{32,48},{48,64},{64,80},{80,96},{96,112},{112,128},... | collective-permute-start | bytes 1572872 | tf_op jit(solution)/shard_map/ppermute | solution.py:10
  46.0 2.0 %copy-start = (bf16[6912,256]{1,0:T(8,128)(2,1)S(1)}, bf16[6912,256]{1,0:T(8,128)(2,1)}, u32[]{:S(2)}) copy-start(bf16[6912,256]{1,0:T(8,128)(2,1)} %param.6) | copy-start | bytes 10616836
  52.1 1.0 copy-start.5
  55.2 6.7 %collective-permute-start.3 = (bf16[1,2,8,64,256]{4,3,2,1,0:T(8,128)(2,1)S(1)}, bf16[1,2,8,64,256]{4,3,2,1,0:T(8,128)(2,1)S(1)}, u32[]{:S(2)}, u32[]{:S(2)}) collective-permute-start(bf16[1,2,8,64,256]{4,3,2,1,0:T(8,128)(2,1)S(1)} %get-tuple-element.4), channel_id=1, source_target_pairs={{0,1},{1,0},{2,3},{3,2},{4,5},{5,4},{6,7},{7,6},{8,9},{9,8},{10,11... | collective-permute-start | bytes 1572872 | tf_op jit(solution)/shard_map/ppermute | solution.py:176
  59.6 7.9 %copy-start.2 = (bf16[2]{0:T(256)(128)(2,1)S(1)}, bf16[2]{0:T(256)(128)(2,1)}, u32[]{:S(2)}) copy-start(bf16[2]{0:T(256)(128)(2,1)} %get-tuple-element.39) | copy-start | bytes 16
  59.6 7.9 %copy-start.3 = (bf16[2]{0:T(256)(128)(2,1)S(1)}, bf16[2]{0:T(256)(128)(2,1)}, u32[]{:S(2)}) copy-start(bf16[2]{0:T(256)(128)(2,1)} %get-tuple-element.41) | copy-start | bytes 16
  59.6 7.9 %copy-start.4 = (bf16[2]{0:T(256)(128)(2,1)S(1)}, bf16[2]{0:T(256)(128)(2,1)}, u32[]{:S(2)}) copy-start(bf16[2]{0:T(256)(128)(2,1)} %get-tuple-element.42) | copy-start | bytes 16
  62.0 16.9 %collective-permute-start.4 = (bf16[1,2,8,64,256]{4,3,2,1,0:T(8,128)(2,1)S(1)}, bf16[1,2,8,64,256]{4,3,2,1,0:T(8,128)(2,1)S(1)}, u32[]{:S(2)}, u32[]{:S(2)}) collective-permute-start(bf16[1,2,8,64,256]{4,3,2,1,0:T(8,128)(2,1)S(1)} %get-tuple-element.4), channel_id=1, source_target_pairs={{16,0},{32,16},{48,32},{64,48},{80,64},{96,80},{112,96},{128,112},... | collective-permute-start | bytes 1572872 | tf_op jit(solution)/shard_map/ppermute | solution.py:10
  69.8 14.7 %collective-permute-start.13 = (f32[9,64,256]{2,1,0:T(8,128)S(1)}, f32[9,64,256]{2,1,0:T(8,128)S(1)}, u32[]{:S(2)}, u32[]{:S(2)}) collective-permute-start(f32[9,64,256]{2,1,0:T(8,128)S(1)} %constant_dynamic-slice_fusion.8), channel_id=1, source_target_pairs={{0,64},{16,80},{32,96},{48,112},{64,0},{80,16},{96,32},{112,48},{1... | collective-permute-start | bytes 1769480 | tf_op jit(solution)/shard_map/ppermute | solution.py:30
  73.2 18.3 %collective-permute-start.10 = (f32[9,64,256]{2,1,0:T(8,128)S(1)}, f32[9,64,256]{2,1,0:T(8,128)S(1)}, u32[]{:S(2)}, u32[]{:S(2)}) collective-permute-start(f32[9,64,256]{2,1,0:T(8,128)S(1)} %constant_dynamic-slice_fusion.11), channel_id=1, source_target_pairs={{0,16},{16,0},{32,48},{48,32},{64,80},{80,64},{96,112},{112,96},{1... | collective-permute-start | bytes 1769480 | tf_op jit(solution)/shard_map/ppermute | solution.py:30
  75.3 17.3 %collective-permute-start.7 = (f32[9,64,256]{2,1,0:T(8,128)S(1)}, f32[9,64,256]{2,1,0:T(8,128)S(1)}, u32[]{:S(2)}, u32[]{:S(2)}) collective-permute-start(f32[9,64,256]{2,1,0:T(8,128)S(1)} %constant_dynamic-slice_fusion.14), channel_id=1, source_target_pairs={{0,2},{2,0},{4,6},{6,4},{8,10},{10,8},{12,14},{14,12},{1,3},{3,1},... | collective-permute-start | bytes 1769480 | tf_op jit(solution)/shard_map/ppermute | solution.py:30
  78.9 13.9 %collective-permute-start.6 = (bf16[1,4,1,64,256]{4,3,2,1,0:T(8,128)(2,1)S(1)}, bf16[1,4,1,64,256]{4,3,2,1,0:T(8,128)(2,1)S(1)}, u32[]{:S(2)}, u32[]{:S(2)}) collective-permute-start(bf16[1,4,1,64,256]{4,3,2,1,0:T(8,128)(2,1)S(1)} %get-tuple-element.26), channel_id=1, source_target_pairs={{1,0},{3,2},{5,4},{7,6},{9,8},{11,10},{13,12},{15,14},{17,16},{19,... | collective-permute-start | bytes 393224 | tf_op jit(solution)/shard_map/ppermute | solution.py:20
  81.7 11.2 %collective-permute-start.5 = (bf16[1,4,1,64,256]{4,3,2,1,0:T(8,128)(2,1)S(1)}, bf16[1,4,1,64,256]{4,3,2,1,0:T(8,128)(2,1)S(1)}, u32[]{:S(2)}, u32[]{:S(2)}) collective-permute-start(bf16[1,4,1,64,256]{4,3,2,1,0:T(8,128)(2,1)S(1)} %get-tuple-element.25), channel_id=1, source_target_pairs={{0,1},{2,3},{4,5},{6,7},{8,9},{10,11},{12,13},{14,15},{16,17},{18,... | collective-permute-start | bytes 393224 | tf_op jit(solution)/shard_map/ppermute | solution.py:17
  84.6 14.0 %collective-permute-start.14 = (f32[9,32,256]{2,1,0:T(8,128)S(1)}, f32[9,32,256]{2,1,0:T(8,128)S(1)}, u32[]{:S(2)}, u32[]{:S(2)}) collective-permute-start(f32[9,32,256]{2,1,0:T(8,128)S(1)} %constant_dynamic-slice_fusion.7), channel_id=1, source_target_pairs={{0,2},{2,0},{4,6},{6,4},{8,10},{10,8},{12,14},{14,12},{1,3},{3,1},... | collective-permute-start | bytes 884744 | tf_op jit(solution)/shard_map/ppermute | solution.py:30
  91.6 8.7 %collective-permute-start.11 = (f32[9,32,256]{2,1,0:T(8,128)S(1)}, f32[9,32,256]{2,1,0:T(8,128)S(1)}, u32[]{:S(2)}, u32[]{:S(2)}) collective-permute-start(f32[9,32,256]{2,1,0:T(8,128)S(1)} %constant_dynamic-slice_fusion.10), channel_id=1, source_target_pairs={{0,64},{16,80},{32,96},{48,112},{64,0},{80,16},{96,32},{112,48},{1... | collective-permute-start | bytes 884744 | tf_op jit(solution)/shard_map/ppermute | solution.py:30
  92.8 9.3 %collective-permute-start.8 = (f32[9,32,256]{2,1,0:T(8,128)S(1)}, f32[9,32,256]{2,1,0:T(8,128)S(1)}, u32[]{:S(2)}, u32[]{:S(2)}) collective-permute-start(f32[9,32,256]{2,1,0:T(8,128)S(1)} %constant_dynamic-slice_fusion.13), channel_id=1, source_target_pairs={{0,16},{16,0},{32,48},{48,32},{64,80},{80,64},{96,112},{112,96},{1... | collective-permute-start | bytes 884744 | tf_op jit(solution)/shard_map/ppermute | solution.py:30
  96.7 0.7 copy-start.1
  98.8 4.4 %collective-permute-start.15 = (f32[9,16,256]{2,1,0:T(8,128)S(1)}, f32[9,16,256]{2,1,0:T(8,128)S(1)}, u32[]{:S(2)}, u32[]{:S(2)}) collective-permute-start(f32[9,16,256]{2,1,0:T(8,128)S(1)} %constant_dynamic-slice_fusion.6), channel_id=1, source_target_pairs={{0,16},{16,0},{32,48},{48,32},{64,80},{80,64},{96,112},{112,96},{1... | collective-permute-start | bytes 442376 | tf_op jit(solution)/shard_map/ppermute | solution.py:30
  100.4 4.6 %collective-permute-start.12 = (f32[9,16,256]{2,1,0:T(8,128)S(1)}, f32[9,16,256]{2,1,0:T(8,128)S(1)}, u32[]{:S(2)}, u32[]{:S(2)}) collective-permute-start(f32[9,16,256]{2,1,0:T(8,128)S(1)} %constant_dynamic-slice_fusion.9), channel_id=1, source_target_pairs={{0,2},{2,0},{4,6},{6,4},{8,10},{10,8},{12,14},{14,12},{1,3},{3,1},... | collective-permute-start | bytes 442376 | tf_op jit(solution)/shard_map/ppermute | solution.py:30
  102.2 4.4 %collective-permute-start.9 = (f32[9,16,256]{2,1,0:T(8,128)S(1)}, f32[9,16,256]{2,1,0:T(8,128)S(1)}, u32[]{:S(2)}, u32[]{:S(2)}) collective-permute-start(f32[9,16,256]{2,1,0:T(8,128)S(1)} %constant_dynamic-slice_fusion.12), channel_id=1, source_target_pairs={{0,64},{16,80},{32,96},{48,112},{64,0},{80,16},{96,32},{112,48},{1... | collective-permute-start | bytes 442376 | tf_op jit(solution)/shard_map/ppermute | solution.py:30
  106.7 9.6 %collective-permute-start.18 = (f32[3,9,4,256]{3,2,1,0:T(4,128)S(1)}, f32[3,9,4,256]{3,2,1,0:T(4,128)S(1)}, u32[]{:S(2)}, u32[]{:S(2)}) collective-permute-start(f32[3,9,4,256]{3,2,1,0:T(4,128)S(1)} %get-tuple-element.28), channel_id=1, source_target_pairs={{0,160},{16,176},{32,128},{48,144},{64,224},{80,240},{96,192},{112... | collective-permute-start | bytes 331784 | tf_op jit(solution)/shard_map/ppermute | solution.py:43
  114.2 5.9 %collective-permute-start.17 = (f32[3,9,4,256]{3,2,1,0:T(4,128)S(1)}, f32[3,9,4,256]{3,2,1,0:T(4,128)S(1)}, u32[]{:S(2)}, u32[]{:S(2)}) collective-permute-start(f32[3,9,4,256]{3,2,1,0:T(4,128)S(1)} %get-tuple-element.29), channel_id=1, source_target_pairs={{0,128},{16,144},{32,160},{48,176},{64,192},{80,208},{96,224},{112... | collective-permute-start | bytes 331784 | tf_op jit(solution)/shard_map/ppermute | solution.py:43
  114.2 5.9 %collective-permute-start.16 = (f32[3,9,4,256]{3,2,1,0:T(4,128)S(1)}, f32[3,9,4,256]{3,2,1,0:T(4,128)S(1)}, u32[]{:S(2)}, u32[]{:S(2)}) collective-permute-start(f32[3,9,4,256]{3,2,1,0:T(4,128)S(1)} %get-tuple-element.27), channel_id=1, source_target_pairs={{0,32},{16,48},{32,0},{48,16},{64,96},{80,112},{96,64},{112,80},{1... | collective-permute-start | bytes 331784 | tf_op jit(solution)/shard_map/ppermute | solution.py:43
  120.3 8.5 %collective-permute-start.21 = (f32[3,9,1,256]{3,2,1,0:T(1,128)S(1)}, f32[3,9,1,256]{3,2,1,0:T(1,128)S(1)}, u32[]{:S(2)}, u32[]{:S(2)}) collective-permute-start(f32[3,9,1,256]{3,2,1,0:T(1,128)S(1)} %get-tuple-element.31), channel_id=1, source_target_pairs={{0,12},{2,14},{4,8},{6,10},{8,4},{10,6},{12,0},{14,2},{1,13},{3,15... | collective-permute-start | bytes 82952 | tf_op jit(solution)/shard_map/ppermute | solution.py:43
  126.0 6.7 %collective-permute-start.20 = (f32[3,9,1,256]{3,2,1,0:T(1,128)S(1)}, f32[3,9,1,256]{3,2,1,0:T(1,128)S(1)}, u32[]{:S(2)}, u32[]{:S(2)}) collective-permute-start(f32[3,9,1,256]{3,2,1,0:T(1,128)S(1)} %get-tuple-element.32), channel_id=1, source_target_pairs={{0,8},{2,10},{4,12},{6,14},{8,0},{10,2},{12,4},{14,6},{1,9},{3,11}... | collective-permute-start | bytes 82952 | tf_op jit(solution)/shard_map/ppermute | solution.py:43
  127.0 5.7 %collective-permute-start.19 = (f32[3,9,1,256]{3,2,1,0:T(1,128)S(1)}, f32[3,9,1,256]{3,2,1,0:T(1,128)S(1)}, u32[]{:S(2)}, u32[]{:S(2)}) collective-permute-start(f32[3,9,1,256]{3,2,1,0:T(1,128)S(1)} %get-tuple-element.30), channel_id=1, source_target_pairs={{0,4},{2,6},{4,0},{6,2},{8,12},{10,14},{12,8},{14,10},{1,5},{3,7},... | collective-permute-start | bytes 82952 | tf_op jit(solution)/shard_map/ppermute | solution.py:43
  132.8 20.8 %collective-permute-start.24 = (f32[9,1,256]{2,1,0:T(1,128)S(1)}, f32[9,1,256]{2,1,0:T(1,128)S(1)}, u32[]{:S(2)}, u32[]{:S(2)}) collective-permute-start(f32[9,1,256]{2,1,0:T(1,128)S(1)} %get-tuple-element.34), channel_id=1, source_target_pairs={{0,0},{1,128},{2,32},{3,160},{4,2},{5,130},{6,34},{7,162},{8,1},{9... | collective-permute-start | bytes 27656 | tf_op jit(solution)/shard_map/ppermute | solution.py:106
  140.1 13.4 %collective-permute-start.23 = (f32[9,1,256]{2,0,1:T(8,128)S(1)}, f32[9,1,256]{2,0,1:T(8,128)S(1)}, u32[]{:S(2)}, u32[]{:S(2)}) collective-permute-start(f32[9,1,256]{2,0,1:T(8,128)S(1)} %bitcast.388), channel_id=1, source_target_pairs={{0,0},{1,128},{2,16},{3,144},{4,2},{5,130},{6,18},{7,146},{8,1},{9... | collective-permute-start | bytes 27656 | tf_op jit(solution)/shard_map/ppermute | solution.py:106
  150.2 9.6 %collective-permute-start.22 = (f32[9,1,256]{2,0,1:T(8,128)S(1)}, f32[9,1,256]{2,0,1:T(8,128)S(1)}, u32[]{:S(2)}, u32[]{:S(2)}) collective-permute-start(f32[9,1,256]{2,0,1:T(8,128)S(1)} %bitcast.389), channel_id=1, source_target_pairs={{0,0},{1,128},{2,64},{3,192},{4,2},{5,130},{6,66},{7,194},{8,1},{9... | collective-permute-start | bytes 27656 | tf_op jit(solution)/shard_map/ppermute | solution.py:106
